TPU v7x, 512 devices: a whole 4x8x8 slice. The times are simulated.
512 devices in a mesh: grp: 16 (over x_lo, z), seq: 32 (over y, x_hi, core).
Axes of the slice: x: 4 (x_hi: 2, x_lo: 2; x = x_hi * 2 + x_lo), y: 8, z: 8, core: 2. Of those that a mesh axis runs over, the one named last changes fastest.
Arguments:
- signal: bfloat16 [131072, 256], P(('grp', 'seq')), may hold values from -6 to 6
- cotangent: bfloat16 [131072, 256], P(('grp', 'seq')), may hold values from -6 to 6
- w_taps: bfloat16 [512, 1024], replicated, may hold values from -0.25 to 0.25
- gate_bias: float32 [1024], replicated, may hold values from -3 to 3
- w_out: bfloat16 [512, 256], replicated, may hold values from -0.25 to 0.25
Outputs:
- block_out: bfloat16 [131072, 256], P(('grp', 'seq'))
- grad_in: bfloat16 [131072, 256], P(('grp', 'seq'))
- grad_taps: float32 [512, 1024], P('seq')
- grad_bias: float32 [1024], P('seq')
- grad_out: float32 [512, 256], P('seq')
All inputs are finite; a program needn't handle non-finite values.
Results may differ from a plain program's by a relative error of at most 0.0045.
Values may be sent and summed in bfloat16 or wider, within the bound.
No kernel may reach another device: no remote copies, remote signals or barrier semaphores. Data moves between devices by JAX's collectives and lax.ppermute only.
A program may use at most 64 MiB of HBM per device.

v0:
```python
import jax
import jax.numpy as jnp
from jax import lax
from jax.sharding import PartitionSpec as P


def from_behind(array, axis, by):
    count = lax.axis_size(axis)
    pairs = [(i, i + by) for i in range(count) if 0 <= i + by < count]
    return lax.ppermute(array, axis, pairs)


def reduced_row_axes(left, right):
    return lax.dot_general(
        left, right, (((0,), (0,)), ((), ())), preferred_element_type=jnp.float32
    )


def contract_cols(left, right):
    return lax.dot_general(
        left, right, (((1,), (1,)), ((), ())), preferred_element_type=jnp.float32
    )


def per_device(signal, cotangent, w_taps, gate_bias, w_out):
    width = signal.shape[1]
    units = w_out.shape[0]
    lagged_input = from_behind(signal, ("grp", "seq"), 2)
    preact = jnp.dot(signal, w_taps[width:], preferred_element_type=jnp.float32)
    preact = (
        preact
        + jnp.dot(lagged_input, w_taps[:width], preferred_element_type=jnp.float32)
        + gate_bias
    )
    squashed = jnp.tanh(preact[:, :units])
    opened = jax.nn.sigmoid(preact[:, units:])
    hidden_state = (squashed * opened).astype(jnp.bfloat16)
    block_out = (
        signal.astype(jnp.float32)
        + jnp.dot(hidden_state, w_out, preferred_element_type=jnp.float32)
    ).astype(jnp.bfloat16)
    grad_hidden = contract_cols(cotangent, w_out)
    grad_pre = jnp.concatenate(
        [
            grad_hidden * opened * (1.0 - squashed * squashed),
            grad_hidden * squashed * opened * (1.0 - opened),
        ],
        axis=1,
    ).astype(jnp.bfloat16)
    part_out = reduced_row_axes(hidden_state, cotangent)
    part_taps = jnp.concatenate(
        [reduced_row_axes(lagged_input, grad_pre), reduced_row_axes(signal, grad_pre)], axis=0
    )
    part_bias = jnp.sum(grad_pre.astype(jnp.float32), axis=0)
    later_pre = from_behind(grad_pre, ("grp", "seq"), -2)
    tapped_signal = contract_cols(later_pre, w_taps[:width])
    nearby = cotangent.astype(jnp.float32) + contract_cols(grad_pre, w_taps[width:])
    grad_in = (nearby + tapped_signal).astype(jnp.bfloat16)
    total_taps, total_bias, total_out = lax.psum((part_taps, part_bias, part_out), ("grp", "seq"))
    groups = lax.axis_size("seq")
    where = lax.axis_index("seq")
    share_taps = total_taps.shape[0] // groups
    share_bias = total_bias.shape[0] // groups
    share_out = total_out.shape[0] // groups
    grad_taps = lax.dynamic_slice_in_dim(total_taps, where * share_taps, share_taps, 0)
    grad_bias = lax.dynamic_slice_in_dim(total_bias, where * share_bias, share_bias, 0)
    grad_out = lax.dynamic_slice_in_dim(total_out, where * share_out, share_out, 0)
    return (block_out, grad_in, grad_taps, grad_bias, grad_out)


def solution(mesh):
    placed = (P(("grp", "seq"), None), P(("grp", "seq"), None), P(), P(), P())
    return jax.shard_map(
        per_device,
        mesh=mesh,
        in_specs=placed,
        out_specs=(
            P(("grp", "seq"), None),
            P(("grp", "seq"), None),
            P("seq", None),
            P("seq"),
            P("seq", None),
        ),
        check_vma=False,
    )
```

profile of v0, /device:TPU:56, one launch (start us, length us, event | category | flops | bytes accessed | tf_op | source)
XLA Modules:
  0.0 319.6 jit_solution(16530091480007034787)
XLA Ops:
  7.2 0.0 copy-start
  7.2 0.0 copy-start.3
  7.2 0.0 all-reduce.3.cloned.1.call-start
  7.2 5.1 %collective-permute-start = (bf16[256,256]{1,0:T(8,128)(2,1)}, bf16[256,256]{1,0:T(8,128)(2,1)S(1)}, u32[]{:S(2)}, u32[]{:S(2)}) collective-permute-start(bf16[256,256]{1,0:T(8,128)(2,1)} %param.5), channel_id=1, source_target_pairs={{0,2},{1,3},{2,4},{3,5},{4,6},{5,7},{6,8},{7,9},{8,10},{9,11},{10,... | collective-permute-start | bytes 393224 | tf_op jit(solution)/shard_map/ppermute | solution.py:10
  12.3 1.4 fusion.9
  13.7 3.4 %collective-permute-done = bf16[256,256]{1,0:T(8,128)(2,1)S(1)} collective-permute-done((bf16[256,256]{1,0:T(8,128)(2,1)}, bf16[256,256]{1,0:T(8,128)(2,1)S(1)}, u32[]{:S(2)}, u32[]{:S(2)}) %collective-permute-start) | collective-permute-done | bytes 131104 | tf_op jit(solution)/shard_map/ppermute | solution.py:10
  17.1 1.3 fusion
  18.5 0.0 copy-done
  18.5 0.0 copy-done.3
  18.5 0.0 copy-start.2
  18.5 0.5 multiply_convert_fusion.1
  19.0 1.1 fusion.11
  20.0 0.0 copy-done.2
  20.1 0.3 convolution_bitcast_fusion
  20.4 0.3 convolution_bitcast_fusion.1
  20.7 1.4 pad_maximum_fusion
  22.2 0.0 copy-start.1
  22.2 0.0 all-reduce.3.cloned.1.call-update
  22.2 0.1 pad_maximum_fusion.1
  22.3 4.9 %collective-permute-start.1 = (bf16[256,1024]{1,0:T(8,128)(2,1)S(1)}, bf16[256,1024]{1,0:T(8,128)(2,1)S(1)}, u32[]{:S(2)}, u32[]{:S(2)}) collective-permute-start(bf16[256,1024]{1,0:T(8,128)(2,1)S(1)} %pad_maximum_fusion.1), channel_id=1, source_target_pairs={{2,0},{3,1},{4,2},{5,3},{6,4},{7,5},{8,6},{9,7},{10,8},{11,9},{12,... | collective-permute-start | bytes 1572872 | tf_op jit(solution)/shard_map/ppermute | solution.py:10
  27.2 0.1 convert_reduce_fusion
  27.3 108.6 %psum.22 = f32[1024]{0:T(1024)S(1)} all-reduce(f32[1024]{0:T(1024)S(1)} %convert_reduce_fusion), channel_id=1, replica_groups=mesh['grp'=16,'seq'=32] {'grp','seq'}, use_global_device_ids=true, to_apply=%region_2.0 | all-reduce | flops 1024 | bytes 8192 | tf_op jit(solution)/shard_map/psum | solution.py:59
  136.0 0.6 dynamic_slice.10
  136.5 0.9 fusion.1
  137.4 0.0 copy-done.1
  137.4 0.3 convolution_add_fusion.3
  137.8 0.0 collective-permute-done.1
  137.8 1.0 fusion.2
  138.8 171.2 %all-reduce.3.cloned.1.call-done = (f32[512,1024]{1,0:T(8,128)}, f32[512,256]{1,0:T(8,128)}) async-done(((f32[512,1024]{1,0:T(8,128)}, f32[512,256]{1,0:T(8,128)}), (f32[512,1024]{1,0:T(8,128)}, f32[512,256]{1,0:T(8,128)})) %all-reduce.3.cloned.1.call-update) | async-done | bytes 2621456 | tf_op jit(solution)/shard_map/psum | solution.py:59
  310.0 1.5 constant_dynamic-slice_fusion.1
  311.5 1.3 constant_dynamic-slice_fusion
Async XLA Ops:
  7.2 11.3 %copy-start = (bf16[512,256]{1,0:T(8,128)(2,1)S(1)}, bf16[512,256]{1,0:T(8,128)(2,1)}, u32[]{:S(2)}) copy-start(bf16[512,256]{1,0:T(8,128)(2,1)} %param.9) | copy-start | bytes 786436
  7.2 11.3 %copy-start.3 = (bf16[256,256]{1,0:T(8,128)(2,1)S(1)}, bf16[256,256]{1,0:T(8,128)(2,1)}, u32[]{:S(2)}) copy-start(bf16[256,256]{1,0:T(8,128)(2,1)} %param.6) | copy-start | bytes 393220
  7.2 302.8 %all-reduce.3.cloned.1.call-start = ((), (), s32[]{:S(2)}) async-start(), calls=%async_computation | async-start | bytes 5242880 | tf_op jit(solution)/shard_map/psum | solution.py:59
  7.2 9.9 %collective-permute-start = (bf16[256,256]{1,0:T(8,128)(2,1)}, bf16[256,256]{1,0:T(8,128)(2,1)S(1)}, u32[]{:S(2)}, u32[]{:S(2)}) collective-permute-start(bf16[256,256]{1,0:T(8,128)(2,1)} %param.5), channel_id=1, source_target_pairs={{0,2},{1,3},{2,4},{3,5},{4,6},{5,7},{6,8},{7,9},{8,10},{9,11},{10,... | collective-permute-start | bytes 393224 | tf_op jit(solution)/shard_map/ppermute | solution.py:10
  18.5 1.6 copy-start.2
  22.2 115.3 %copy-start.1 = (bf16[512,1024]{1,0:T(8,128)(2,1)S(1)}, bf16[512,1024]{1,0:T(8,128)(2,1)}, u32[]{:S(2)}) copy-start(bf16[512,1024]{1,0:T(8,128)(2,1)} %param.7) | copy-start | bytes 3145732
  22.3 115.5 %collective-permute-start.1 = (bf16[256,1024]{1,0:T(8,128)(2,1)S(1)}, bf16[256,1024]{1,0:T(8,128)(2,1)S(1)}, u32[]{:S(2)}, u32[]{:S(2)}) collective-permute-start(bf16[256,1024]{1,0:T(8,128)(2,1)S(1)} %pad_maximum_fusion.1), channel_id=1, source_target_pairs={{2,0},{3,1},{4,2},{5,3},{6,4},{7,5},{8,6},{9,7},{10,8},{11,9},{12,... | collective-permute-start | bytes 1572872 | tf_op jit(solution)/shard_map/ppermute | solution.py:10
Sparse Core Ops, SparseCore 0:
  22.3 287.6 all-reduce.2
where the time goes:
time: 322 us; the launch traced here: 320 us
  waiting for transfers between devices  175 us (54%)
  blocking collectives  109 us (34%)
  between operations  14.1 us (4%)
  starting transfers between devices  10 us (3%)
  matrix products  7.19 us (2%)
  local copies, waits for them, and re-layouts  3.4 us (1%)
    psum x1, waiting for transfers between devices, per_device(): lax.psum((part_taps, part_bias, part_out), ('grp', 'seq'))  171 us
    psum x1, blocking collectives, per_device(): lax.psum((part_taps, part_bias, part_out), ('grp', 'seq'))  109 us
    ppermute x2, starting transfers between devices, from_behind(): return lax.ppermute(array, axis, pairs)  10 us
  transfers between devices with their start and end apart: 3, of which 2 were waited for; matrix products, arithmetic and copies ran while one was open for 1% of the time, Pallas kernels for 0%

commit v1 on v0

--- a/solution.py
+++ b/solution.py
@@ -56,15 +56,28 @@
     tapped_signal = contract_cols(later_pre, w_taps[:width])
     nearby = cotangent.astype(jnp.float32) + contract_cols(grad_pre, w_taps[width:])
     grad_in = (nearby + tapped_signal).astype(jnp.bfloat16)
-    total_taps, total_bias, total_out = lax.psum((part_taps, part_bias, part_out), ("grp", "seq"))
     groups = lax.axis_size("seq")
-    where = lax.axis_index("seq")
-    share_taps = total_taps.shape[0] // groups
-    share_bias = total_bias.shape[0] // groups
-    share_out = total_out.shape[0] // groups
-    grad_taps = lax.dynamic_slice_in_dim(total_taps, where * share_taps, share_taps, 0)
-    grad_bias = lax.dynamic_slice_in_dim(total_bias, where * share_bias, share_bias, 0)
-    grad_out = lax.dynamic_slice_in_dim(total_out, where * share_out, share_out, 0)
+    lanes = 128
+    rows_taps = part_taps.shape[0] // groups
+    rows_out = part_out.shape[0] // groups
+    share_bias = part_bias.shape[0] // groups
+    taps_r = rows_taps * part_taps.shape[1] // lanes
+    out_r = rows_out * part_out.shape[1] // lanes
+    bias_r = 8
+    bias_rows = jnp.pad(part_bias.reshape(groups, 1, share_bias), ((0, 0), (0, bias_r), (0, lanes - share_bias)))[:, :bias_r]
+    packed = jnp.concatenate(
+        [
+            part_taps.reshape(groups, taps_r, lanes),
+            part_out.reshape(groups, out_r, lanes),
+            bias_rows,
+        ],
+        axis=1,
+    ).reshape(groups * (taps_r + out_r + bias_r), lanes)
+    mine = lax.psum_scatter(packed, "seq", scatter_dimension=0, tiled=True)
+    mine = lax.psum(mine, "grp")
+    grad_taps = mine[:taps_r].reshape(rows_taps, part_taps.shape[1])
+    grad_out = mine[taps_r : taps_r + out_r].reshape(rows_out, part_out.shape[1])
+    grad_bias = mine[taps_r + out_r, :share_bias]
     return (block_out, grad_in, grad_taps, grad_bias, grad_out)
 
 

time: 322 us -> 308 us (0.957)
  blocking collectives: 109 us -> 0 us
  waiting for transfers between devices: 175 us -> 265 us
  local copies, waits for them, and re-layouts: 3.4 us -> 6.88 us
    unnamed x1 -> x3, waiting for transfers between devices: 0.02 us -> 123 us
    psum x1 -> x0, blocking collectives: 109 us -> none  [per_device(): lax.psum((part_taps, part_bias, part_out), ('grp', 'seq'))]
    psum x1, waiting for transfers between devices: 171 us -> 138 us  [per_device(): mine = lax.psum(mine, 'grp')]
    dynamic_slice x3 -> x0, local copies, waits for them, and re-layouts: 3.38 us -> none  [the longest x1 1.47 us: per_device(): lax.dynamic_slice_in_dim(total_taps, where * share_taps, share_taps, 0)]
  transfers between devices with their start and end apart: 3 -> 4, of which waited for: 2 -> 3; matrix products, arithmetic and copies ran while one was open for 1% -> 1% of each run, Pallas kernels for 0% -> 0%
where the time goes in v1:
time: 308 us; the launch traced here: 307 us
  waiting for transfers between devices  265 us (86%)
  between operations  14.2 us (5%)
  starting transfers between devices  10.1 us (3%)
  local copies, waits for them, and re-layouts  6.88 us (2%)
  matrix products  6.37 us (2%)
  other arithmetic  4.29 us (1%)
    psum x1, waiting for transfers between devices, per_device(): mine = lax.psum(mine, 'grp')  138 us
    unnamed x3, waiting for transfers between devices  123 us
    ppermute x2, starting transfers between devices, from_behind(): return lax.ppermute(array, axis, pairs)  10 us
  transfers between devices with their start and end apart: 4, of which 3 were waited for; matrix products, arithmetic and copies ran while one was open for 1% of the time, Pallas kernels for 0%

profile of v1, /device:TPU:56, one launch (start us, length us, event | category | flops | bytes accessed | tf_op | source)
XLA Modules:
  0.0 306.7 jit_solution(14182650442721048356)
XLA Ops:
  7.2 0.0 copy-start
  7.2 0.0 copy-start.5
  7.2 0.0 reduce-scatter.4.cloned.1.call-start
  7.2 5.1 %collective-permute-start = (bf16[256,256]{1,0:T(8,128)(2,1)}, bf16[256,256]{1,0:T(8,128)(2,1)S(1)}, u32[]{:S(2)}, u32[]{:S(2)}) collective-permute-start(bf16[256,256]{1,0:T(8,128)(2,1)} %param.5), channel_id=1, source_target_pairs={{0,2},{1,3},{2,4},{3,5},{4,6},{5,7},{6,8},{7,9},{8,10},{9,11},{10,... | collective-permute-start | bytes 393224 | tf_op jit(solution)/shard_map/ppermute | solution.py:10
  12.3 1.4 fusion.9
  13.7 3.4 %collective-permute-done = bf16[256,256]{1,0:T(8,128)(2,1)S(1)} collective-permute-done((bf16[256,256]{1,0:T(8,128)(2,1)}, bf16[256,256]{1,0:T(8,128)(2,1)S(1)}, u32[]{:S(2)}, u32[]{:S(2)}) %collective-permute-start) | collective-permute-done | bytes 131104 | tf_op jit(solution)/shard_map/ppermute | solution.py:10
  17.1 1.3 fusion
  18.5 0.0 copy-done
  18.5 0.0 copy-done.5
  18.5 0.0 copy-start.2
  18.5 0.4 multiply_convert_fusion.1
  19.0 0.0 copy-start.3
  19.0 0.1 convert_reduce_fusion
  19.1 0.3 copy-done.2
  19.4 0.3 convolution_bitcast_fusion
  19.7 0.1 reshape.31
  19.8 0.7 pad_slice_fusion
  20.5 0.3 fusion.11
  20.8 0.3 convolution_bitcast_fusion.1
  21.1 0.0 copy-done.3
  21.2 1.5 pad_maximum_fusion.1
  22.6 1.7 reshape.29
  24.4 2.6 pad_maximum_fusion
  27.0 0.0 copy-start.4
  27.0 0.0 copy-start.1
  27.0 0.0 copy-start.6
  27.0 0.0 reduce-scatter.4.cloned.1.call-update
  27.0 0.0 all-reduce.4.cloned.1.call-start
  27.1 0.1 pad_maximum_fusion.2
  27.2 4.9 %collective-permute-start.1 = (bf16[256,1024]{1,0:T(8,128)(2,1)S(1)}, bf16[256,1024]{1,0:T(8,128)(2,1)S(1)}, u32[]{:S(2)}, u32[]{:S(2)}) collective-permute-start(bf16[256,1024]{1,0:T(8,128)(2,1)S(1)} %pad_maximum_fusion.2), channel_id=1, source_target_pairs={{2,0},{3,1},{4,2},{5,3},{6,4},{7,5},{8,6},{9,7},{10,8},{11,9},{12,... | collective-permute-start | bytes 1572872 | tf_op jit(solution)/shard_map/ppermute | solution.py:10
  32.1 0.0 copy-done.4
  32.1 0.9 fusion.1
  33.0 0.0 copy-done.1
  33.0 0.0 copy-done.6
  33.0 0.3 convolution_add_fusion.3
  33.4 123.3 %reduce-scatter.4.cloned.1.call-done = f32[168,128]{1,0:T(8,128)} async-done(((f32[5376,128]{1,0:T(8,128)}), f32[168,128]{1,0:T(8,128)}) %reduce-scatter.4.cloned.1.call-update) | async-done | bytes 86032
  156.7 0.0 all-reduce.4.cloned.1.call-update
  156.7 0.0 collective-permute-done.1
  156.7 1.0 fusion.2
  157.7 138.1 %all-reduce.4.cloned.1.call-done = f32[168,128]{1,0:T(8,128)} async-done(((f32[168,128]{1,0:T(8,128)}), f32[168,128]{1,0:T(8,128)}) %all-reduce.4.cloned.1.call-update) | async-done | bytes 86032 | tf_op jit(solution)/shard_map/psum | solution.py:77
  295.8 0.8 slice.36
  296.7 0.6 reshape.33
  297.3 0.7 slice.38
  298.0 0.6 reshape.34
  298.7 1.2 slice_bitcast_fusion
  (1 shorter events, 0.0 us)
Async XLA Ops:
  7.2 11.3 %copy-start = (bf16[512,256]{1,0:T(8,128)(2,1)S(1)}, bf16[512,256]{1,0:T(8,128)(2,1)}, u32[]{:S(2)}) copy-start(bf16[512,256]{1,0:T(8,128)(2,1)} %param.9) | copy-start | bytes 786436
  7.2 11.3 %copy-start.5 = (bf16[256,256]{1,0:T(8,128)(2,1)S(1)}, bf16[256,256]{1,0:T(8,128)(2,1)}, u32[]{:S(2)}) copy-start(bf16[256,256]{1,0:T(8,128)(2,1)} %param.6) | copy-start | bytes 393220
  7.2 149.5 %reduce-scatter.4.cloned.1.call-start = ((), (), s32[]{:S(2)}) async-start(), calls=%async_computation.2 | async-start | bytes 2838528
  7.2 9.9 %collective-permute-start = (bf16[256,256]{1,0:T(8,128)(2,1)}, bf16[256,256]{1,0:T(8,128)(2,1)S(1)}, u32[]{:S(2)}, u32[]{:S(2)}) collective-permute-start(bf16[256,256]{1,0:T(8,128)(2,1)} %param.5), channel_id=1, source_target_pairs={{0,2},{1,3},{2,4},{3,5},{4,6},{5,7},{6,8},{7,9},{8,10},{9,11},{10,... | collective-permute-start | bytes 393224 | tf_op jit(solution)/shard_map/ppermute | solution.py:10
  18.5 0.9 copy-start.2
  19.0 2.2 copy-start.3
  27.0 5.1 %copy-start.4 = (bf16[256,512]{1,0:T(8,128)(2,1)S(1)}, bf16[256,512]{1,0:T(8,128)(2,1)}, u32[]{:S(2)}) copy-start(bf16[256,512]{1,0:T(8,128)(2,1)} %copy-done.3) | copy-start | bytes 786436
  27.0 6.0 %copy-start.1 = (bf16[512,1024]{1,0:T(8,128)(2,1)S(1)}, bf16[512,1024]{1,0:T(8,128)(2,1)}, u32[]{:S(2)}) copy-start(bf16[512,1024]{1,0:T(8,128)(2,1)} %param.7) | copy-start | bytes 3145732
  27.0 6.0 %copy-start.6 = (bf16[256,256]{1,0:T(8,128)(2,1)S(1)}, bf16[256,256]{1,0:T(8,128)(2,1)}, u32[]{:S(2)}) copy-start(bf16[256,256]{1,0:T(8,128)(2,1)} %param.6) | copy-start | bytes 393220
  27.0 268.8 %all-reduce.4.cloned.1.call-start = ((), (), s32[]{:S(2)}) async-start(), calls=%async_computation.1 | async-start | bytes 172032 | tf_op jit(solution)/shard_map/psum | solution.py:77
  27.2 129.6 %collective-permute-start.1 = (bf16[256,1024]{1,0:T(8,128)(2,1)S(1)}, bf16[256,1024]{1,0:T(8,128)(2,1)S(1)}, u32[]{:S(2)}, u32[]{:S(2)}) collective-permute-start(bf16[256,1024]{1,0:T(8,128)(2,1)S(1)} %pad_maximum_fusion.2), channel_id=1, source_target_pairs={{2,0},{3,1},{4,2},{5,3},{6,4},{7,5},{8,6},{9,7},{10,8},{11,9},{12,... | collective-permute-start | bytes 1572872 | tf_op jit(solution)/shard_map/ppermute | solution.py:10
Sparse Core Ops, SparseCore 0:
  27.2 129.4 reduce-scatter.3
  159.6 136.1 all-reduce.3

commit v2 on v1

--- a/solution.py
+++ b/solution.py
@@ -20,6 +20,49 @@
     return lax.dot_general(
         left, right, (((1,), (1,)), ((), ())), preferred_element_type=jnp.float32
     )
+
+
+def exchange(array, axis, mask):
+    count = lax.axis_size(axis)
+    return lax.ppermute(array, axis, [(i, i ^ mask) for i in range(count)])
+
+
+def bit_order(count):
+    bits = count.bit_length() - 1
+    order = [0] + list(range(2, bits)) + [1] if bits > 2 else list(range(bits))
+    if bits == 5:
+        order = [0, 2, 3, 1, 4]
+    return order
+
+
+def halving_scatter(shares, axis):
+    count = shares.shape[0]
+    bits = count.bit_length() - 1
+    order = bit_order(count)
+    rest = shares.shape[1:]
+    shaped = shares.reshape((2,) * bits + rest)
+    shaped = jnp.transpose(
+        shaped, [bits - 1 - b for b in order] + list(range(bits, bits + len(rest)))
+    )
+    buf = shaped.reshape((count,) + rest)
+    where = lax.axis_index(axis)
+    for b in order:
+        mask = 1 << b
+        bit = (where >> b) & 1
+        halves = buf.reshape((2, buf.shape[0] // 2) + rest)
+        keep = lax.dynamic_index_in_dim(halves, bit, 0, keepdims=False)
+        send = lax.dynamic_index_in_dim(halves, 1 - bit, 0, keepdims=False)
+        buf = keep + exchange(send, axis, mask)
+    return buf[0]
+
+
+def butterfly_sum(array, axis):
+    count = lax.axis_size(axis)
+    bits = count.bit_length() - 1
+    order = [0, bits - 1] + list(range(1, bits - 1)) if bits > 1 else list(range(bits))
+    for b in order:
+        array = array + exchange(array, axis, 1 << b)
+    return array
 
 
 def per_device(signal, cotangent, w_taps, gate_bias, w_out):
@@ -72,9 +115,9 @@
             bias_rows,
         ],
         axis=1,
-    ).reshape(groups * (taps_r + out_r + bias_r), lanes)
-    mine = lax.psum_scatter(packed, "seq", scatter_dimension=0, tiled=True)
-    mine = lax.psum(mine, "grp")
+    )
+    mine = halving_scatter(packed, "seq")
+    mine = butterfly_sum(mine, "grp")
     grad_taps = mine[:taps_r].reshape(rows_taps, part_taps.shape[1])
     grad_out = mine[taps_r : taps_r + out_r].reshape(rows_out, part_out.shape[1])
     grad_bias = mine[taps_r + out_r, :share_bias]

time: 308 us -> 136 us (0.44)
  waiting for transfers between devices: 265 us -> 68.3 us
  starting transfers between devices: 10.1 us -> 45.3 us
  between operations: 14.2 us -> 1.03 us
    psum x1 -> x0, waiting for transfers between devices: 138 us -> none  [per_device(): mine = lax.psum(mine, 'grp')]
    unnamed x3 -> x0, waiting for transfers between devices: 123 us -> none
    ppermute x0 -> x9, waiting for transfers between devices: none -> 64.9 us  [exchange(): return lax.ppermute(array, axis, [(i, i ^ mask) for i in range(count)])]
    ppermute x0 -> x9, starting transfers between devices: none -> 37 us  [exchange(): return lax.ppermute(array, axis, [(i, i ^ mask) for i in range(count)])]
  transfers between devices with their start and end apart: 4 -> 11, of which waited for: 3 -> 9; matrix products, arithmetic and copies ran while one was open for 1% -> 3% of each run, Pallas kernels for 0% -> 0%
where the time goes in v2:
time: 136 us; the launch traced here: 133 us
  waiting for transfers between devices  68.3 us (50%)
  starting transfers between devices  45.3 us (33%)
  matrix products  7.28 us (5%)
  local copies, waits for them, and re-layouts  6.62 us (5%)
  other arithmetic  4.67 us (3%)
    ppermute x9, waiting for transfers between devices, exchange(): return lax.ppermute(array, axis, [(i, i ^ mask) for i in range(count)])  64.9 us
    ppermute x9, starting transfers between devices, exchange(): return lax.ppermute(array, axis, [(i, i ^ mask) for i in range(count)])  37 us
    ppermute x2, starting transfers between devices, from_behind(): return lax.ppermute(array, axis, pairs)  8.3 us
    ppermute x2, waiting for transfers between devices, from_behind(): return lax.ppermute(array, axis, pairs)  3.38 us
  transfers between devices with their start and end apart: 11, of which 9 were waited for; matrix products, arithmetic and copies ran while one was open for 3% of the time, Pallas kernels for 0%

profile of v2, /device:TPU:56, one launch (start us, length us, event | category | flops | bytes accessed | tf_op | source)
XLA Modules:
  0.0 133.2 jit_solution(8899692428174522897)
XLA Ops:
  0.6 0.0 copy-start
  0.6 0.0 copy-start.7
  0.7 5.1 %collective-permute-start = (bf16[256,256]{1,0:T(8,128)(2,1)}, bf16[256,256]{1,0:T(8,128)(2,1)S(1)}, u32[]{:S(2)}, u32[]{:S(2)}) collective-permute-start(bf16[256,256]{1,0:T(8,128)(2,1)} %param.5), channel_id=1, source_target_pairs={{0,2},{1,3},{2,4},{3,5},{4,6},{5,7},{6,8},{7,9},{8,10},{9,11},{10,... | collective-permute-start | bytes 393224 | tf_op jit(solution)/shard_map/ppermute | solution.py:10
  5.7 1.4 %fusion.9 = f32[256,1024]{1,0:T(8,128)S(1)} fusion(bf16[256,256]{1,0:T(8,128)(2,1)} %param.5, bf16[512,1024]{1,0:T(8,128)(2,1)} %param.7), kind=kOutput, calls=%fused_computation.28 | convolution fusion | flops 134217728 | bytes 1703936 | tf_op jit(solution)/shard_map/dot_general | solution.py:72
  7.2 3.4 %collective-permute-done = bf16[256,256]{1,0:T(8,128)(2,1)S(1)} collective-permute-done((bf16[256,256]{1,0:T(8,128)(2,1)}, bf16[256,256]{1,0:T(8,128)(2,1)S(1)}, u32[]{:S(2)}, u32[]{:S(2)}) %collective-permute-start) | collective-permute-done | bytes 131104 | tf_op jit(solution)/shard_map/ppermute | solution.py:10
  10.5 1.3 %fusion = f32[256,1024]{1,0:T(8,128)S(1)} fusion(f32[256,1024]{1,0:T(8,128)S(1)} %fusion.9, bf16[256,256]{1,0:T(8,128)(2,1)S(1)} %collective-permute-done, f32[1024]{0:T(1024)} %param.8, bf16[512,1024]{1,0:T(8,128)(2,1)} %param.7), kind=kOutput, calls=%fused_computation.7 | convolution fusion | flops 134742016 | bytes 2756608 | tf_op jit(solution)/shard_map/dot_general | solution.py:75
  11.9 0.0 copy-done
  11.9 0.0 copy-done.7
  11.9 0.0 copy-start.3
  11.9 0.5 multiply_convert_fusion.1
  12.4 0.0 copy-start.5
  12.4 0.1 convert_reduce_fusion
  12.5 0.3 copy-done.3
  12.8 0.3 convolution_bitcast_fusion
  13.2 0.1 reshape.42
  13.3 0.3 fusion.11
  13.6 0.0 copy-done.5
  13.6 0.3 convolution_bitcast_fusion.1
  13.9 1.5 %pad_maximum_fusion.1 = f32[512,1024]{1,0:T(8,128)} fusion(f32[256,1024]{1,0:T(8,128)S(1)} %convolution_bitcast_fusion, f32[256,1024]{1,0:T(8,128)S(1)} %convolution_bitcast_fusion.1), kind=kLoop, calls=%fused_computation.1 | loop fusion | flops 524288 | bytes 4194304 | tf_op jit(solution)/shard_map/concatenate | solution.py:94
  15.4 1.7 %concatenate.19 = f32[2,2,2,2,2,128,128]{6,5,4,3,2,1,0:T(8,128)S(1)} reshape(f32[512,1024]{1,0:T(8,128)} %pad_maximum_fusion.1) | data formatting | bytes 4194304 | tf_op jit(solution)/shard_map/concatenate | solution.py:111
  17.1 0.3 pad_maximum_fusion
  17.4 0.2 copy.15
  17.6 1.2 dynamic-slice_bitcast_fusion
  18.8 1.9 %collective-permute-start.2 = (f32[16,168,128]{2,1,0:T(8,128)}, f32[16,168,128]{2,1,0:T(8,128)}, u32[]{:S(2)}, u32[]{:S(2)}) collective-permute-start(f32[16,168,128]{2,1,0:T(8,128)} %dynamic-slice_bitcast_fusion), channel_id=1, source_target_pairs={{0,1},{1,0},{2,3},{3,2},{4,5},{5,4},{6,7},{7,6},{8,9},{9,8},{10,11... | collective-permute-start | bytes 4128776 | tf_op jit(solution)/shard_map/ppermute | solution.py:27
  20.8 3.4 %collective-permute-done.2 = f32[16,168,128]{2,1,0:T(8,128)} collective-permute-done((f32[16,168,128]{2,1,0:T(8,128)}, f32[16,168,128]{2,1,0:T(8,128)}, u32[]{:S(2)}, u32[]{:S(2)}) %collective-permute-start.2) | collective-permute-done | bytes 1376288 | tf_op jit(solution)/shard_map/ppermute | solution.py:27
  24.2 1.5 %bitcast_add_fusion = f32[16,168,128]{2,1,0:T(8,128)S(1)} fusion(f32[16,168,128]{2,1,0:T(8,128)} %collective-permute-done.2, f32[2,16,168,128]{3,2,1,0:T(8,128)S(1)} %bitcast.43, s32[]{:T(128)S(6)} %select_n.35), kind=kLoop, calls=%fused_computation.2 | loop fusion | flops 344064 | bytes 4128772 | tf_op jit(solution)/shard_map/add | solution.py:55
  25.7 0.0 copy-start.1
  25.7 1.1 copy-done.1
  26.8 3.3 %collective-permute-start.3 = (f32[8,168,128]{2,1,0:T(8,128)S(1)}, f32[8,168,128]{2,1,0:T(8,128)S(1)}, u32[]{:S(2)}, u32[]{:S(2)}) collective-permute-start(f32[8,168,128]{2,1,0:T(8,128)S(1)} %dynamic-slice_bitcast_fusion.1), channel_id=1, source_target_pairs={{0,4},{1,5},{2,6},{3,7},{4,0},{5,1},{6,2},{7,3},{8,12},{9,13},{10,... | collective-permute-start | bytes 2064392 | tf_op jit(solution)/shard_map/ppermute | solution.py:27
  30.1 16.1 %collective-permute-done.3 = f32[8,168,128]{2,1,0:T(8,128)S(1)} collective-permute-done((f32[8,168,128]{2,1,0:T(8,128)S(1)}, f32[8,168,128]{2,1,0:T(8,128)S(1)}, u32[]{:S(2)}, u32[]{:S(2)}) %collective-permute-start.3) | collective-permute-done | bytes 688160 | tf_op jit(solution)/shard_map/ppermute | solution.py:27
  46.2 1.2 bitcast_add_fusion.1
  47.4 0.0 copy-start.2
  47.4 5.0 %collective-permute-start.4 = (f32[4,168,128]{2,1,0:T(8,128)S(1)}, f32[4,168,128]{2,1,0:T(8,128)S(1)}, u32[]{:S(2)}, u32[]{:S(2)}) collective-permute-start(f32[4,168,128]{2,1,0:T(8,128)S(1)} %dynamic-slice_bitcast_fusion.2), channel_id=1, source_target_pairs={{0,8},{1,9},{2,10},{3,11},{4,12},{5,13},{6,14},{7,15},{8,0},{9,1},... | collective-permute-start | bytes 1032200 | tf_op jit(solution)/shard_map/ppermute | solution.py:27
  52.4 15.1 %collective-permute-done.4 = f32[4,168,128]{2,1,0:T(8,128)S(1)} collective-permute-done((f32[4,168,128]{2,1,0:T(8,128)S(1)}, f32[4,168,128]{2,1,0:T(8,128)S(1)}, u32[]{:S(2)}, u32[]{:S(2)}) %collective-permute-start.4) | collective-permute-done | bytes 344096 | tf_op jit(solution)/shard_map/ppermute | solution.py:27
  67.6 3.4 %collective-permute-start.5 = (f32[2,168,128]{2,1,0:T(8,128)S(1)}, f32[2,168,128]{2,1,0:T(8,128)S(1)}, u32[]{:S(2)}, u32[]{:S(2)}) collective-permute-start(f32[2,168,128]{2,1,0:T(8,128)S(1)} %dynamic-slice_bitcast_fusion.3), channel_id=1, source_target_pairs={{0,2},{1,3},{2,0},{3,1},{4,6},{5,7},{6,4},{7,5},{8,10},{9,11},{10,... | collective-permute-start | bytes 516104 | tf_op jit(solution)/shard_map/ppermute | solution.py:27
  71.1 0.0 copy-start.4
  71.1 0.0 copy-start.6
  71.1 5.3 %collective-permute-done.5 = f32[2,168,128]{2,1,0:T(8,128)S(1)} collective-permute-done((f32[2,168,128]{2,1,0:T(8,128)S(1)}, f32[2,168,128]{2,1,0:T(8,128)S(1)}, u32[]{:S(2)}, u32[]{:S(2)}) %collective-permute-start.5) | collective-permute-done | bytes 172064 | tf_op jit(solution)/shard_map/ppermute | solution.py:27
  76.5 4.9 %collective-permute-start.6 = (f32[1,168,128]{2,1,0:T(8,128)S(1)}, f32[1,168,128]{2,1,0:T(8,128)S(1)}, u32[]{:S(2)}, u32[]{:S(2)}) collective-permute-start(f32[1,168,128]{2,1,0:T(8,128)S(1)} %constant_dynamic-slice_fusion), channel_id=1, source_target_pairs={{0,16},{1,17},{2,18},{3,19},{4,20},{5,21},{6,22},{7,23},{8,24},{9,... | collective-permute-start | bytes 258056 | tf_op jit(solution)/shard_map/ppermute | solution.py:27
  81.4 5.9 %collective-permute-done.6 = f32[1,168,128]{2,1,0:T(8,128)S(1)} collective-permute-done((f32[1,168,128]{2,1,0:T(8,128)S(1)}, f32[1,168,128]{2,1,0:T(8,128)S(1)}, u32[]{:S(2)}, u32[]{:S(2)}) %collective-permute-start.6) | collective-permute-done | bytes 86048 | tf_op jit(solution)/shard_map/ppermute | solution.py:27
  87.3 4.3 %collective-permute-start.7 = (f32[168,128]{1,0:T(8,128)S(1)}, f32[168,128]{1,0:T(8,128)S(1)}, u32[]{:S(2)}, u32[]{:S(2)}) collective-permute-start(f32[168,128]{1,0:T(8,128)S(1)} %add_bitcast_fusion), channel_id=1, source_target_pairs={{0,32},{32,0},{64,96},{96,64},{128,160},{160,128},{192,224},{224,1... | collective-permute-start | bytes 258056 | tf_op jit(solution)/shard_map/ppermute | solution.py:27
  91.6 0.1 pad_maximum_fusion.2
  91.7 3.2 %collective-permute-start.1 = (bf16[256,1024]{1,0:T(8,128)(2,1)S(1)}, bf16[256,1024]{1,0:T(8,128)(2,1)S(1)}, u32[]{:S(2)}, u32[]{:S(2)}) collective-permute-start(bf16[256,1024]{1,0:T(8,128)(2,1)S(1)} %pad_maximum_fusion.2), channel_id=1, source_target_pairs={{2,0},{3,1},{4,2},{5,3},{6,4},{7,5},{8,6},{9,7},{10,8},{11,9},{12,... | collective-permute-start | bytes 1572872 | tf_op jit(solution)/shard_map/ppermute | solution.py:10
  94.9 0.0 collective-permute-done.7
  94.9 3.8 %collective-permute-start.8 = (f32[168,128]{1,0:T(8,128)S(1)}, f32[168,128]{1,0:T(8,128)S(1)}, u32[]{:S(2)}, u32[]{:S(2)}) collective-permute-start(f32[168,128]{1,0:T(8,128)S(1)} %add.114), channel_id=1, source_target_pairs={{0,256},{32,288},{64,320},{96,352},{128,384},{160,416},{192,448},{... | collective-permute-start | bytes 258056 | tf_op jit(solution)/shard_map/ppermute | solution.py:27
  98.8 0.0 copy-done.2
  98.8 1.2 convolution_add_fusion.3
  100.0 12.5 %collective-permute-done.8 = f32[168,128]{1,0:T(8,128)S(1)} collective-permute-done((f32[168,128]{1,0:T(8,128)S(1)}, f32[168,128]{1,0:T(8,128)S(1)}, u32[]{:S(2)}, u32[]{:S(2)}) %collective-permute-start.8) | collective-permute-done | bytes 86048 | tf_op jit(solution)/shard_map/ppermute | solution.py:27
  112.6 2.5 %collective-permute-start.9 = (f32[168,128]{1,0:T(8,128)S(1)}, f32[168,128]{1,0:T(8,128)S(1)}, u32[]{:S(2)}, u32[]{:S(2)}) collective-permute-start(f32[168,128]{1,0:T(8,128)S(1)} %add.115), channel_id=1, source_target_pairs={{0,64},{32,96},{64,0},{96,32},{128,192},{160,224},{192,128},{224,1... | collective-permute-start | bytes 258056 | tf_op jit(solution)/shard_map/ppermute | solution.py:27
  115.1 0.0 copy-done.4
  115.1 0.0 copy-done.6
  115.1 0.9 fusion.1
  116.0 4.8 %collective-permute-done.9 = f32[168,128]{1,0:T(8,128)S(1)} collective-permute-done((f32[168,128]{1,0:T(8,128)S(1)}, f32[168,128]{1,0:T(8,128)S(1)}, u32[]{:S(2)}, u32[]{:S(2)}) %collective-permute-start.9) | collective-permute-done | bytes 86048 | tf_op jit(solution)/shard_map/ppermute | solution.py:27
  120.8 8.0 %collective-permute-start.10 = (f32[168,128]{1,0:T(8,128)S(1)}, f32[168,128]{1,0:T(8,128)S(1)}, u32[]{:S(2)}, u32[]{:S(2)}) collective-permute-start(f32[168,128]{1,0:T(8,128)S(1)} %add.116), channel_id=1, source_target_pairs={{0,128},{32,160},{64,192},{96,224},{128,0},{160,32},{192,64},{224,... | collective-permute-start | bytes 258056 | tf_op jit(solution)/shard_map/ppermute | solution.py:27
  128.7 0.0 collective-permute-done.1
  128.7 1.0 fusion.2
  129.7 1.7 %collective-permute-done.10 = f32[168,128]{1,0:T(8,128)S(1)} collective-permute-done((f32[168,128]{1,0:T(8,128)S(1)}, f32[168,128]{1,0:T(8,128)S(1)}, u32[]{:S(2)}, u32[]{:S(2)}) %collective-permute-start.10) | collective-permute-done | bytes 86048 | tf_op jit(solution)/shard_map/ppermute | solution.py:27
  131.5 0.5 slice_bitcast_fusion
  132.0 0.6 reshape.46
  132.6 0.6 reshape.47
  (15 shorter events, 0.3 us)
Async XLA Ops:
  0.6 11.3 %copy-start = (bf16[512,256]{1,0:T(8,128)(2,1)S(1)}, bf16[512,256]{1,0:T(8,128)(2,1)}, u32[]{:S(2)}) copy-start(bf16[512,256]{1,0:T(8,128)(2,1)} %param.9) | copy-start | bytes 786436
  0.6 11.3 %copy-start.7 = (bf16[256,256]{1,0:T(8,128)(2,1)S(1)}, bf16[256,256]{1,0:T(8,128)(2,1)}, u32[]{:S(2)}) copy-start(bf16[256,256]{1,0:T(8,128)(2,1)} %param.6) | copy-start | bytes 393220
  0.7 9.9 %collective-permute-start = (bf16[256,256]{1,0:T(8,128)(2,1)}, bf16[256,256]{1,0:T(8,128)(2,1)S(1)}, u32[]{:S(2)}, u32[]{:S(2)}) collective-permute-start(bf16[256,256]{1,0:T(8,128)(2,1)} %param.5), channel_id=1, source_target_pairs={{0,2},{1,3},{2,4},{3,5},{4,6},{5,7},{6,8},{7,9},{8,10},{9,11},{10,... | collective-permute-start | bytes 393224 | tf_op jit(solution)/shard_map/ppermute | solution.py:10
  11.9 0.9 copy-start.3
  12.4 1.2 copy-start.5
  18.8 5.4 %collective-permute-start.2 = (f32[16,168,128]{2,1,0:T(8,128)}, f32[16,168,128]{2,1,0:T(8,128)}, u32[]{:S(2)}, u32[]{:S(2)}) collective-permute-start(f32[16,168,128]{2,1,0:T(8,128)} %dynamic-slice_bitcast_fusion), channel_id=1, source_target_pairs={{0,1},{1,0},{2,3},{3,2},{4,5},{5,4},{6,7},{7,6},{8,9},{9,8},{10,11... | collective-permute-start | bytes 4128776 | tf_op jit(solution)/shard_map/ppermute | solution.py:27
  25.7 1.1 copy-start.1
  26.8 19.4 %collective-permute-start.3 = (f32[8,168,128]{2,1,0:T(8,128)S(1)}, f32[8,168,128]{2,1,0:T(8,128)S(1)}, u32[]{:S(2)}, u32[]{:S(2)}) collective-permute-start(f32[8,168,128]{2,1,0:T(8,128)S(1)} %dynamic-slice_bitcast_fusion.1), channel_id=1, source_target_pairs={{0,4},{1,5},{2,6},{3,7},{4,0},{5,1},{6,2},{7,3},{8,12},{9,13},{10,... | collective-permute-start | bytes 2064392 | tf_op jit(solution)/shard_map/ppermute | solution.py:27
  47.4 51.4 %copy-start.2 = (bf16[512,1024]{1,0:T(8,128)(2,1)S(1)}, bf16[512,1024]{1,0:T(8,128)(2,1)}, u32[]{:S(2)}) copy-start(bf16[512,1024]{1,0:T(8,128)(2,1)} %param.7) | copy-start | bytes 3145732
  47.4 20.2 %collective-permute-start.4 = (f32[4,168,128]{2,1,0:T(8,128)S(1)}, f32[4,168,128]{2,1,0:T(8,128)S(1)}, u32[]{:S(2)}, u32[]{:S(2)}) collective-permute-start(f32[4,168,128]{2,1,0:T(8,128)S(1)} %dynamic-slice_bitcast_fusion.2), channel_id=1, source_target_pairs={{0,8},{1,9},{2,10},{3,11},{4,12},{5,13},{6,14},{7,15},{8,0},{9,1},... | collective-permute-start | bytes 1032200 | tf_op jit(solution)/shard_map/ppermute | solution.py:27
  67.6 8.8 %collective-permute-start.5 = (f32[2,168,128]{2,1,0:T(8,128)S(1)}, f32[2,168,128]{2,1,0:T(8,128)S(1)}, u32[]{:S(2)}, u32[]{:S(2)}) collective-permute-start(f32[2,168,128]{2,1,0:T(8,128)S(1)} %dynamic-slice_bitcast_fusion.3), channel_id=1, source_target_pairs={{0,2},{1,3},{2,0},{3,1},{4,6},{5,7},{6,4},{7,5},{8,10},{9,11},{10,... | collective-permute-start | bytes 516104 | tf_op jit(solution)/shard_map/ppermute | solution.py:27
  71.1 44.0 %copy-start.4 = (bf16[256,256]{1,0:T(8,128)(2,1)S(1)}, bf16[256,256]{1,0:T(8,128)(2,1)}, u32[]{:S(2)}) copy-start(bf16[256,256]{1,0:T(8,128)(2,1)} %param.5) | copy-start | bytes 393220
  71.1 44.0 %copy-start.6 = (bf16[256,512]{1,0:T(8,128)(2,1)S(1)}, bf16[256,512]{1,0:T(8,128)(2,1)}, u32[]{:S(2)}) copy-start(bf16[256,512]{1,0:T(8,128)(2,1)} %copy-done.5) | copy-start | bytes 786436
  76.5 10.8 %collective-permute-start.6 = (f32[1,168,128]{2,1,0:T(8,128)S(1)}, f32[1,168,128]{2,1,0:T(8,128)S(1)}, u32[]{:S(2)}, u32[]{:S(2)}) collective-permute-start(f32[1,168,128]{2,1,0:T(8,128)S(1)} %constant_dynamic-slice_fusion), channel_id=1, source_target_pairs={{0,16},{1,17},{2,18},{3,19},{4,20},{5,21},{6,22},{7,23},{8,24},{9,... | collective-permute-start | bytes 258056 | tf_op jit(solution)/shard_map/ppermute | solution.py:27
  87.3 7.6 %collective-permute-start.7 = (f32[168,128]{1,0:T(8,128)S(1)}, f32[168,128]{1,0:T(8,128)S(1)}, u32[]{:S(2)}, u32[]{:S(2)}) collective-permute-start(f32[168,128]{1,0:T(8,128)S(1)} %add_bitcast_fusion), channel_id=1, source_target_pairs={{0,32},{32,0},{64,96},{96,64},{128,160},{160,128},{192,224},{224,1... | collective-permute-start | bytes 258056 | tf_op jit(solution)/shard_map/ppermute | solution.py:27
  91.7 37.1 %collective-permute-start.1 = (bf16[256,1024]{1,0:T(8,128)(2,1)S(1)}, bf16[256,1024]{1,0:T(8,128)(2,1)S(1)}, u32[]{:S(2)}, u32[]{:S(2)}) collective-permute-start(bf16[256,1024]{1,0:T(8,128)(2,1)S(1)} %pad_maximum_fusion.2), channel_id=1, source_target_pairs={{2,0},{3,1},{4,2},{5,3},{6,4},{7,5},{8,6},{9,7},{10,8},{11,9},{12,... | collective-permute-start | bytes 1572872 | tf_op jit(solution)/shard_map/ppermute | solution.py:10
  94.9 17.6 %collective-permute-start.8 = (f32[168,128]{1,0:T(8,128)S(1)}, f32[168,128]{1,0:T(8,128)S(1)}, u32[]{:S(2)}, u32[]{:S(2)}) collective-permute-start(f32[168,128]{1,0:T(8,128)S(1)} %add.114), channel_id=1, source_target_pairs={{0,256},{32,288},{64,320},{96,352},{128,384},{160,416},{192,448},{... | collective-permute-start | bytes 258056 | tf_op jit(solution)/shard_map/ppermute | solution.py:27
  112.6 8.2 %collective-permute-start.9 = (f32[168,128]{1,0:T(8,128)S(1)}, f32[168,128]{1,0:T(8,128)S(1)}, u32[]{:S(2)}, u32[]{:S(2)}) collective-permute-start(f32[168,128]{1,0:T(8,128)S(1)} %add.115), channel_id=1, source_target_pairs={{0,64},{32,96},{64,0},{96,32},{128,192},{160,224},{192,128},{224,1... | collective-permute-start | bytes 258056 | tf_op jit(solution)/shard_map/ppermute | solution.py:27
  120.8 10.7 %collective-permute-start.10 = (f32[168,128]{1,0:T(8,128)S(1)}, f32[168,128]{1,0:T(8,128)S(1)}, u32[]{:S(2)}, u32[]{:S(2)}) collective-permute-start(f32[168,128]{1,0:T(8,128)S(1)} %add.116), channel_id=1, source_target_pairs={{0,128},{32,160},{64,192},{96,224},{128,0},{160,32},{192,64},{224,... | collective-permute-start | bytes 258056 | tf_op jit(solution)/shard_map/ppermute | solution.py:27

commit v3 on v0

--- a/solution.py
+++ b/solution.py
@@ -20,6 +20,51 @@
     return lax.dot_general(
         left, right, (((1,), (1,)), ((), ())), preferred_element_type=jnp.float32
     )
+
+
+def exchange(array, axes, mask):
+    count = lax.axis_size(axes)
+    return lax.ppermute(array, axes, [(i, i ^ mask) for i in range(count)])
+
+
+def chain_layout(order, home):
+    bits = len(order)
+    return [bits - 1 - home[b] for b in order]
+
+
+def halving_scatter(packed, axes, orders, widths, home):
+    bits = len(orders[0])
+    count = packed.shape[0]
+    where = lax.axis_index(axes)
+    bufs = []
+    col = 0
+    for order, width in zip(orders, widths):
+        part = packed[:, col : col + width].reshape((2,) * bits + (width,))
+        part = jnp.transpose(part, chain_layout(order, home) + [bits])
+        bufs.append(part.reshape(count, width))
+        col += width
+    for step in range(bits):
+        keeps, sends = [], []
+        for i, order in enumerate(orders):
+            bit = (where >> order[step]) & 1
+            buf = bufs[i]
+            halves = buf.reshape((2, buf.shape[0] // 2, buf.shape[1]))
+            keeps.append(lax.dynamic_index_in_dim(halves, bit, 0, keepdims=False))
+            sends.append(lax.dynamic_index_in_dim(halves, 1 - bit, 0, keepdims=False))
+        sends = lax.optimization_barrier(sends)
+        got = [exchange(send, axes, 1 << order[step]) for send, order in zip(sends, orders)]
+        got = lax.optimization_barrier(got)
+        bufs = [keep + recv for keep, recv in zip(keeps, got)]
+    return jnp.concatenate(bufs, axis=1)
+
+
+def doubling_gather(piece, axes, bits):
+    where = lax.axis_index(axes)
+    for b in bits:
+        got = exchange(piece, axes, 1 << b)
+        upper = ((where >> b) & 1) == 1
+        piece = jnp.where(upper, jnp.concatenate([got, piece]), jnp.concatenate([piece, got]))
+    return piece
 
 
 def per_device(signal, cotangent, w_taps, gate_bias, w_out):
@@ -56,15 +101,44 @@
     tapped_signal = contract_cols(later_pre, w_taps[:width])
     nearby = cotangent.astype(jnp.float32) + contract_cols(grad_pre, w_taps[width:])
     grad_in = (nearby + tapped_signal).astype(jnp.bfloat16)
-    total_taps, total_bias, total_out = lax.psum((part_taps, part_bias, part_out), ("grp", "seq"))
-    groups = lax.axis_size("seq")
-    where = lax.axis_index("seq")
-    share_taps = total_taps.shape[0] // groups
-    share_bias = total_bias.shape[0] // groups
-    share_out = total_out.shape[0] // groups
-    grad_taps = lax.dynamic_slice_in_dim(total_taps, where * share_taps, share_taps, 0)
-    grad_bias = lax.dynamic_slice_in_dim(total_bias, where * share_bias, share_bias, 0)
-    grad_out = lax.dynamic_slice_in_dim(total_out, where * share_out, share_out, 0)
+    seq_n = lax.axis_size("seq")
+    grp_n = lax.axis_size("grp")
+    chunks = seq_n * grp_n
+    pair = part_bias.shape[0] // chunks
+    used = part_taps.shape[1] + part_out.shape[1] + pair
+    lanes = 128
+    width = -(-used // lanes) * lanes
+    packed = jnp.concatenate(
+        [
+            part_taps.reshape(chunks, -1),
+            part_out.reshape(chunks, -1),
+            part_bias.reshape(chunks, pair),
+            jnp.zeros((chunks, width - used), jnp.float32),
+        ],
+        axis=1,
+    )
+    seq_bits = seq_n.bit_length() - 1
+    grp_bits = grp_n.bit_length() - 1
+    home = {}
+    for b in range(seq_bits + grp_bits):
+        home[b] = b + grp_bits if b < seq_bits else b - seq_bits
+    core, x_hi, y1, y2, y4 = 0, 1, 2, 3, 4
+    z1, z2, z4, x_lo = 5, 6, 7, 8
+    orders = (
+        [core, y1, z1, x_lo, y2, z2, x_hi, y4, z4],
+        [core, z1, x_lo, y1, z2, x_hi, y2, z4, y4],
+        [core, x_lo, y1, z1, x_hi, y2, z2, y4, z4],
+    )
+    lanes_per = width // lanes
+    split = [lanes_per // 3 + (1 if i < lanes_per % 3 else 0) for i in range(3)]
+    widths = [n * lanes for n in split]
+    mine = halving_scatter(packed, ("grp", "seq"), orders, widths, home)
+    share = doubling_gather(mine, ("grp", "seq"), [z1, z2, z4, x_lo])
+    taps_w = part_taps.shape[1]
+    out_w = part_out.shape[1]
+    grad_taps = share[:, :taps_w]
+    grad_out = share[:, taps_w : taps_w + out_w]
+    grad_bias = share[:, taps_w + out_w : used].reshape(-1)
     return (block_out, grad_in, grad_taps, grad_bias, grad_out)
 
 

time: 322 us -> 195 us (0.61)
  the two profiles are of different devices: /device:TPU:56 before, /device:TPU:120 now
where the time goes in v3:
time: 195 us; the launch traced here: 194 us
  starting transfers between devices  125 us (64%)
  waiting for transfers between devices  44.5 us (23%)
  local copies, waits for them, and re-layouts  12.7 us (7%)
  matrix products  6.05 us (3%)
  other arithmetic  4.41 us (2%)
    ppermute x31, starting transfers between devices, exchange(): return lax.ppermute(array, axes, [(i, i ^ mask) for i in range(count)])  115 us
    ppermute x31, waiting for transfers between devices, exchange(): return lax.ppermute(array, axes, [(i, i ^ mask) for i in range(count)])  41.2 us
    ppermute x2, starting transfers between devices, from_behind(): return lax.ppermute(array, axis, pairs)  9.85 us
  transfers between devices with their start and end apart: 33, of which 13 were waited for; matrix products, arithmetic and copies ran while one was open for 2% of the time, Pallas kernels for 0%

profile of v3, /device:TPU:120, one launch (start us, length us, event | category | flops | bytes accessed | tf_op | source)
XLA Modules:
  0.0 194.3 jit_solution(14135189444119215899)
XLA Ops:
  0.7 5.1 %collective-permute-start = (bf16[256,256]{1,0:T(8,128)(2,1)}, bf16[256,256]{1,0:T(8,128)(2,1)S(1)}, u32[]{:S(2)}, u32[]{:S(2)}) collective-permute-start(bf16[256,256]{1,0:T(8,128)(2,1)} %param.5), channel_id=1, source_target_pairs={{0,2},{1,3},{2,4},{3,5},{4,6},{5,7},{6,8},{7,9},{8,10},{9,11},{10,... | collective-permute-start | bytes 393224 | tf_op jit(solution)/shard_map/ppermute | solution.py:10
  5.7 1.4 fusion.10
  7.3 3.3 %collective-permute-done = bf16[256,256]{1,0:T(8,128)(2,1)S(1)} collective-permute-done((bf16[256,256]{1,0:T(8,128)(2,1)}, bf16[256,256]{1,0:T(8,128)(2,1)S(1)}, u32[]{:S(2)}, u32[]{:S(2)}) %collective-permute-start) | collective-permute-done | bytes 131104 | tf_op jit(solution)/shard_map/ppermute | solution.py:10
  10.5 0.7 copy-done.9
  11.6 1.2 multiply_convert_fusion.1
  14.3 0.6 reshape.104
  14.9 0.8 copy.13
  15.8 0.6 reshape.105
  16.4 0.8 copy.14
  17.2 1.8 constant_dynamic-slice_fusion.21
  19.0 0.8 copy.29
  19.9 0.8 copy.30
  22.7 0.7 constant_dynamic-slice_fusion.20
  23.4 1.9 collective-permute-start.2
  25.4 2.4 %collective-permute-start.3 = (f32[256,512]{1,0:T(8,128)}, f32[256,512]{1,0:T(8,128)}, u32[]{:S(2)}, u32[]{:S(2)}) collective-permute-start(f32[256,512]{1,0:T(8,128)} %bitcast.158), channel_id=1, source_target_pairs={{0,1},{1,0},{2,3},{3,2},{4,5},{5,4},{6,7},{7,6},{8,9},{9,8},{10,11... | collective-permute-start | bytes 1572872 | tf_op jit(solution)/shard_map/ppermute | solution.py:27
  27.8 1.9 collective-permute-start.4
  29.7 1.7 collective-permute-done.4
  31.5 0.7 dynamic-slice_bitcast_fusion.2
  32.2 1.1 bitcast_add_fusion
  33.3 1.1 bitcast_add_fusion.1
  34.5 3.3 %collective-permute-start.5 = (f32[128,512]{1,0:T(8,128)S(1)}, f32[128,512]{1,0:T(8,128)S(1)}, u32[]{:S(2)}, u32[]{:S(2)}) collective-permute-start(f32[128,512]{1,0:T(8,128)S(1)} %dynamic-slice_bitcast_fusion.1), channel_id=1, source_target_pairs={{0,4},{1,5},{2,6},{3,7},{4,0},{5,1},{6,2},{7,3},{8,12},{9,13},{10,... | collective-permute-start | bytes 786440 | tf_op jit(solution)/shard_map/ppermute | solution.py:27
  37.8 1.9 collective-permute-start.6
  39.7 3.4 %collective-permute-start.7 = (f32[128,384]{1,0:T(8,128)}, f32[128,384]{1,0:T(8,128)}, u32[]{:S(2)}, u32[]{:S(2)}) collective-permute-start(f32[128,384]{1,0:T(8,128)} %dynamic-slice_bitcast_fusion.2), channel_id=1, source_target_pairs={{0,256},{1,257},{2,258},{3,259},{4,260},{5,261},{6,262},{7,263},{8... | collective-permute-start | bytes 589832 | tf_op jit(solution)/shard_map/ppermute | solution.py:27
  43.1 5.5 %collective-permute-done.7 = f32[128,384]{1,0:T(8,128)} collective-permute-done((f32[128,384]{1,0:T(8,128)}, f32[128,384]{1,0:T(8,128)}, u32[]{:S(2)}, u32[]{:S(2)}) %collective-permute-start.7) | collective-permute-done | bytes 196640 | tf_op jit(solution)/shard_map/ppermute | solution.py:27
  48.6 1.0 bitcast_add_fusion.5
  49.7 3.6 %collective-permute-start.8 = (f32[64,512]{1,0:T(8,128)S(1)}, f32[64,512]{1,0:T(8,128)S(1)}, u32[]{:S(2)}, u32[]{:S(2)}) collective-permute-start(f32[64,512]{1,0:T(8,128)S(1)} %dynamic-slice_bitcast_fusion.4), channel_id=1, source_target_pairs={{0,32},{1,33},{2,34},{3,35},{4,36},{5,37},{6,38},{7,39},{8,40},{9,... | collective-permute-start | bytes 393224 | tf_op jit(solution)/shard_map/ppermute | solution.py:27
  53.3 3.4 %collective-permute-start.9 = (f32[64,512]{1,0:T(8,128)S(1)}, f32[64,512]{1,0:T(8,128)S(1)}, u32[]{:S(2)}, u32[]{:S(2)}) collective-permute-start(f32[64,512]{1,0:T(8,128)S(1)} %dynamic-slice_bitcast_fusion.3), channel_id=1, source_target_pairs={{0,256},{1,257},{2,258},{3,259},{4,260},{5,261},{6,262},{7,263},{8... | collective-permute-start | bytes 393224 | tf_op jit(solution)/shard_map/ppermute | solution.py:27
  56.7 2.6 %collective-permute-start.10 = (f32[64,384]{1,0:T(8,128)S(1)}, f32[64,384]{1,0:T(8,128)S(1)}, u32[]{:S(2)}, u32[]{:S(2)}) collective-permute-start(f32[64,384]{1,0:T(8,128)S(1)} %dynamic-slice_bitcast_fusion.5), channel_id=1, source_target_pairs={{0,4},{1,5},{2,6},{3,7},{4,0},{5,1},{6,2},{7,3},{8,12},{9,13},{10,... | collective-permute-start | bytes 294920 | tf_op jit(solution)/shard_map/ppermute | solution.py:27
  59.3 3.9 %collective-permute-done.10 = f32[64,384]{1,0:T(8,128)S(1)} collective-permute-done((f32[64,384]{1,0:T(8,128)S(1)}, f32[64,384]{1,0:T(8,128)S(1)}, u32[]{:S(2)}, u32[]{:S(2)}) %collective-permute-start.10) | collective-permute-done | bytes 98336 | tf_op jit(solution)/shard_map/ppermute | solution.py:27
  63.4 2.6 %collective-permute-start.11 = (f32[32,512]{1,0:T(8,128)S(1)}, f32[32,512]{1,0:T(8,128)S(1)}, u32[]{:S(2)}, u32[]{:S(2)}) collective-permute-start(f32[32,512]{1,0:T(8,128)S(1)} %dynamic-slice_bitcast_fusion.7), channel_id=1, source_target_pairs={{0,256},{1,257},{2,258},{3,259},{4,260},{5,261},{6,262},{7,263},{8... | collective-permute-start | bytes 196616 | tf_op jit(solution)/shard_map/ppermute | solution.py:27
  66.0 2.6 %collective-permute-start.12 = (f32[32,512]{1,0:T(8,128)S(1)}, f32[32,512]{1,0:T(8,128)S(1)}, u32[]{:S(2)}, u32[]{:S(2)}) collective-permute-start(f32[32,512]{1,0:T(8,128)S(1)} %dynamic-slice_bitcast_fusion.6), channel_id=1, source_target_pairs={{0,4},{1,5},{2,6},{3,7},{4,0},{5,1},{6,2},{7,3},{8,12},{9,13},{10,... | collective-permute-start | bytes 196616 | tf_op jit(solution)/shard_map/ppermute | solution.py:27
  68.6 2.2 %collective-permute-start.13 = (f32[32,384]{1,0:T(8,128)S(1)}, f32[32,384]{1,0:T(8,128)S(1)}, u32[]{:S(2)}, u32[]{:S(2)}) collective-permute-start(f32[32,384]{1,0:T(8,128)S(1)} %dynamic-slice_bitcast_fusion.8), channel_id=1, source_target_pairs={{0,32},{1,33},{2,34},{3,35},{4,36},{5,37},{6,38},{7,39},{8,40},{9,... | collective-permute-start | bytes 147464 | tf_op jit(solution)/shard_map/ppermute | solution.py:27
  70.8 3.8 %collective-permute-done.13 = f32[32,384]{1,0:T(8,128)S(1)} collective-permute-done((f32[32,384]{1,0:T(8,128)S(1)}, f32[32,384]{1,0:T(8,128)S(1)}, u32[]{:S(2)}, u32[]{:S(2)}) %collective-permute-start.13) | collective-permute-done | bytes 49184 | tf_op jit(solution)/shard_map/ppermute | solution.py:27
  74.7 4.9 %collective-permute-start.14 = (f32[16,512]{1,0:T(8,128)S(1)}, f32[16,512]{1,0:T(8,128)S(1)}, u32[]{:S(2)}, u32[]{:S(2)}) collective-permute-start(f32[16,512]{1,0:T(8,128)S(1)} %dynamic-slice_bitcast_fusion.10), channel_id=1, source_target_pairs={{0,8},{1,9},{2,10},{3,11},{4,12},{5,13},{6,14},{7,15},{8,0},{9,1},... | collective-permute-start | bytes 98312 | tf_op jit(solution)/shard_map/ppermute | solution.py:27
  79.6 6.1 %collective-permute-start.15 = (f32[16,512]{1,0:T(8,128)S(1)}, f32[16,512]{1,0:T(8,128)S(1)}, u32[]{:S(2)}, u32[]{:S(2)}) collective-permute-start(f32[16,512]{1,0:T(8,128)S(1)} %dynamic-slice_bitcast_fusion.9), channel_id=1, source_target_pairs={{0,64},{1,65},{2,66},{3,67},{4,68},{5,69},{6,70},{7,71},{8,72},{9,... | collective-permute-start | bytes 98312 | tf_op jit(solution)/shard_map/ppermute | solution.py:27
  85.7 3.2 %collective-permute-start.16 = (f32[16,384]{1,0:T(8,128)S(1)}, f32[16,384]{1,0:T(8,128)S(1)}, u32[]{:S(2)}, u32[]{:S(2)}) collective-permute-start(f32[16,384]{1,0:T(8,128)S(1)} %dynamic-slice_bitcast_fusion.11), channel_id=1, source_target_pairs={{0,2},{1,3},{2,0},{3,1},{4,6},{5,7},{6,4},{7,5},{8,10},{9,11},{10,... | collective-permute-start | bytes 73736 | tf_op jit(solution)/shard_map/ppermute | solution.py:27
  88.9 4.0 %collective-permute-done.16 = f32[16,384]{1,0:T(8,128)S(1)} collective-permute-done((f32[16,384]{1,0:T(8,128)S(1)}, f32[16,384]{1,0:T(8,128)S(1)}, u32[]{:S(2)}, u32[]{:S(2)}) %collective-permute-start.16) | collective-permute-done | bytes 24608 | tf_op jit(solution)/shard_map/ppermute | solution.py:27
  93.0 1.9 collective-permute-start.17
  95.0 3.2 %collective-permute-start.18 = (f32[8,512]{1,0:T(8,128)S(1)}, f32[8,512]{1,0:T(8,128)S(1)}, u32[]{:S(2)}, u32[]{:S(2)}) collective-permute-start(f32[8,512]{1,0:T(8,128)S(1)} %dynamic-slice_bitcast_fusion.12), channel_id=1, source_target_pairs={{0,2},{1,3},{2,0},{3,1},{4,6},{5,7},{6,4},{7,5},{8,10},{9,11},{10,... | collective-permute-start | bytes 49160 | tf_op jit(solution)/shard_map/ppermute | solution.py:27
  98.2 2.7 %collective-permute-start.19 = (f32[8,384]{1,0:T(8,128)S(1)}, f32[8,384]{1,0:T(8,128)S(1)}, u32[]{:S(2)}, u32[]{:S(2)}) collective-permute-start(f32[8,384]{1,0:T(8,128)S(1)} %fusion.15), channel_id=1, source_target_pairs={{0,8},{1,9},{2,10},{3,11},{4,12},{5,13},{6,14},{7,15},{8,0},{9,1},... | collective-permute-start | bytes 36872 | tf_op jit(solution)/shard_map/ppermute | solution.py:27
  100.9 3.8 %collective-permute-done.19 = f32[8,384]{1,0:T(8,128)S(1)} collective-permute-done((f32[8,384]{1,0:T(8,128)S(1)}, f32[8,384]{1,0:T(8,128)S(1)}, u32[]{:S(2)}, u32[]{:S(2)}) %collective-permute-start.19) | collective-permute-done | bytes 12320 | tf_op jit(solution)/shard_map/ppermute | solution.py:27
  104.8 4.1 %collective-permute-start.20 = (f32[4,512]{1,0:T(4,128)S(1)}, f32[4,512]{1,0:T(4,128)S(1)}, u32[]{:S(2)}, u32[]{:S(2)}) collective-permute-start(f32[4,512]{1,0:T(4,128)S(1)} %fusion.20), channel_id=1, source_target_pairs={{0,2},{1,3},{2,0},{3,1},{4,6},{5,7},{6,4},{7,5},{8,10},{9,11},{10,... | collective-permute-start | bytes 24584 | tf_op jit(solution)/shard_map/ppermute | solution.py:27
  109.0 1.9 collective-permute-start.21
  110.9 4.8 %collective-permute-start.22 = (f32[4,384]{1,0:T(4,128)S(1)}, f32[4,384]{1,0:T(4,128)S(1)}, u32[]{:S(2)}, u32[]{:S(2)}) collective-permute-start(f32[4,384]{1,0:T(4,128)S(1)} %fusion.24), channel_id=1, source_target_pairs={{0,64},{1,65},{2,66},{3,67},{4,68},{5,69},{6,70},{7,71},{8,72},{9,... | collective-permute-start | bytes 18440 | tf_op jit(solution)/shard_map/ppermute | solution.py:27
  115.7 1.6 collective-permute-done.22
  117.5 6.0 %collective-permute-start.23 = (f32[2,512]{1,0:T(2,128)S(1)}, f32[2,512]{1,0:T(2,128)S(1)}, u32[]{:S(2)}, u32[]{:S(2)}) collective-permute-start(f32[2,512]{1,0:T(2,128)S(1)} %fusion.29), channel_id=1, source_target_pairs={{0,16},{1,17},{2,18},{3,19},{4,20},{5,21},{6,22},{7,23},{8,24},{9,... | collective-permute-start | bytes 12296 | tf_op jit(solution)/shard_map/ppermute | solution.py:27
  123.4 7.5 %collective-permute-start.24 = (f32[2,512]{1,0:T(2,128)S(1)}, f32[2,512]{1,0:T(2,128)S(1)}, u32[]{:S(2)}, u32[]{:S(2)}) collective-permute-start(f32[2,512]{1,0:T(2,128)S(1)} %fusion.30), channel_id=1, source_target_pairs={{0,128},{1,129},{2,130},{3,131},{4,132},{5,133},{6,134},{7,135},{8... | collective-permute-start | bytes 12296 | tf_op jit(solution)/shard_map/ppermute | solution.py:27
  130.9 5.1 %collective-permute-start.25 = (f32[2,384]{1,0:T(2,128)S(1)}, f32[2,384]{1,0:T(2,128)S(1)}, u32[]{:S(2)}, u32[]{:S(2)}) collective-permute-start(f32[2,384]{1,0:T(2,128)S(1)} %fusion.33), channel_id=1, source_target_pairs={{0,16},{1,17},{2,18},{3,19},{4,20},{5,21},{6,22},{7,23},{8,24},{9,... | collective-permute-start | bytes 9224 | tf_op jit(solution)/shard_map/ppermute | solution.py:27
  136.0 4.3 %collective-permute-done.25 = f32[2,384]{1,0:T(2,128)S(1)} collective-permute-done((f32[2,384]{1,0:T(2,128)S(1)}, f32[2,384]{1,0:T(2,128)S(1)}, u32[]{:S(2)}, u32[]{:S(2)}) %collective-permute-start.25) | collective-permute-done | bytes 3104 | tf_op jit(solution)/shard_map/ppermute | solution.py:27
  140.4 2.3 %collective-permute-start.26 = (f32[1,512]{1,0:T(1,128)S(1)}, f32[1,512]{1,0:T(1,128)S(1)}, u32[]{:S(2)}, u32[]{:S(2)}) collective-permute-start(f32[1,512]{1,0:T(1,128)S(1)} %constant_dynamic-slice_fusion.6), channel_id=1, source_target_pairs={{0,128},{1,129},{2,130},{3,131},{4,132},{5,133},{6,134},{7,135},{8... | collective-permute-start | bytes 6152 | tf_op jit(solution)/shard_map/ppermute | solution.py:27
  142.7 4.7 %collective-permute-start.27 = (f32[1,512]{1,0:T(1,128)S(1)}, f32[1,512]{1,0:T(1,128)S(1)}, u32[]{:S(2)}, u32[]{:S(2)}) collective-permute-start(f32[1,512]{1,0:T(1,128)S(1)} %constant_dynamic-slice_fusion.4), channel_id=1, source_target_pairs={{0,16},{1,17},{2,18},{3,19},{4,20},{5,21},{6,22},{7,23},{8,24},{9,... | collective-permute-start | bytes 6152 | tf_op jit(solution)/shard_map/ppermute | solution.py:27
  147.4 7.8 %collective-permute-start.28 = (f32[1,384]{1,0:T(1,128)S(1)}, f32[1,384]{1,0:T(1,128)S(1)}, u32[]{:S(2)}, u32[]{:S(2)}) collective-permute-start(f32[1,384]{1,0:T(1,128)S(1)} %constant_dynamic-slice_fusion.2), channel_id=1, source_target_pairs={{0,128},{1,129},{2,130},{3,131},{4,132},{5,133},{6,134},{7,135},{8... | collective-permute-start | bytes 4616 | tf_op jit(solution)/shard_map/ppermute | solution.py:27
  155.3 1.5 collective-permute-done.28
  156.9 2.5 %collective-permute-start.29 = (f32[1,1408]{1,0:T(1,128)S(1)}, f32[1,1408]{1,0:T(1,128)S(1)}, u32[]{:S(2)}, u32[]{:S(2)}) collective-permute-start(f32[1,1408]{1,0:T(1,128)S(1)} %pad_maximum_fusion.2), channel_id=1, source_target_pairs={{0,32},{1,33},{2,34},{3,35},{4,36},{5,37},{6,38},{7,39},{8,40},{9,... | collective-permute-start | bytes 16904 | tf_op jit(solution)/shard_map/ppermute | solution.py:27
  159.7 2.7 %collective-permute-done.29 = f32[1,1408]{1,0:T(1,128)S(1)} collective-permute-done((f32[1,1408]{1,0:T(1,128)S(1)}, f32[1,1408]{1,0:T(1,128)S(1)}, u32[]{:S(2)}, u32[]{:S(2)}) %collective-permute-start.29) | collective-permute-done | bytes 5664 | tf_op jit(solution)/shard_map/ppermute | solution.py:27
  162.4 4.4 %collective-permute-start.30 = (f32[2,1408]{1,0:T(2,128)S(1)}, f32[2,1408]{1,0:T(2,128)S(1)}, u32[]{:S(2)}, u32[]{:S(2)}) collective-permute-start(f32[2,1408]{1,0:T(2,128)S(1)} %maximum_select_fusion.3), channel_id=1, source_target_pairs={{0,64},{1,65},{2,66},{3,67},{4,68},{5,69},{6,70},{7,71},{8,72},{9,... | collective-permute-start | bytes 33800 | tf_op jit(solution)/shard_map/ppermute | solution.py:27
  166.9 4.8 %collective-permute-start.1 = (bf16[256,1024]{1,0:T(8,128)(2,1)S(1)}, bf16[256,1024]{1,0:T(8,128)(2,1)S(1)}, u32[]{:S(2)}, u32[]{:S(2)}) collective-permute-start(bf16[256,1024]{1,0:T(8,128)(2,1)S(1)} %pad_maximum_fusion.1), channel_id=1, source_target_pairs={{2,0},{3,1},{4,2},{5,3},{6,4},{7,5},{8,6},{9,7},{10,8},{11,9},{12,... | collective-permute-start | bytes 1572872 | tf_op jit(solution)/shard_map/ppermute | solution.py:10
  171.7 7.8 %collective-permute-start.31 = (f32[4,1408]{1,0:T(4,128)S(1)}, f32[4,1408]{1,0:T(4,128)S(1)}, u32[]{:S(2)}, u32[]{:S(2)}) collective-permute-start(f32[4,1408]{1,0:T(4,128)S(1)} %maximum_select_fusion.2), channel_id=1, source_target_pairs={{0,128},{1,129},{2,130},{3,131},{4,132},{5,133},{6,134},{7,135},{8... | collective-permute-start | bytes 67592 | tf_op jit(solution)/shard_map/ppermute | solution.py:27
  179.5 0.9 fusion.1
  180.4 6.0 %collective-permute-done.31 = f32[4,1408]{1,0:T(4,128)S(1)} collective-permute-done((f32[4,1408]{1,0:T(4,128)S(1)}, f32[4,1408]{1,0:T(4,128)S(1)}, u32[]{:S(2)}, u32[]{:S(2)}) %collective-permute-start.31) | collective-permute-done | bytes 22560 | tf_op jit(solution)/shard_map/ppermute | solution.py:27
  186.5 2.5 %collective-permute-start.32 = (f32[8,1408]{1,0:T(8,128)S(1)}, f32[8,1408]{1,0:T(8,128)S(1)}, u32[]{:S(2)}, u32[]{:S(2)}) collective-permute-start(f32[8,1408]{1,0:T(8,128)S(1)} %maximum_select_fusion.1), channel_id=1, source_target_pairs={{0,256},{1,257},{2,258},{3,259},{4,260},{5,261},{6,262},{7,263},{8... | collective-permute-start | bytes 135176 | tf_op jit(solution)/shard_map/ppermute | solution.py:27
  189.0 1.0 fusion.2
  190.0 2.4 %collective-permute-done.32 = f32[8,1408]{1,0:T(8,128)S(1)} collective-permute-done((f32[8,1408]{1,0:T(8,128)S(1)}, f32[8,1408]{1,0:T(8,128)S(1)}, u32[]{:S(2)}, u32[]{:S(2)}) %collective-permute-start.32) | collective-permute-done | bytes 45088 | tf_op jit(solution)/shard_map/ppermute | solution.py:27
  192.4 0.6 slice.42
  (126 shorter events, 6.5 us)
Async XLA Ops:
  0.6 10.9 %copy-start = (bf16[512,256]{1,0:T(8,128)(2,1)S(1)}, bf16[512,256]{1,0:T(8,128)(2,1)}, u32[]{:S(2)}) copy-start(bf16[512,256]{1,0:T(8,128)(2,1)} %param.9) | copy-start | bytes 786436
  0.6 10.6 %copy-start.5 = (bf16[512,1024]{1,0:T(8,128)(2,1)S(1)}, bf16[512,1024]{1,0:T(8,128)(2,1)}, u32[]{:S(2)}) copy-start(bf16[512,1024]{1,0:T(8,128)(2,1)} %param.7) | copy-start | bytes 3145732
  0.7 10.5 %copy-start.14 = (f32[1024]{0:T(1024)S(1)}, f32[1024]{0:T(1024)}, u32[]{:S(2)}) copy-start(f32[1024]{0:T(1024)} %param.8) | copy-start | bytes 12292
  0.7 9.9 %collective-permute-start = (bf16[256,256]{1,0:T(8,128)(2,1)}, bf16[256,256]{1,0:T(8,128)(2,1)S(1)}, u32[]{:S(2)}, u32[]{:S(2)}) collective-permute-start(bf16[256,256]{1,0:T(8,128)(2,1)} %param.5), channel_id=1, source_target_pairs={{0,2},{1,3},{2,4},{3,5},{4,6},{5,7},{6,8},{7,9},{8,10},{9,11},{10,... | collective-permute-start | bytes 393224 | tf_op jit(solution)/shard_map/ppermute | solution.py:10
  7.3 4.3 %copy-start.11 = (bf16[256,256]{1,0:T(8,128)(2,1)S(1)}, bf16[256,256]{1,0:T(8,128)(2,1)}, u32[]{:S(2)}) copy-start(bf16[256,256]{1,0:T(8,128)(2,1)} %param.6) | copy-start | bytes 393220
  10.5 0.7 copy-start.9
  11.5 1.2 copy-start.7
  12.7 0.7 copy-start.1
  12.7 0.8 copy-start.3
  12.7 1.0 copy-start.10
  19.9 1.4 copy-start.8
  19.9 1.4 copy-start.12
  23.4 8.0 %collective-permute-start.2 = (f32[256,512]{1,0:T(8,128)}, f32[256,512]{1,0:T(8,128)}, u32[]{:S(2)}, u32[]{:S(2)}) collective-permute-start(f32[256,512]{1,0:T(8,128)} %bitcast.159), channel_id=1, source_target_pairs={{0,1},{1,0},{2,3},{3,2},{4,5},{5,4},{6,7},{7,6},{8,9},{9,8},{10,11... | collective-permute-start | bytes 1572872 | tf_op jit(solution)/shard_map/ppermute | solution.py:27
  25.4 6.0 %collective-permute-start.3 = (f32[256,512]{1,0:T(8,128)}, f32[256,512]{1,0:T(8,128)}, u32[]{:S(2)}, u32[]{:S(2)}) collective-permute-start(f32[256,512]{1,0:T(8,128)} %bitcast.158), channel_id=1, source_target_pairs={{0,1},{1,0},{2,3},{3,2},{4,5},{5,4},{6,7},{7,6},{8,9},{9,8},{10,11... | collective-permute-start | bytes 1572872 | tf_op jit(solution)/shard_map/ppermute | solution.py:27
  27.8 3.6 %collective-permute-start.4 = (f32[256,384]{1,0:T(8,128)S(1)}, f32[256,384]{1,0:T(8,128)S(1)}, u32[]{:S(2)}, u32[]{:S(2)}) collective-permute-start(f32[256,384]{1,0:T(8,128)S(1)} %bitcast.180), channel_id=1, source_target_pairs={{0,1},{1,0},{2,3},{3,2},{4,5},{5,4},{6,7},{7,6},{8,9},{9,8},{10,11... | collective-permute-start | bytes 1179656 | tf_op jit(solution)/shard_map/ppermute | solution.py:27
  34.5 14.1 %collective-permute-start.5 = (f32[128,512]{1,0:T(8,128)S(1)}, f32[128,512]{1,0:T(8,128)S(1)}, u32[]{:S(2)}, u32[]{:S(2)}) collective-permute-start(f32[128,512]{1,0:T(8,128)S(1)} %dynamic-slice_bitcast_fusion.1), channel_id=1, source_target_pairs={{0,4},{1,5},{2,6},{3,7},{4,0},{5,1},{6,2},{7,3},{8,12},{9,13},{10,... | collective-permute-start | bytes 786440 | tf_op jit(solution)/shard_map/ppermute | solution.py:27
  37.8 10.8 %collective-permute-start.6 = (f32[128,512]{1,0:T(8,128)S(1)}, f32[128,512]{1,0:T(8,128)S(1)}, u32[]{:S(2)}, u32[]{:S(2)}) collective-permute-start(f32[128,512]{1,0:T(8,128)S(1)} %dynamic-slice_bitcast_fusion), channel_id=1, source_target_pairs={{0,32},{1,33},{2,34},{3,35},{4,36},{5,37},{6,38},{7,39},{8,40},{9,... | collective-permute-start | bytes 786440 | tf_op jit(solution)/shard_map/ppermute | solution.py:27
  39.7 8.9 %collective-permute-start.7 = (f32[128,384]{1,0:T(8,128)}, f32[128,384]{1,0:T(8,128)}, u32[]{:S(2)}, u32[]{:S(2)}) collective-permute-start(f32[128,384]{1,0:T(8,128)} %dynamic-slice_bitcast_fusion.2), channel_id=1, source_target_pairs={{0,256},{1,257},{2,258},{3,259},{4,260},{5,261},{6,262},{7,263},{8... | collective-permute-start | bytes 589832 | tf_op jit(solution)/shard_map/ppermute | solution.py:27
  49.7 13.6 %collective-permute-start.8 = (f32[64,512]{1,0:T(8,128)S(1)}, f32[64,512]{1,0:T(8,128)S(1)}, u32[]{:S(2)}, u32[]{:S(2)}) collective-permute-start(f32[64,512]{1,0:T(8,128)S(1)} %dynamic-slice_bitcast_fusion.4), channel_id=1, source_target_pairs={{0,32},{1,33},{2,34},{3,35},{4,36},{5,37},{6,38},{7,39},{8,40},{9,... | collective-permute-start | bytes 393224 | tf_op jit(solution)/shard_map/ppermute | solution.py:27
  53.3 9.9 %collective-permute-start.9 = (f32[64,512]{1,0:T(8,128)S(1)}, f32[64,512]{1,0:T(8,128)S(1)}, u32[]{:S(2)}, u32[]{:S(2)}) collective-permute-start(f32[64,512]{1,0:T(8,128)S(1)} %dynamic-slice_bitcast_fusion.3), channel_id=1, source_target_pairs={{0,256},{1,257},{2,258},{3,259},{4,260},{5,261},{6,262},{7,263},{8... | collective-permute-start | bytes 393224 | tf_op jit(solution)/shard_map/ppermute | solution.py:27
  56.7 6.5 %collective-permute-start.10 = (f32[64,384]{1,0:T(8,128)S(1)}, f32[64,384]{1,0:T(8,128)S(1)}, u32[]{:S(2)}, u32[]{:S(2)}) collective-permute-start(f32[64,384]{1,0:T(8,128)S(1)} %dynamic-slice_bitcast_fusion.5), channel_id=1, source_target_pairs={{0,4},{1,5},{2,6},{3,7},{4,0},{5,1},{6,2},{7,3},{8,12},{9,13},{10,... | collective-permute-start | bytes 294920 | tf_op jit(solution)/shard_map/ppermute | solution.py:27
  63.3 96.0 %copy-start.2 = (bf16[256,512]{1,0:T(8,128)(2,1)S(1)}, bf16[256,512]{1,0:T(8,128)(2,1)}, u32[]{:S(2)}) copy-start(bf16[256,512]{1,0:T(8,128)(2,1)} %copy-done.1) | copy-start | bytes 786436
  63.4 96.0 %copy-start.4 = (bf16[256,512]{1,0:T(8,128)(2,1)S(1)}, bf16[256,512]{1,0:T(8,128)(2,1)}, u32[]{:S(2)}) copy-start(bf16[256,512]{1,0:T(8,128)(2,1)} %copy-done.3) | copy-start | bytes 786436
  63.4 96.0 %copy-start.6 = (bf16[512,1024]{1,0:T(8,128)(2,1)S(1)}, bf16[512,1024]{1,0:T(8,128)(2,1)}, u32[]{:S(2)}) copy-start(bf16[512,1024]{1,0:T(8,128)(2,1)} %param.7) | copy-start | bytes 3145732
  63.4 96.0 %copy-start.13 = (bf16[256,256]{1,0:T(8,128)(2,1)S(1)}, bf16[256,256]{1,0:T(8,128)(2,1)}, u32[]{:S(2)}) copy-start(bf16[256,256]{1,0:T(8,128)(2,1)} %param.6) | copy-start | bytes 393220
  63.4 11.2 %collective-permute-start.11 = (f32[32,512]{1,0:T(8,128)S(1)}, f32[32,512]{1,0:T(8,128)S(1)}, u32[]{:S(2)}, u32[]{:S(2)}) collective-permute-start(f32[32,512]{1,0:T(8,128)S(1)} %dynamic-slice_bitcast_fusion.7), channel_id=1, source_target_pairs={{0,256},{1,257},{2,258},{3,259},{4,260},{5,261},{6,262},{7,263},{8... | collective-permute-start | bytes 196616 | tf_op jit(solution)/shard_map/ppermute | solution.py:27
  66.0 8.6 %collective-permute-start.12 = (f32[32,512]{1,0:T(8,128)S(1)}, f32[32,512]{1,0:T(8,128)S(1)}, u32[]{:S(2)}, u32[]{:S(2)}) collective-permute-start(f32[32,512]{1,0:T(8,128)S(1)} %dynamic-slice_bitcast_fusion.6), channel_id=1, source_target_pairs={{0,4},{1,5},{2,6},{3,7},{4,0},{5,1},{6,2},{7,3},{8,12},{9,13},{10,... | collective-permute-start | bytes 196616 | tf_op jit(solution)/shard_map/ppermute | solution.py:27
  68.6 6.0 %collective-permute-start.13 = (f32[32,384]{1,0:T(8,128)S(1)}, f32[32,384]{1,0:T(8,128)S(1)}, u32[]{:S(2)}, u32[]{:S(2)}) collective-permute-start(f32[32,384]{1,0:T(8,128)S(1)} %dynamic-slice_bitcast_fusion.8), channel_id=1, source_target_pairs={{0,32},{1,33},{2,34},{3,35},{4,36},{5,37},{6,38},{7,39},{8,40},{9,... | collective-permute-start | bytes 147464 | tf_op jit(solution)/shard_map/ppermute | solution.py:27
  74.7 18.2 %collective-permute-start.14 = (f32[16,512]{1,0:T(8,128)S(1)}, f32[16,512]{1,0:T(8,128)S(1)}, u32[]{:S(2)}, u32[]{:S(2)}) collective-permute-start(f32[16,512]{1,0:T(8,128)S(1)} %dynamic-slice_bitcast_fusion.10), channel_id=1, source_target_pairs={{0,8},{1,9},{2,10},{3,11},{4,12},{5,13},{6,14},{7,15},{8,0},{9,1},... | collective-permute-start | bytes 98312 | tf_op jit(solution)/shard_map/ppermute | solution.py:27
  79.6 13.3 %collective-permute-start.15 = (f32[16,512]{1,0:T(8,128)S(1)}, f32[16,512]{1,0:T(8,128)S(1)}, u32[]{:S(2)}, u32[]{:S(2)}) collective-permute-start(f32[16,512]{1,0:T(8,128)S(1)} %dynamic-slice_bitcast_fusion.9), channel_id=1, source_target_pairs={{0,64},{1,65},{2,66},{3,67},{4,68},{5,69},{6,70},{7,71},{8,72},{9,... | collective-permute-start | bytes 98312 | tf_op jit(solution)/shard_map/ppermute | solution.py:27
  85.7 7.2 %collective-permute-start.16 = (f32[16,384]{1,0:T(8,128)S(1)}, f32[16,384]{1,0:T(8,128)S(1)}, u32[]{:S(2)}, u32[]{:S(2)}) collective-permute-start(f32[16,384]{1,0:T(8,128)S(1)} %dynamic-slice_bitcast_fusion.11), channel_id=1, source_target_pairs={{0,2},{1,3},{2,0},{3,1},{4,6},{5,7},{6,4},{7,5},{8,10},{9,11},{10,... | collective-permute-start | bytes 73736 | tf_op jit(solution)/shard_map/ppermute | solution.py:27
  93.0 11.6 %collective-permute-start.17 = (f32[8,512]{1,0:T(8,128)S(1)}, f32[8,512]{1,0:T(8,128)S(1)}, u32[]{:S(2)}, u32[]{:S(2)}) collective-permute-start(f32[8,512]{1,0:T(8,128)S(1)} %dynamic-slice_bitcast_fusion.13), channel_id=1, source_target_pairs={{0,64},{1,65},{2,66},{3,67},{4,68},{5,69},{6,70},{7,71},{8,72},{9,... | collective-permute-start | bytes 49160 | tf_op jit(solution)/shard_map/ppermute | solution.py:27
  95.0 9.7 %collective-permute-start.18 = (f32[8,512]{1,0:T(8,128)S(1)}, f32[8,512]{1,0:T(8,128)S(1)}, u32[]{:S(2)}, u32[]{:S(2)}) collective-permute-start(f32[8,512]{1,0:T(8,128)S(1)} %dynamic-slice_bitcast_fusion.12), channel_id=1, source_target_pairs={{0,2},{1,3},{2,0},{3,1},{4,6},{5,7},{6,4},{7,5},{8,10},{9,11},{10,... | collective-permute-start | bytes 49160 | tf_op jit(solution)/shard_map/ppermute | solution.py:27
  98.2 6.5 %collective-permute-start.19 = (f32[8,384]{1,0:T(8,128)S(1)}, f32[8,384]{1,0:T(8,128)S(1)}, u32[]{:S(2)}, u32[]{:S(2)}) collective-permute-start(f32[8,384]{1,0:T(8,128)S(1)} %fusion.15), channel_id=1, source_target_pairs={{0,8},{1,9},{2,10},{3,11},{4,12},{5,13},{6,14},{7,15},{8,0},{9,1},... | collective-permute-start | bytes 36872 | tf_op jit(solution)/shard_map/ppermute | solution.py:27
  104.8 12.5 %collective-permute-start.20 = (f32[4,512]{1,0:T(4,128)S(1)}, f32[4,512]{1,0:T(4,128)S(1)}, u32[]{:S(2)}, u32[]{:S(2)}) collective-permute-start(f32[4,512]{1,0:T(4,128)S(1)} %fusion.20), channel_id=1, source_target_pairs={{0,2},{1,3},{2,0},{3,1},{4,6},{5,7},{6,4},{7,5},{8,10},{9,11},{10,... | collective-permute-start | bytes 24584 | tf_op jit(solution)/shard_map/ppermute | solution.py:27
  109.0 8.4 %collective-permute-start.21 = (f32[4,512]{1,0:T(4,128)S(1)}, f32[4,512]{1,0:T(4,128)S(1)}, u32[]{:S(2)}, u32[]{:S(2)}) collective-permute-start(f32[4,512]{1,0:T(4,128)S(1)} %fusion.21), channel_id=1, source_target_pairs={{0,8},{1,9},{2,10},{3,11},{4,12},{5,13},{6,14},{7,15},{8,0},{9,1},... | collective-permute-start | bytes 24584 | tf_op jit(solution)/shard_map/ppermute | solution.py:27
  110.9 6.4 %collective-permute-start.22 = (f32[4,384]{1,0:T(4,128)S(1)}, f32[4,384]{1,0:T(4,128)S(1)}, u32[]{:S(2)}, u32[]{:S(2)}) collective-permute-start(f32[4,384]{1,0:T(4,128)S(1)} %fusion.24), channel_id=1, source_target_pairs={{0,64},{1,65},{2,66},{3,67},{4,68},{5,69},{6,70},{7,71},{8,72},{9,... | collective-permute-start | bytes 18440 | tf_op jit(solution)/shard_map/ppermute | solution.py:27
  117.5 22.8 %collective-permute-start.23 = (f32[2,512]{1,0:T(2,128)S(1)}, f32[2,512]{1,0:T(2,128)S(1)}, u32[]{:S(2)}, u32[]{:S(2)}) collective-permute-start(f32[2,512]{1,0:T(2,128)S(1)} %fusion.29), channel_id=1, source_target_pairs={{0,16},{1,17},{2,18},{3,19},{4,20},{5,21},{6,22},{7,23},{8,24},{9,... | collective-permute-start | bytes 12296 | tf_op jit(solution)/shard_map/ppermute | solution.py:27
  123.4 16.9 %collective-permute-start.24 = (f32[2,512]{1,0:T(2,128)S(1)}, f32[2,512]{1,0:T(2,128)S(1)}, u32[]{:S(2)}, u32[]{:S(2)}) collective-permute-start(f32[2,512]{1,0:T(2,128)S(1)} %fusion.30), channel_id=1, source_target_pairs={{0,128},{1,129},{2,130},{3,131},{4,132},{5,133},{6,134},{7,135},{8... | collective-permute-start | bytes 12296 | tf_op jit(solution)/shard_map/ppermute | solution.py:27
  130.9 9.4 %collective-permute-start.25 = (f32[2,384]{1,0:T(2,128)S(1)}, f32[2,384]{1,0:T(2,128)S(1)}, u32[]{:S(2)}, u32[]{:S(2)}) collective-permute-start(f32[2,384]{1,0:T(2,128)S(1)} %fusion.33), channel_id=1, source_target_pairs={{0,16},{1,17},{2,18},{3,19},{4,20},{5,21},{6,22},{7,23},{8,24},{9,... | collective-permute-start | bytes 9224 | tf_op jit(solution)/shard_map/ppermute | solution.py:27
  140.4 16.4 %collective-permute-start.26 = (f32[1,512]{1,0:T(1,128)S(1)}, f32[1,512]{1,0:T(1,128)S(1)}, u32[]{:S(2)}, u32[]{:S(2)}) collective-permute-start(f32[1,512]{1,0:T(1,128)S(1)} %constant_dynamic-slice_fusion.6), channel_id=1, source_target_pairs={{0,128},{1,129},{2,130},{3,131},{4,132},{5,133},{6,134},{7,135},{8... | collective-permute-start | bytes 6152 | tf_op jit(solution)/shard_map/ppermute | solution.py:27
  142.7 14.1 %collective-permute-start.27 = (f32[1,512]{1,0:T(1,128)S(1)}, f32[1,512]{1,0:T(1,128)S(1)}, u32[]{:S(2)}, u32[]{:S(2)}) collective-permute-start(f32[1,512]{1,0:T(1,128)S(1)} %constant_dynamic-slice_fusion.4), channel_id=1, source_target_pairs={{0,16},{1,17},{2,18},{3,19},{4,20},{5,21},{6,22},{7,23},{8,24},{9,... | collective-permute-start | bytes 6152 | tf_op jit(solution)/shard_map/ppermute | solution.py:27
  147.4 9.4 %collective-permute-start.28 = (f32[1,384]{1,0:T(1,128)S(1)}, f32[1,384]{1,0:T(1,128)S(1)}, u32[]{:S(2)}, u32[]{:S(2)}) collective-permute-start(f32[1,384]{1,0:T(1,128)S(1)} %constant_dynamic-slice_fusion.2), channel_id=1, source_target_pairs={{0,128},{1,129},{2,130},{3,131},{4,132},{5,133},{6,134},{7,135},{8... | collective-permute-start | bytes 4616 | tf_op jit(solution)/shard_map/ppermute | solution.py:27
  156.9 5.5 %collective-permute-start.29 = (f32[1,1408]{1,0:T(1,128)S(1)}, f32[1,1408]{1,0:T(1,128)S(1)}, u32[]{:S(2)}, u32[]{:S(2)}) collective-permute-start(f32[1,1408]{1,0:T(1,128)S(1)} %pad_maximum_fusion.2), channel_id=1, source_target_pairs={{0,32},{1,33},{2,34},{3,35},{4,36},{5,37},{6,38},{7,39},{8,40},{9,... | collective-permute-start | bytes 16904 | tf_op jit(solution)/shard_map/ppermute | solution.py:27
  162.4 9.2 %collective-permute-start.30 = (f32[2,1408]{1,0:T(2,128)S(1)}, f32[2,1408]{1,0:T(2,128)S(1)}, u32[]{:S(2)}, u32[]{:S(2)}) collective-permute-start(f32[2,1408]{1,0:T(2,128)S(1)} %maximum_select_fusion.3), channel_id=1, source_target_pairs={{0,64},{1,65},{2,66},{3,67},{4,68},{5,69},{6,70},{7,71},{8,72},{9,... | collective-permute-start | bytes 33800 | tf_op jit(solution)/shard_map/ppermute | solution.py:27
  166.9 22.1 %collective-permute-start.1 = (bf16[256,1024]{1,0:T(8,128)(2,1)S(1)}, bf16[256,1024]{1,0:T(8,128)(2,1)S(1)}, u32[]{:S(2)}, u32[]{:S(2)}) collective-permute-start(bf16[256,1024]{1,0:T(8,128)(2,1)S(1)} %pad_maximum_fusion.1), channel_id=1, source_target_pairs={{2,0},{3,1},{4,2},{5,3},{6,4},{7,5},{8,6},{9,7},{10,8},{11,9},{12,... | collective-permute-start | bytes 1572872 | tf_op jit(solution)/shard_map/ppermute | solution.py:10
  171.7 14.8 %collective-permute-start.31 = (f32[4,1408]{1,0:T(4,128)S(1)}, f32[4,1408]{1,0:T(4,128)S(1)}, u32[]{:S(2)}, u32[]{:S(2)}) collective-permute-start(f32[4,1408]{1,0:T(4,128)S(1)} %maximum_select_fusion.2), channel_id=1, source_target_pairs={{0,128},{1,129},{2,130},{3,131},{4,132},{5,133},{6,134},{7,135},{8... | collective-permute-start | bytes 67592 | tf_op jit(solution)/shard_map/ppermute | solution.py:27
  186.5 5.9 %collective-permute-start.32 = (f32[8,1408]{1,0:T(8,128)S(1)}, f32[8,1408]{1,0:T(8,128)S(1)}, u32[]{:S(2)}, u32[]{:S(2)}) collective-permute-start(f32[8,1408]{1,0:T(8,128)S(1)} %maximum_select_fusion.1), channel_id=1, source_target_pairs={{0,256},{1,257},{2,258},{3,259},{4,260},{5,261},{6,262},{7,263},{8... | collective-permute-start | bytes 135176 | tf_op jit(solution)/shard_map/ppermute | solution.py:27

commit v4 on v3

--- a/solution.py
+++ b/solution.py
@@ -32,30 +32,27 @@
     return [bits - 1 - home[b] for b in order]
 
 
-def halving_scatter(packed, axes, orders, widths, home):
+def halving_scatter(packed, axes, orders, home):
     bits = len(orders[0])
-    count = packed.shape[0]
+    count, width = packed.shape
+    lead = orders[0][0]
     where = lax.axis_index(axes)
-    bufs = []
-    col = 0
-    for order, width in zip(orders, widths):
-        part = packed[:, col : col + width].reshape((2,) * bits + (width,))
-        part = jnp.transpose(part, chain_layout(order, home) + [bits])
-        bufs.append(part.reshape(count, width))
-        col += width
+    natural = packed.reshape((2,) * bits + (width,))
+    halves = []
+    for k, order in enumerate(orders):
+        part = jnp.transpose(natural, chain_layout(order, home) + [bits])[k]
+        halves.append(part.reshape(count // 2, width))
+    buf = jnp.concatenate(halves)
+    first = (where >> lead) & 1
     for step in range(bits):
-        keeps, sends = [], []
-        for i, order in enumerate(orders):
-            bit = (where >> order[step]) & 1
-            buf = bufs[i]
-            halves = buf.reshape((2, buf.shape[0] // 2, buf.shape[1]))
-            keeps.append(lax.dynamic_index_in_dim(halves, bit, 0, keepdims=False))
-            sends.append(lax.dynamic_index_in_dim(halves, 1 - bit, 0, keepdims=False))
-        sends = lax.optimization_barrier(sends)
-        got = [exchange(send, axes, 1 << order[step]) for send, order in zip(sends, orders)]
-        got = lax.optimization_barrier(got)
-        bufs = [keep + recv for keep, recv in zip(keeps, got)]
-    return jnp.concatenate(bufs, axis=1)
+        shift = [order[step] for order in orders]
+        bit = jnp.where(first == 0, (where >> shift[0]) & 1, (where >> shift[1]) & 1)
+        pairs = [(i, i ^ (1 << shift[(i >> lead) & 1])) for i in range(count)]
+        split = buf.reshape((2, buf.shape[0] // 2, width))
+        keep = lax.dynamic_index_in_dim(split, bit, 0, keepdims=False)
+        send = lax.dynamic_index_in_dim(split, 1 - bit, 0, keepdims=False)
+        buf = keep + lax.ppermute(send, axes, pairs)
+    return buf
 
 
 def doubling_gather(piece, axes, bits):
@@ -126,13 +123,9 @@
     z1, z2, z4, x_lo = 5, 6, 7, 8
     orders = (
         [core, y1, z1, x_lo, y2, z2, x_hi, y4, z4],
-        [core, z1, x_lo, y1, z2, x_hi, y2, z4, y4],
-        [core, x_lo, y1, z1, x_hi, y2, z2, y4, z4],
+        [core, z1, x_lo, y1, z2, y2, x_hi, z4, y4],
     )
-    lanes_per = width // lanes
-    split = [lanes_per // 3 + (1 if i < lanes_per % 3 else 0) for i in range(3)]
-    widths = [n * lanes for n in split]
-    mine = halving_scatter(packed, ("grp", "seq"), orders, widths, home)
+    mine = halving_scatter(packed, ("grp", "seq"), orders, home)
     share = doubling_gather(mine, ("grp", "seq"), [z1, z2, z4, x_lo])
     taps_w = part_taps.shape[1]
     out_w = part_out.shape[1]

time: 195 us -> 163 us (0.84)
  starting transfers between devices: 125 us -> 68.3 us
  local copies, waits for them, and re-layouts: 12.7 us -> 30.8 us
  waiting for transfers between devices: 44.5 us -> 51.8 us
    ppermute x31 -> x4, starting transfers between devices: 115 us -> 17.8 us  [exchange(): return lax.ppermute(array, axes, [(i, i ^ mask) for i in range(count)])]
    ppermute x0 -> x9, starting transfers between devices: none -> 40.5 us  [halving_scatter(): buf = keep + lax.ppermute(send, axes, pairs)]
    ppermute x0 -> x9, waiting for transfers between devices: none -> 37.1 us  [halving_scatter(): buf = keep + lax.ppermute(send, axes, pairs)]
    ppermute x31 -> x4, waiting for transfers between devices: 41.2 us -> 11.3 us  [exchange(): return lax.ppermute(array, axes, [(i, i ^ mask) for i in range(count)])]
    concatenate x5 -> x7, local copies, waits for them, and re-layouts: 1.33 us -> 17.7 us  [per_device(): jnp.concatenate([part_taps.reshape(chunks, -1), part_out.reshape(chunks,...]
    another operation x0 -> x2, local copies, waits for them, and re-layouts: none -> 5.22 us  [halving_scatter(): halves.append(part.reshape(count // 2, width))]
    reshape x10 -> x2, local copies, waits for them, and re-layouts: 2.94 us -> 0.04 us  [halving_scatter(): split = buf.reshape((2, buf.shape[0] // 2, width))]
    dynamic_slice x2 -> x0, local copies, waits for them, and re-layouts: 2.49 us -> none  [halving_scatter(): keeps.append(lax.dynamic_index_in_dim(halves, bit, 0, keepdims=False))]
  transfers between devices with their start and end apart: 33 -> 15, of which waited for: 13 -> 13; matrix products, arithmetic and copies ran while one was open for 2% -> 2% of each run, Pallas kernels for 0% -> 0%
where the time goes in v4:
time: 163 us
  starting transfers between devices  68.3 us (42%)
  waiting for transfers between devices  51.8 us (32%)
  local copies, waits for them, and re-layouts  30.8 us (19%)
  matrix products  5.33 us (3%)
  other arithmetic  5.15 us (3%)
    ppermute x9, starting transfers between devices, halving_scatter(): buf = keep + lax.ppermute(send, axes, pairs)  40.5 us
    ppermute x9, waiting for transfers between devices, halving_scatter(): buf = keep + lax.ppermute(send, axes, pairs)  37.1 us
    ppermute x4, starting transfers between devices, exchange(): return lax.ppermute(array, axes, [(i, i ^ mask) for i in range(count)])  17.8 us
    concatenate x7, local copies, waits for them, and re-layouts, per_device(): jnp.concatenate([part_taps.reshape(chunks, -1), part_out.reshape(chunks,...  17.7 us
    ppermute x4, waiting for transfers between devices, exchange(): return lax.ppermute(array, axes, [(i, i ^ mask) for i in range(count)])  11.3 us
    ppermute x2, starting transfers between devices, from_behind(): return lax.ppermute(array, axis, pairs)  9.99 us
    another operation x2, local copies, waits for them, and re-layouts, halving_scatter(): halves.append(part.reshape(count // 2, width))  5.22 us
    ppermute x2, waiting for transfers between devices, from_behind(): return lax.ppermute(array, axis, pairs)  3.36 us
  transfers between devices with their start and end apart: 15, of which 13 were waited for; matrix products, arithmetic and copies ran while one was open for 2% of the time, Pallas kernels for 0%

profile of v4, /device:TPU:120, one launch (start us, length us, event | category | flops | bytes accessed | tf_op | source)
XLA Modules:
  0.0 162.5 jit_solution(17720223540502921530)
XLA Ops:
  0.6 0.0 copy-start
  0.7 5.1 %collective-permute-start = (bf16[256,256]{1,0:T(8,128)(2,1)}, bf16[256,256]{1,0:T(8,128)(2,1)S(1)}, u32[]{:S(2)}, u32[]{:S(2)}) collective-permute-start(bf16[256,256]{1,0:T(8,128)(2,1)} %param.5), channel_id=1, source_target_pairs={{0,2},{1,3},{2,4},{3,5},{4,6},{5,7},{6,8},{7,9},{8,10},{9,11},{10,... | collective-permute-start | bytes 393224 | tf_op jit(solution)/shard_map/ppermute | solution.py:10
  5.7 1.4 fusion.9
  7.2 0.0 copy-start.9
  7.2 3.4 %collective-permute-done = bf16[256,256]{1,0:T(8,128)(2,1)S(1)} collective-permute-done((bf16[256,256]{1,0:T(8,128)(2,1)}, bf16[256,256]{1,0:T(8,128)(2,1)S(1)}, u32[]{:S(2)}, u32[]{:S(2)}) %collective-permute-start) | collective-permute-done | bytes 131104 | tf_op jit(solution)/shard_map/ppermute | solution.py:10
  10.6 0.3 fusion
  10.9 0.5 multiply_convert_fusion.1
  11.4 0.4 copy-done.6
  11.8 0.3 convolution_bitcast_fusion
  12.1 0.1 convert_reduce_fusion
  12.2 0.3 convolution_bitcast_fusion.1
  12.6 0.1 pad_maximum_fusion.1
  12.7 2.2 %concatenate.46 = f32[2,2,2,2,2,2,2,2,2,1024]{9,8,7,6,5,4,3,2,1,0:T(2,128)} reshape(f32[512,1024]{1,0:T(8,128)S(1)} %pad_maximum_fusion.1) | data formatting | bytes 4194304 | tf_op jit(solution)/shard_map/concatenate | solution.py:108
  15.0 4.6 %copy.13 = f32[2,2,2,2,2,2,2,2,2,1024]{9,0,6,3,1,7,2,5,8,4:T(2,128)} copy(f32[2,2,2,2,2,2,2,2,2,1024]{9,8,7,6,5,4,3,2,1,0:T(2,128)} %concatenate.46) | data formatting | bytes 4194304 | tf_op jit(solution)/shard_map/concatenate | solution.py:108
  19.6 0.3 fusion.12
  19.8 0.3 concatenate.47
  20.1 1.2 copy.14
  21.3 0.4 concatenate.48
  21.8 0.9 copy.15
  22.7 0.8 broadcast_in_dim.4
  23.5 8.0 %concatenate.49 = f32[2,2,2,2,2,2,2,2,2,1408]{9,0,6,3,1,7,2,5,8,4:T(2,128)S(1)} concatenate(f32[2,2,2,2,2,2,2,2,2,1024]{9,0,6,3,1,7,2,5,8,4:T(2,128)} %copy.13, f32[2,2,2,2,2,2,2,2,2,256]{9,0,6,3,1,7,2,5,8,4:T(2,128)} %copy.14, f32[2,2,2,2,2,2,2,2,2,2]{9,0,6,3,1,7,2,5,8,4:T(2,128)} %copy.15, f32[2,2,2,2,2,2,2,2,2,126]{9,0,6,3,1,7,2,5,8,4:T(2,128)} %broadcast_in_dim.4), dimensions={9} | concatenate | bytes 5767168 | tf_op jit(solution)/shard_map/concatenate | solution.py:108
  31.5 1.3 slice.41
  32.8 3.1 %reshape_squeeze.7 = f32[256,1408]{1,0:T(8,128)} reshape(f32[1,2,2,2,2,2,2,2,2,1408]{9,8,7,6,5,4,3,2,1,0:T(2,128)} %slice.41) | data formatting | bytes 2883584 | tf_op jit(solution)/shard_map/reshape;squeeze | solution.py:44
  35.9 0.2 slice.40
  36.1 0.7 copy.16
  36.8 2.1 %reshape_squeeze.6 = f32[256,1408]{1,0:T(8,128)} reshape(f32[1,2,2,2,2,2,2,2,2,1408]{9,8,7,6,5,4,3,2,1,0:T(2,128)S(1)} %copy.16) | data formatting | bytes 2883584 | tf_op jit(solution)/shard_map/reshape;squeeze | solution.py:44
  38.9 2.0 %pad_maximum_fusion = f32[512,1408]{1,0:T(8,128)S(1)} fusion(f32[256,1408]{1,0:T(8,128)} %reshape_squeeze.7, f32[256,1408]{1,0:T(8,128)} %reshape_squeeze.6), kind=kLoop, calls=%fused_computation | loop fusion | flops 720896 | bytes 5767168 | tf_op jit(solution)/shard_map/concatenate | solution.py:45
  40.9 1.2 dynamic-slice_bitcast_fusion
  42.1 1.9 %collective-permute-start.2 = (f32[256,1408]{1,0:T(8,128)}, f32[256,1408]{1,0:T(8,128)}, u32[]{:S(2)}, u32[]{:S(2)}) collective-permute-start(f32[256,1408]{1,0:T(8,128)} %dynamic-slice_bitcast_fusion), channel_id=1, source_target_pairs={{0,1},{1,0},{2,3},{3,2},{4,5},{5,4},{6,7},{7,6},{8,9},{9,8},{10,11... | collective-permute-start | bytes 4325384 | tf_op jit(solution)/shard_map/ppermute | solution.py:54
  44.1 3.5 %collective-permute-done.2 = f32[256,1408]{1,0:T(8,128)} collective-permute-done((f32[256,1408]{1,0:T(8,128)}, f32[256,1408]{1,0:T(8,128)}, u32[]{:S(2)}, u32[]{:S(2)}) %collective-permute-start.2) | collective-permute-done | bytes 1441824 | tf_op jit(solution)/shard_map/ppermute | solution.py:54
  47.6 1.5 bitcast_add_fusion
  49.1 1.1 copy-done.1
  50.3 3.3 %collective-permute-start.3 = (f32[128,1408]{1,0:T(8,128)S(1)}, f32[128,1408]{1,0:T(8,128)S(1)}, u32[]{:S(2)}, u32[]{:S(2)}) collective-permute-start(f32[128,1408]{1,0:T(8,128)S(1)} %dynamic-slice_bitcast_fusion.1), channel_id=1, source_target_pairs={{0,4},{1,33},{2,6},{3,35},{4,0},{5,37},{6,2},{7,39},{8,12},{9,41},... | collective-permute-start | bytes 2162696 | tf_op jit(solution)/shard_map/ppermute | solution.py:54
  53.6 9.9 %collective-permute-done.3 = f32[128,1408]{1,0:T(8,128)S(1)} collective-permute-done((f32[128,1408]{1,0:T(8,128)S(1)}, f32[128,1408]{1,0:T(8,128)S(1)}, u32[]{:S(2)}, u32[]{:S(2)}) %collective-permute-start.3) | collective-permute-done | bytes 720928 | tf_op jit(solution)/shard_map/ppermute | solution.py:54
  63.5 1.2 bitcast_add_fusion.1
  64.7 1.9 %collective-permute-start.4 = (f32[64,1408]{1,0:T(8,128)S(1)}, f32[64,1408]{1,0:T(8,128)S(1)}, u32[]{:S(2)}, u32[]{:S(2)}) collective-permute-start(f32[64,1408]{1,0:T(8,128)S(1)} %dynamic-slice_bitcast_fusion.2), channel_id=1, source_target_pairs={{0,32},{1,257},{2,34},{3,259},{4,36},{5,261},{6,38},{7,263},{8,40}... | collective-permute-start | bytes 1081352 | tf_op jit(solution)/shard_map/ppermute | solution.py:54
  66.7 7.4 %collective-permute-done.4 = f32[64,1408]{1,0:T(8,128)S(1)} collective-permute-done((f32[64,1408]{1,0:T(8,128)S(1)}, f32[64,1408]{1,0:T(8,128)S(1)}, u32[]{:S(2)}, u32[]{:S(2)}) %collective-permute-start.4) | collective-permute-done | bytes 360480 | tf_op jit(solution)/shard_map/ppermute | solution.py:54
  74.1 3.4 %collective-permute-start.5 = (f32[32,1408]{1,0:T(8,128)S(1)}, f32[32,1408]{1,0:T(8,128)S(1)}, u32[]{:S(2)}, u32[]{:S(2)}) collective-permute-start(f32[32,1408]{1,0:T(8,128)S(1)} %dynamic-slice_bitcast_fusion.3), channel_id=1, source_target_pairs={{0,256},{1,5},{2,258},{3,7},{4,260},{5,1},{6,262},{7,3},{8,264},{9... | collective-permute-start | bytes 540680 | tf_op jit(solution)/shard_map/ppermute | solution.py:54
  77.5 4.0 %collective-permute-done.5 = f32[32,1408]{1,0:T(8,128)S(1)} collective-permute-done((f32[32,1408]{1,0:T(8,128)S(1)}, f32[32,1408]{1,0:T(8,128)S(1)}, u32[]{:S(2)}, u32[]{:S(2)}) %collective-permute-start.5) | collective-permute-done | bytes 180256 | tf_op jit(solution)/shard_map/ppermute | solution.py:54
  81.5 4.6 %collective-permute-start.6 = (f32[16,1408]{1,0:T(8,128)S(1)}, f32[16,1408]{1,0:T(8,128)S(1)}, u32[]{:S(2)}, u32[]{:S(2)}) collective-permute-start(f32[16,1408]{1,0:T(8,128)S(1)} %dynamic-slice_bitcast_fusion.4), channel_id=1, source_target_pairs={{0,8},{1,65},{2,10},{3,67},{4,12},{5,69},{6,14},{7,71},{8,0},{9,73... | collective-permute-start | bytes 270344 | tf_op jit(solution)/shard_map/ppermute | solution.py:54
  86.1 2.7 %collective-permute-done.6 = f32[16,1408]{1,0:T(8,128)S(1)} collective-permute-done((f32[16,1408]{1,0:T(8,128)S(1)}, f32[16,1408]{1,0:T(8,128)S(1)}, u32[]{:S(2)}, u32[]{:S(2)}) %collective-permute-start.6) | collective-permute-done | bytes 90144 | tf_op jit(solution)/shard_map/ppermute | solution.py:54
  88.9 6.1 %collective-permute-start.7 = (f32[8,1408]{1,0:T(8,128)S(1)}, f32[8,1408]{1,0:T(8,128)S(1)}, u32[]{:S(2)}, u32[]{:S(2)}) collective-permute-start(f32[8,1408]{1,0:T(8,128)S(1)} %dynamic-slice_bitcast_fusion.5), channel_id=1, source_target_pairs={{0,64},{1,9},{2,66},{3,11},{4,68},{5,13},{6,70},{7,15},{8,72},{9,1... | collective-permute-start | bytes 135176 | tf_op jit(solution)/shard_map/ppermute | solution.py:54
  95.0 2.0 %collective-permute-done.7 = f32[8,1408]{1,0:T(8,128)S(1)} collective-permute-done((f32[8,1408]{1,0:T(8,128)S(1)}, f32[8,1408]{1,0:T(8,128)S(1)}, u32[]{:S(2)}, u32[]{:S(2)}) %collective-permute-start.7) | collective-permute-done | bytes 45088 | tf_op jit(solution)/shard_map/ppermute | solution.py:54
  97.1 5.0 %collective-permute-start.8 = (f32[4,1408]{1,0:T(4,128)S(1)}, f32[4,1408]{1,0:T(4,128)S(1)}, u32[]{:S(2)}, u32[]{:S(2)}) collective-permute-start(f32[4,1408]{1,0:T(4,128)S(1)} %dynamic-slice_bitcast_fusion.6), channel_id=1, source_target_pairs={{0,2},{1,3},{2,0},{3,1},{4,6},{5,7},{6,4},{7,5},{8,10},{9,11},{10,... | collective-permute-start | bytes 67592 | tf_op jit(solution)/shard_map/ppermute | solution.py:54
  102.1 2.2 %collective-permute-done.8 = f32[4,1408]{1,0:T(4,128)S(1)} collective-permute-done((f32[4,1408]{1,0:T(4,128)S(1)}, f32[4,1408]{1,0:T(4,128)S(1)}, u32[]{:S(2)}, u32[]{:S(2)}) %collective-permute-start.8) | collective-permute-done | bytes 22560 | tf_op jit(solution)/shard_map/ppermute | solution.py:54
  104.3 5.6 %collective-permute-start.9 = (f32[2,1408]{1,0:T(2,128)S(1)}, f32[2,1408]{1,0:T(2,128)S(1)}, u32[]{:S(2)}, u32[]{:S(2)}) collective-permute-start(f32[2,1408]{1,0:T(2,128)S(1)} %dynamic-slice_bitcast_fusion.7), channel_id=1, source_target_pairs={{0,16},{1,129},{2,18},{3,131},{4,20},{5,133},{6,22},{7,135},{8,24}... | collective-permute-start | bytes 33800 | tf_op jit(solution)/shard_map/ppermute | solution.py:54
  109.9 3.9 %collective-permute-done.9 = f32[2,1408]{1,0:T(2,128)S(1)} collective-permute-done((f32[2,1408]{1,0:T(2,128)S(1)}, f32[2,1408]{1,0:T(2,128)S(1)}, u32[]{:S(2)}, u32[]{:S(2)}) %collective-permute-start.9) | collective-permute-done | bytes 11296 | tf_op jit(solution)/shard_map/ppermute | solution.py:54
  113.8 8.7 %collective-permute-start.10 = (f32[1,1408]{1,0:T(1,128)S(1)}, f32[1,1408]{1,0:T(1,128)S(1)}, u32[]{:S(2)}, u32[]{:S(2)}) collective-permute-start(f32[1,1408]{1,0:T(1,128)S(1)} %constant_dynamic-slice_fusion), channel_id=1, source_target_pairs={{0,128},{1,17},{2,130},{3,19},{4,132},{5,21},{6,134},{7,23},{8,136... | collective-permute-start | bytes 16904 | tf_op jit(solution)/shard_map/ppermute | solution.py:54
  122.6 1.6 collective-permute-done.10
  124.2 2.6 %collective-permute-start.11 = (f32[1,1408]{1,0:T(1,128)S(1)}, f32[1,1408]{1,0:T(1,128)S(1)}, u32[]{:S(2)}, u32[]{:S(2)}) collective-permute-start(f32[1,1408]{1,0:T(1,128)S(1)} %dynamic-slice_add_fusion), channel_id=1, source_target_pairs={{0,32},{1,33},{2,34},{3,35},{4,36},{5,37},{6,38},{7,39},{8,40},{9,... | collective-permute-start | bytes 16904 | tf_op jit(solution)/shard_map/ppermute | solution.py:27
  126.8 0.3 convolution_add_fusion.3
  127.2 2.7 %collective-permute-done.11 = f32[1,1408]{1,0:T(1,128)S(1)} collective-permute-done((f32[1,1408]{1,0:T(1,128)S(1)}, f32[1,1408]{1,0:T(1,128)S(1)}, u32[]{:S(2)}, u32[]{:S(2)}) %collective-permute-start.11) | collective-permute-done | bytes 5664 | tf_op jit(solution)/shard_map/ppermute | solution.py:27
  129.9 4.8 %collective-permute-start.12 = (f32[2,1408]{1,0:T(2,128)S(1)}, f32[2,1408]{1,0:T(2,128)S(1)}, u32[]{:S(2)}, u32[]{:S(2)}) collective-permute-start(f32[2,1408]{1,0:T(2,128)S(1)} %maximum_select_fusion.3), channel_id=1, source_target_pairs={{0,64},{1,65},{2,66},{3,67},{4,68},{5,69},{6,70},{7,71},{8,72},{9,... | collective-permute-start | bytes 33800 | tf_op jit(solution)/shard_map/ppermute | solution.py:27
  134.6 0.1 pad_maximum_fusion.2
  134.7 4.9 %collective-permute-start.1 = (bf16[256,1024]{1,0:T(8,128)(2,1)S(1)}, bf16[256,1024]{1,0:T(8,128)(2,1)S(1)}, u32[]{:S(2)}, u32[]{:S(2)}) collective-permute-start(bf16[256,1024]{1,0:T(8,128)(2,1)S(1)} %pad_maximum_fusion.2), channel_id=1, source_target_pairs={{2,0},{3,1},{4,2},{5,3},{6,4},{7,5},{8,6},{9,7},{10,8},{11,9},{12,... | collective-permute-start | bytes 1572872 | tf_op jit(solution)/shard_map/ppermute | solution.py:10
  139.7 7.8 %collective-permute-start.13 = (f32[4,1408]{1,0:T(4,128)S(1)}, f32[4,1408]{1,0:T(4,128)S(1)}, u32[]{:S(2)}, u32[]{:S(2)}) collective-permute-start(f32[4,1408]{1,0:T(4,128)S(1)} %maximum_select_fusion.2), channel_id=1, source_target_pairs={{0,128},{1,129},{2,130},{3,131},{4,132},{5,133},{6,134},{7,135},{8... | collective-permute-start | bytes 67592 | tf_op jit(solution)/shard_map/ppermute | solution.py:27
  147.5 0.9 fusion.1
  148.4 6.3 %collective-permute-done.13 = f32[4,1408]{1,0:T(4,128)S(1)} collective-permute-done((f32[4,1408]{1,0:T(4,128)S(1)}, f32[4,1408]{1,0:T(4,128)S(1)}, u32[]{:S(2)}, u32[]{:S(2)}) %collective-permute-start.13) | collective-permute-done | bytes 22560 | tf_op jit(solution)/shard_map/ppermute | solution.py:27
  154.7 2.6 %collective-permute-start.14 = (f32[8,1408]{1,0:T(8,128)S(1)}, f32[8,1408]{1,0:T(8,128)S(1)}, u32[]{:S(2)}, u32[]{:S(2)}) collective-permute-start(f32[8,1408]{1,0:T(8,128)S(1)} %maximum_select_fusion.1), channel_id=1, source_target_pairs={{0,256},{1,257},{2,258},{3,259},{4,260},{5,261},{6,262},{7,263},{8... | collective-permute-start | bytes 135176 | tf_op jit(solution)/shard_map/ppermute | solution.py:27
  157.4 1.0 fusion.2
  158.4 2.3 %collective-permute-done.14 = f32[8,1408]{1,0:T(8,128)S(1)} collective-permute-done((f32[8,1408]{1,0:T(8,128)S(1)}, f32[8,1408]{1,0:T(8,128)S(1)}, u32[]{:S(2)}, u32[]{:S(2)}) %collective-permute-start.14) | collective-permute-done | bytes 45088 | tf_op jit(solution)/shard_map/ppermute | solution.py:27
  160.7 0.6 slice.42
  161.3 0.6 slice.44
  161.9 0.6 reshape.58
  (44 shorter events, 0.5 us)
Async XLA Ops:
  0.6 10.2 %copy-start = (bf16[512,256]{1,0:T(8,128)(2,1)S(1)}, bf16[512,256]{1,0:T(8,128)(2,1)}, u32[]{:S(2)}) copy-start(bf16[512,256]{1,0:T(8,128)(2,1)} %param.9) | copy-start | bytes 786436
  0.6 9.9 %copy-start.4 = (bf16[512,1024]{1,0:T(8,128)(2,1)S(1)}, bf16[512,1024]{1,0:T(8,128)(2,1)}, u32[]{:S(2)}) copy-start(bf16[512,1024]{1,0:T(8,128)(2,1)} %param.7) | copy-start | bytes 3145732
  0.7 9.9 %copy-start.11 = (f32[1024]{0:T(1024)S(1)}, f32[1024]{0:T(1024)}, u32[]{:S(2)}) copy-start(f32[1024]{0:T(1024)} %param.8) | copy-start | bytes 12292
  0.7 9.9 %collective-permute-start = (bf16[256,256]{1,0:T(8,128)(2,1)}, bf16[256,256]{1,0:T(8,128)(2,1)S(1)}, u32[]{:S(2)}, u32[]{:S(2)}) collective-permute-start(bf16[256,256]{1,0:T(8,128)(2,1)} %param.5), channel_id=1, source_target_pairs={{0,2},{1,3},{2,4},{3,5},{4,6},{5,7},{6,8},{7,9},{8,10},{9,11},{10,... | collective-permute-start | bytes 393224 | tf_op jit(solution)/shard_map/ppermute | solution.py:10
  7.2 3.7 %copy-start.9 = (bf16[256,256]{1,0:T(8,128)(2,1)S(1)}, bf16[256,256]{1,0:T(8,128)(2,1)}, u32[]{:S(2)}) copy-start(bf16[256,256]{1,0:T(8,128)(2,1)} %param.6) | copy-start | bytes 393220
  10.9 0.9 copy-start.6
  11.4 0.9 copy-start.2
  11.4 8.2 %copy-start.7 = (bf16[256,512]{1,0:T(8,128)(2,1)}, bf16[256,512]{1,0:T(8,128)(2,1)S(1)}, u32[]{:S(2)}) copy-start(bf16[256,512]{1,0:T(8,128)(2,1)S(1)} %get-tuple-element.7) | copy-start | bytes 786436
  42.1 5.4 %collective-permute-start.2 = (f32[256,1408]{1,0:T(8,128)}, f32[256,1408]{1,0:T(8,128)}, u32[]{:S(2)}, u32[]{:S(2)}) collective-permute-start(f32[256,1408]{1,0:T(8,128)} %dynamic-slice_bitcast_fusion), channel_id=1, source_target_pairs={{0,1},{1,0},{2,3},{3,2},{4,5},{5,4},{6,7},{7,6},{8,9},{9,8},{10,11... | collective-permute-start | bytes 4325384 | tf_op jit(solution)/shard_map/ppermute | solution.py:54
  49.1 1.1 copy-start.1
  50.3 13.2 %collective-permute-start.3 = (f32[128,1408]{1,0:T(8,128)S(1)}, f32[128,1408]{1,0:T(8,128)S(1)}, u32[]{:S(2)}, u32[]{:S(2)}) collective-permute-start(f32[128,1408]{1,0:T(8,128)S(1)} %dynamic-slice_bitcast_fusion.1), channel_id=1, source_target_pairs={{0,4},{1,33},{2,6},{3,35},{4,0},{5,37},{6,2},{7,39},{8,12},{9,41},... | collective-permute-start | bytes 2162696 | tf_op jit(solution)/shard_map/ppermute | solution.py:54
  64.7 9.3 %collective-permute-start.4 = (f32[64,1408]{1,0:T(8,128)S(1)}, f32[64,1408]{1,0:T(8,128)S(1)}, u32[]{:S(2)}, u32[]{:S(2)}) collective-permute-start(f32[64,1408]{1,0:T(8,128)S(1)} %dynamic-slice_bitcast_fusion.2), channel_id=1, source_target_pairs={{0,32},{1,257},{2,34},{3,259},{4,36},{5,261},{6,38},{7,263},{8,40}... | collective-permute-start | bytes 1081352 | tf_op jit(solution)/shard_map/ppermute | solution.py:54
  66.6 60.2 %copy-start.3 = (bf16[256,512]{1,0:T(8,128)(2,1)S(1)}, bf16[256,512]{1,0:T(8,128)(2,1)}, u32[]{:S(2)}) copy-start(bf16[256,512]{1,0:T(8,128)(2,1)} %copy-done.2) | copy-start | bytes 786436
  66.6 60.2 %copy-start.5 = (bf16[512,1024]{1,0:T(8,128)(2,1)S(1)}, bf16[512,1024]{1,0:T(8,128)(2,1)}, u32[]{:S(2)}) copy-start(bf16[512,1024]{1,0:T(8,128)(2,1)} %param.7) | copy-start | bytes 3145732
  66.7 60.2 %copy-start.10 = (bf16[256,256]{1,0:T(8,128)(2,1)S(1)}, bf16[256,256]{1,0:T(8,128)(2,1)}, u32[]{:S(2)}) copy-start(bf16[256,256]{1,0:T(8,128)(2,1)} %param.6) | copy-start | bytes 393220
  74.1 7.4 %collective-permute-start.5 = (f32[32,1408]{1,0:T(8,128)S(1)}, f32[32,1408]{1,0:T(8,128)S(1)}, u32[]{:S(2)}, u32[]{:S(2)}) collective-permute-start(f32[32,1408]{1,0:T(8,128)S(1)} %dynamic-slice_bitcast_fusion.3), channel_id=1, source_target_pairs={{0,256},{1,5},{2,258},{3,7},{4,260},{5,1},{6,262},{7,3},{8,264},{9... | collective-permute-start | bytes 540680 | tf_op jit(solution)/shard_map/ppermute | solution.py:54
  81.5 7.3 %collective-permute-start.6 = (f32[16,1408]{1,0:T(8,128)S(1)}, f32[16,1408]{1,0:T(8,128)S(1)}, u32[]{:S(2)}, u32[]{:S(2)}) collective-permute-start(f32[16,1408]{1,0:T(8,128)S(1)} %dynamic-slice_bitcast_fusion.4), channel_id=1, source_target_pairs={{0,8},{1,65},{2,10},{3,67},{4,12},{5,69},{6,14},{7,71},{8,0},{9,73... | collective-permute-start | bytes 270344 | tf_op jit(solution)/shard_map/ppermute | solution.py:54
  88.9 8.1 %collective-permute-start.7 = (f32[8,1408]{1,0:T(8,128)S(1)}, f32[8,1408]{1,0:T(8,128)S(1)}, u32[]{:S(2)}, u32[]{:S(2)}) collective-permute-start(f32[8,1408]{1,0:T(8,128)S(1)} %dynamic-slice_bitcast_fusion.5), channel_id=1, source_target_pairs={{0,64},{1,9},{2,66},{3,11},{4,68},{5,13},{6,70},{7,15},{8,72},{9,1... | collective-permute-start | bytes 135176 | tf_op jit(solution)/shard_map/ppermute | solution.py:54
  97.1 7.2 %collective-permute-start.8 = (f32[4,1408]{1,0:T(4,128)S(1)}, f32[4,1408]{1,0:T(4,128)S(1)}, u32[]{:S(2)}, u32[]{:S(2)}) collective-permute-start(f32[4,1408]{1,0:T(4,128)S(1)} %dynamic-slice_bitcast_fusion.6), channel_id=1, source_target_pairs={{0,2},{1,3},{2,0},{3,1},{4,6},{5,7},{6,4},{7,5},{8,10},{9,11},{10,... | collective-permute-start | bytes 67592 | tf_op jit(solution)/shard_map/ppermute | solution.py:54
  104.3 9.5 %collective-permute-start.9 = (f32[2,1408]{1,0:T(2,128)S(1)}, f32[2,1408]{1,0:T(2,128)S(1)}, u32[]{:S(2)}, u32[]{:S(2)}) collective-permute-start(f32[2,1408]{1,0:T(2,128)S(1)} %dynamic-slice_bitcast_fusion.7), channel_id=1, source_target_pairs={{0,16},{1,129},{2,18},{3,131},{4,20},{5,133},{6,22},{7,135},{8,24}... | collective-permute-start | bytes 33800 | tf_op jit(solution)/shard_map/ppermute | solution.py:54
  113.8 10.3 %collective-permute-start.10 = (f32[1,1408]{1,0:T(1,128)S(1)}, f32[1,1408]{1,0:T(1,128)S(1)}, u32[]{:S(2)}, u32[]{:S(2)}) collective-permute-start(f32[1,1408]{1,0:T(1,128)S(1)} %constant_dynamic-slice_fusion), channel_id=1, source_target_pairs={{0,128},{1,17},{2,130},{3,19},{4,132},{5,21},{6,134},{7,23},{8,136... | collective-permute-start | bytes 16904 | tf_op jit(solution)/shard_map/ppermute | solution.py:54
  124.2 23.3 %copy-start.8 = (bf16[256,512]{1,0:T(8,128)(2,1)S(1)}, bf16[256,512]{1,0:T(8,128)(2,1)}, u32[]{:S(2)}) copy-start(bf16[256,512]{1,0:T(8,128)(2,1)} %copy-done.7) | copy-start | bytes 786436
  124.2 5.6 %collective-permute-start.11 = (f32[1,1408]{1,0:T(1,128)S(1)}, f32[1,1408]{1,0:T(1,128)S(1)}, u32[]{:S(2)}, u32[]{:S(2)}) collective-permute-start(f32[1,1408]{1,0:T(1,128)S(1)} %dynamic-slice_add_fusion), channel_id=1, source_target_pairs={{0,32},{1,33},{2,34},{3,35},{4,36},{5,37},{6,38},{7,39},{8,40},{9,... | collective-permute-start | bytes 16904 | tf_op jit(solution)/shard_map/ppermute | solution.py:27
  129.9 9.8 %collective-permute-start.12 = (f32[2,1408]{1,0:T(2,128)S(1)}, f32[2,1408]{1,0:T(2,128)S(1)}, u32[]{:S(2)}, u32[]{:S(2)}) collective-permute-start(f32[2,1408]{1,0:T(2,128)S(1)} %maximum_select_fusion.3), channel_id=1, source_target_pairs={{0,64},{1,65},{2,66},{3,67},{4,68},{5,69},{6,70},{7,71},{8,72},{9,... | collective-permute-start | bytes 33800 | tf_op jit(solution)/shard_map/ppermute | solution.py:27
  134.7 22.7 %collective-permute-start.1 = (bf16[256,1024]{1,0:T(8,128)(2,1)S(1)}, bf16[256,1024]{1,0:T(8,128)(2,1)S(1)}, u32[]{:S(2)}, u32[]{:S(2)}) collective-permute-start(bf16[256,1024]{1,0:T(8,128)(2,1)S(1)} %pad_maximum_fusion.2), channel_id=1, source_target_pairs={{2,0},{3,1},{4,2},{5,3},{6,4},{7,5},{8,6},{9,7},{10,8},{11,9},{12,... | collective-permute-start | bytes 1572872 | tf_op jit(solution)/shard_map/ppermute | solution.py:10
  139.7 15.0 %collective-permute-start.13 = (f32[4,1408]{1,0:T(4,128)S(1)}, f32[4,1408]{1,0:T(4,128)S(1)}, u32[]{:S(2)}, u32[]{:S(2)}) collective-permute-start(f32[4,1408]{1,0:T(4,128)S(1)} %maximum_select_fusion.2), channel_id=1, source_target_pairs={{0,128},{1,129},{2,130},{3,131},{4,132},{5,133},{6,134},{7,135},{8... | collective-permute-start | bytes 67592 | tf_op jit(solution)/shard_map/ppermute | solution.py:27
  154.7 5.9 %collective-permute-start.14 = (f32[8,1408]{1,0:T(8,128)S(1)}, f32[8,1408]{1,0:T(8,128)S(1)}, u32[]{:S(2)}, u32[]{:S(2)}) collective-permute-start(f32[8,1408]{1,0:T(8,128)S(1)} %maximum_select_fusion.1), channel_id=1, source_target_pairs={{0,256},{1,257},{2,258},{3,259},{4,260},{5,261},{6,262},{7,263},{8... | collective-permute-start | bytes 135176 | tf_op jit(solution)/shard_map/ppermute | solution.py:27

commit v5 on v1

--- a/solution.py
+++ b/solution.py
@@ -21,6 +21,61 @@
         left, right, (((1,), (1,)), ((), ())), preferred_element_type=jnp.float32
     )
 
+
+def relabel(index, rotate, size, by=1):
+    ring = (index // rotate) % size
+    return index + (((ring + by) % size) - ring) * rotate
+
+
+def unlabel(index, rotate, size):
+    return relabel(index, rotate, size, -1)
+
+
+def halving_scatter(shares, axis, orders, ring):
+    count = shares.shape[0]
+    bits = count.bit_length() - 1
+    rest = shares.shape[1:]
+    rotate, size = ring
+    where = lax.axis_index(axis)
+    rows = []
+    for c, order in enumerate(orders):
+        for p in range(count // 2):
+            v = c
+            for t, b in enumerate(order[1:]):
+                v |= ((p >> (bits - 2 - t)) & 1) << b
+            rows.append(unlabel(v, rotate, size) if c else v)
+    buf = jnp.concatenate([shares[s : s + 1] for s in rows])
+    core = where & 1
+    mine = jnp.where(core == 1, relabel(where, rotate, size), where)
+    for step in range(bits):
+        shift = [order[step] for order in orders]
+        bit = jnp.where(core == 1, (mine >> shift[1]) & 1, (mine >> shift[0]) & 1)
+        pairs = []
+        for s in range(count):
+            c = s & 1
+            v = relabel(s, rotate, size) if c else s
+            v ^= 1 << shift[c]
+            pairs.append((s, unlabel(v, rotate, size) if c else v))
+        split = buf.reshape((2, buf.shape[0] // 2) + rest)
+        keep = lax.dynamic_index_in_dim(split, bit, 0, keepdims=False)
+        send = lax.dynamic_index_in_dim(split, 1 - bit, 0, keepdims=False)
+        buf = keep + lax.ppermute(send, axis, pairs)
+    return buf[0]
+
+
+def butterfly_sum(array, axes, orders, ring, inner):
+    count = lax.axis_size(axes)
+    rotate, size = ring
+    for step in range(len(orders[0])):
+        pairs = []
+        for i in range(count):
+            g, s = divmod(i, inner)
+            c = s & 1
+            v = relabel(g, rotate, size) if c else g
+            v ^= 1 << orders[c][step]
+            pairs.append((i, (unlabel(v, rotate, size) if c else v) * inner + s))
+        array = array + lax.ppermute(array, axes, pairs)
+    return array
 
 def per_device(signal, cotangent, w_taps, gate_bias, w_out):
     width = signal.shape[1]
@@ -72,9 +127,9 @@
             bias_rows,
         ],
         axis=1,
-    ).reshape(groups * (taps_r + out_r + bias_r), lanes)
-    mine = lax.psum_scatter(packed, "seq", scatter_dimension=0, tiled=True)
-    mine = lax.psum(mine, "grp")
+    )
+    mine = halving_scatter(packed, "seq", ([0, 2, 3, 1, 4], [0, 2, 1, 3, 4]), (4, 8))
+    mine = butterfly_sum(mine, ("grp", "seq"), ([0, 3, 1, 2], [3, 0, 2, 1]), (1, 8), groups)
     grad_taps = mine[:taps_r].reshape(rows_taps, part_taps.shape[1])
     grad_out = mine[taps_r : taps_r + out_r].reshape(rows_out, part_out.shape[1])
     grad_bias = mine[taps_r + out_r, :share_bias]

time: 308 us -> 118 us (0.38)
  waiting for transfers between devices: 265 us -> 55.5 us
  starting transfers between devices: 10.1 us -> 43.9 us
  between operations: 14.2 us -> 1.34 us
    psum x1 -> x0, waiting for transfers between devices: 138 us -> none  [per_device(): mine = lax.psum(mine, 'grp')]
    unnamed x3 -> x0, waiting for transfers between devices: 123 us -> none
    ppermute x0 -> x9, waiting for transfers between devices: none -> 52.2 us  [the longest x5 32.2 us: halving_scatter(): buf = keep + lax.ppermute(send, axis, pairs)]
    ppermute x0 -> x9, starting transfers between devices: none -> 35.2 us  [the longest x5 18.5 us: halving_scatter(): buf = keep + lax.ppermute(send, axis, pairs)]
  transfers between devices with their start and end apart: 4 -> 11, of which waited for: 3 -> 9; matrix products, arithmetic and copies ran while one was open for 1% -> 4% of each run, Pallas kernels for 0% -> 0%
where the time goes in v5:
time: 118 us
  waiting for transfers between devices  55.5 us (47%)
  starting transfers between devices  43.9 us (37%)
  matrix products  7.45 us (6%)
  local copies, waits for them, and re-layouts  6.02 us (5%)
  other arithmetic  3.5 us (3%)
  between operations  1.34 us (1%)
    ppermute x5, waiting for transfers between devices, halving_scatter(): buf = keep + lax.ppermute(send, axis, pairs)  32.2 us
    ppermute x4, waiting for transfers between devices, butterfly_sum(): array = array + lax.ppermute(array, axes, pairs)  20 us
    ppermute x5, starting transfers between devices, halving_scatter(): buf = keep + lax.ppermute(send, axis, pairs)  18.5 us
    ppermute x4, starting transfers between devices, butterfly_sum(): array = array + lax.ppermute(array, axes, pairs)  16.7 us
    ppermute x2, starting transfers between devices, from_behind(): return lax.ppermute(array, axis, pairs)  8.63 us
    ppermute x2, waiting for transfers between devices, from_behind(): return lax.ppermute(array, axis, pairs)  3.33 us
    dot_general x3, matrix products, contract_cols(): lax.dot_general(left, right, (((1,), (1,)), ((), ())), preferred_element_...  2.86 us
  transfers between devices with their start and end apart: 11, of which 9 were waited for; matrix products, arithmetic and copies ran while one was open for 4% of the time, Pallas kernels for 0%

profile of v5, /device:TPU:56, one launch (start us, length us, event | category | flops | bytes accessed | tf_op | source)
XLA Modules:
  0.0 117.6 jit_solution(14040708668625170748)
XLA Ops:
  0.6 0.0 copy-start
  0.6 0.0 copy-start.7
  0.7 5.1 %collective-permute-start = (bf16[256,256]{1,0:T(8,128)(2,1)}, bf16[256,256]{1,0:T(8,128)(2,1)S(1)}, u32[]{:S(2)}, u32[]{:S(2)}) collective-permute-start(bf16[256,256]{1,0:T(8,128)(2,1)} %param.5), channel_id=1, source_target_pairs={{0,2},{1,3},{2,4},{3,5},{4,6},{5,7},{6,8},{7,9},{8,10},{9,11},{10,... | collective-permute-start | bytes 393224 | tf_op jit(solution)/shard_map/ppermute | solution.py:10
  5.7 1.4 %fusion.9 = f32[256,1024]{1,0:T(8,128)S(1)} fusion(bf16[256,256]{1,0:T(8,128)(2,1)} %param.5, bf16[512,1024]{1,0:T(8,128)(2,1)} %param.7), kind=kOutput, calls=%fused_computation.28 | convolution fusion | flops 134217728 | bytes 1703936 | tf_op jit(solution)/shard_map/dot_general | solution.py:84
  7.2 3.3 %collective-permute-done = bf16[256,256]{1,0:T(8,128)(2,1)S(1)} collective-permute-done((bf16[256,256]{1,0:T(8,128)(2,1)}, bf16[256,256]{1,0:T(8,128)(2,1)S(1)}, u32[]{:S(2)}, u32[]{:S(2)}) %collective-permute-start) | collective-permute-done | bytes 131104 | tf_op jit(solution)/shard_map/ppermute | solution.py:10
  10.5 1.3 %fusion = f32[256,1024]{1,0:T(8,128)S(1)} fusion(f32[256,1024]{1,0:T(8,128)S(1)} %fusion.9, bf16[256,256]{1,0:T(8,128)(2,1)S(1)} %collective-permute-done, f32[1024]{0:T(1024)} %param.8, bf16[512,1024]{1,0:T(8,128)(2,1)} %param.7), kind=kOutput, calls=%fused_computation.7 | convolution fusion | flops 134742016 | bytes 2756608 | tf_op jit(solution)/shard_map/dot_general | solution.py:87
  11.9 0.0 copy-done
  11.9 0.0 copy-done.7
  11.9 0.0 copy-start.3
  11.9 0.5 multiply_convert_fusion.1
  12.4 0.0 copy-start.5
  12.4 0.1 convert_reduce_fusion
  12.5 0.3 copy-done.3
  12.8 0.3 convolution_bitcast_fusion
  13.2 0.1 reshape.45
  13.3 0.3 fusion.11
  13.6 0.3 convolution_bitcast_fusion.1
  13.9 0.0 copy-done.5
  13.9 1.5 %pad_maximum_fusion.1 = f32[512,1024]{1,0:T(8,128)} fusion(f32[256,1024]{1,0:T(8,128)S(1)} %convolution_bitcast_fusion, f32[256,1024]{1,0:T(8,128)S(1)} %convolution_bitcast_fusion.1), kind=kLoop, calls=%fused_computation.1 | loop fusion | flops 524288 | bytes 4194304 | tf_op jit(solution)/shard_map/concatenate | solution.py:106
  15.4 1.7 %reshape.43 = f32[32,128,128]{2,1,0:T(8,128)S(1)} reshape(f32[512,1024]{1,0:T(8,128)} %pad_maximum_fusion.1) | data formatting | bytes 4194304 | tf_op jit(solution)/shard_map/reshape | solution.py:125
  17.1 0.2 pad_maximum_fusion
  17.9 0.0 copy-start.1
  17.9 1.5 %copy-done.1 = f32[32,168,128]{2,1,0:T(8,128)} copy-done((f32[32,168,128]{2,1,0:T(8,128)}, f32[32,168,128]{2,1,0:T(8,128)S(1)}, u32[]{:S(2)}) %copy-start.1) | copy-done | bytes 2752536
  19.4 0.1 dynamic-slice_bitcast_fusion
  19.5 1.9 %collective-permute-start.2 = (f32[16,168,128]{2,1,0:T(8,128)S(1)}, f32[16,168,128]{2,1,0:T(8,128)S(1)}, u32[]{:S(2)}, u32[]{:S(2)}) collective-permute-start(f32[16,168,128]{2,1,0:T(8,128)S(1)} %dynamic-slice_bitcast_fusion), channel_id=1, source_target_pairs={{0,1},{1,0},{2,3},{3,2},{4,5},{5,4},{6,7},{7,6},{8,9},{9,8},{10,11... | collective-permute-start | bytes 4128776 | tf_op jit(solution)/shard_map/ppermute | solution.py:62
  21.4 3.1 %collective-permute-done.2 = f32[16,168,128]{2,1,0:T(8,128)S(1)} collective-permute-done((f32[16,168,128]{2,1,0:T(8,128)S(1)}, f32[16,168,128]{2,1,0:T(8,128)S(1)}, u32[]{:S(2)}, u32[]{:S(2)}) %collective-permute-start.2) | collective-permute-done | bytes 1376288 | tf_op jit(solution)/shard_map/ppermute | solution.py:62
  24.5 1.5 %bitcast_add_fusion = f32[16,168,128]{2,1,0:T(8,128)S(1)} fusion(f32[16,168,128]{2,1,0:T(8,128)S(1)} %collective-permute-done.2, f32[2,16,168,128]{3,2,1,0:T(8,128)} %bitcast.42, s32[]{:T(128)S(6)} %select_n.66), kind=kLoop, calls=%fused_computation.2 | loop fusion | flops 344064 | bytes 4128772 | tf_op jit(solution)/shard_map/add | solution.py:62
  26.0 0.1 dynamic-slice_bitcast_fusion.1
  26.1 3.3 %collective-permute-start.3 = (f32[8,168,128]{2,1,0:T(8,128)S(1)}, f32[8,168,128]{2,1,0:T(8,128)S(1)}, u32[]{:S(2)}, u32[]{:S(2)}) collective-permute-start(f32[8,168,128]{2,1,0:T(8,128)S(1)} %dynamic-slice_bitcast_fusion.1), channel_id=1, source_target_pairs={{0,4},{1,29},{2,6},{3,31},{4,0},{5,9},{6,2},{7,11},{8,12},{9,5},{1... | collective-permute-start | bytes 2064392 | tf_op jit(solution)/shard_map/ppermute | solution.py:62
  29.3 9.6 %collective-permute-done.3 = f32[8,168,128]{2,1,0:T(8,128)S(1)} collective-permute-done((f32[8,168,128]{2,1,0:T(8,128)S(1)}, f32[8,168,128]{2,1,0:T(8,128)S(1)}, u32[]{:S(2)}, u32[]{:S(2)}) %collective-permute-start.3) | collective-permute-done | bytes 688160 | tf_op jit(solution)/shard_map/ppermute | solution.py:62
  38.9 0.1 bitcast_add_fusion.1
  39.0 4.6 %collective-permute-start.4 = (f32[4,168,128]{2,1,0:T(8,128)S(1)}, f32[4,168,128]{2,1,0:T(8,128)S(1)}, u32[]{:S(2)}, u32[]{:S(2)}) collective-permute-start(f32[4,168,128]{2,1,0:T(8,128)S(1)} %dynamic-slice_bitcast_fusion.2), channel_id=1, source_target_pairs={{0,8},{1,3},{2,10},{3,1},{4,12},{5,7},{6,14},{7,5},{8,0},{9,11},{1... | collective-permute-start | bytes 1032200 | tf_op jit(solution)/shard_map/ppermute | solution.py:62
  43.6 0.0 copy-start.4
  43.6 0.0 copy-start.6
  43.6 9.1 %collective-permute-done.4 = f32[4,168,128]{2,1,0:T(8,128)S(1)} collective-permute-done((f32[4,168,128]{2,1,0:T(8,128)S(1)}, f32[4,168,128]{2,1,0:T(8,128)S(1)}, u32[]{:S(2)}, u32[]{:S(2)}) %collective-permute-start.4) | collective-permute-done | bytes 344096 | tf_op jit(solution)/shard_map/ppermute | solution.py:62
  52.8 0.0 copy-start.2
  52.8 4.2 %collective-permute-start.5 = (f32[2,168,128]{2,1,0:T(8,128)S(1)}, f32[2,168,128]{2,1,0:T(8,128)S(1)}, u32[]{:S(2)}, u32[]{:S(2)}) collective-permute-start(f32[2,168,128]{2,1,0:T(8,128)S(1)} %dynamic-slice_bitcast_fusion.3), channel_id=1, source_target_pairs={{0,2},{1,9},{2,0},{3,11},{4,6},{5,29},{6,4},{7,31},{8,10},{9,1},{1... | collective-permute-start | bytes 516104 | tf_op jit(solution)/shard_map/ppermute | solution.py:62
  57.0 4.8 %collective-permute-done.5 = f32[2,168,128]{2,1,0:T(8,128)S(1)} collective-permute-done((f32[2,168,128]{2,1,0:T(8,128)S(1)}, f32[2,168,128]{2,1,0:T(8,128)S(1)}, u32[]{:S(2)}, u32[]{:S(2)}) %collective-permute-start.5) | collective-permute-done | bytes 172064 | tf_op jit(solution)/shard_map/ppermute | solution.py:62
  61.8 4.6 %collective-permute-start.6 = (f32[1,168,128]{2,1,0:T(8,128)S(1)}, f32[1,168,128]{2,1,0:T(8,128)S(1)}, u32[]{:S(2)}, u32[]{:S(2)}) collective-permute-start(f32[1,168,128]{2,1,0:T(8,128)S(1)} %constant_dynamic-slice_fusion), channel_id=1, source_target_pairs={{0,16},{1,17},{2,18},{3,19},{4,20},{5,21},{6,22},{7,23},{8,24},{9,... | collective-permute-start | bytes 258056 | tf_op jit(solution)/shard_map/ppermute | solution.py:62
  66.4 5.7 %collective-permute-done.6 = f32[1,168,128]{2,1,0:T(8,128)S(1)} collective-permute-done((f32[1,168,128]{2,1,0:T(8,128)S(1)}, f32[1,168,128]{2,1,0:T(8,128)S(1)}, u32[]{:S(2)}, u32[]{:S(2)}) %collective-permute-start.6) | collective-permute-done | bytes 86048 | tf_op jit(solution)/shard_map/ppermute | solution.py:62
  72.1 4.3 %collective-permute-start.7 = (f32[168,128]{1,0:T(8,128)S(1)}, f32[168,128]{1,0:T(8,128)S(1)}, u32[]{:S(2)}, u32[]{:S(2)}) collective-permute-start(f32[168,128]{1,0:T(8,128)S(1)} %add_bitcast_fusion), channel_id=1, source_target_pairs={{0,32},{1,257},{2,34},{3,259},{4,36},{5,261},{6,38},{7,263},{8,40}... | collective-permute-start | bytes 258056 | tf_op jit(solution)/shard_map/ppermute | solution.py:77
  76.4 0.1 pad_maximum_fusion.2
  76.5 3.6 %collective-permute-start.1 = (bf16[256,1024]{1,0:T(8,128)(2,1)S(1)}, bf16[256,1024]{1,0:T(8,128)(2,1)S(1)}, u32[]{:S(2)}, u32[]{:S(2)}) collective-permute-start(bf16[256,1024]{1,0:T(8,128)(2,1)S(1)} %pad_maximum_fusion.2), channel_id=1, source_target_pairs={{2,0},{3,1},{4,2},{5,3},{6,4},{7,5},{8,6},{9,7},{10,8},{11,9},{12,... | collective-permute-start | bytes 1572872 | tf_op jit(solution)/shard_map/ppermute | solution.py:10
  80.0 0.0 collective-permute-done.7
  80.1 4.8 %collective-permute-start.8 = (f32[168,128]{1,0:T(8,128)S(1)}, f32[168,128]{1,0:T(8,128)S(1)}, u32[]{:S(2)}, u32[]{:S(2)}) collective-permute-start(f32[168,128]{1,0:T(8,128)S(1)} %add.132), channel_id=1, source_target_pairs={{0,256},{1,225},{2,258},{3,227},{4,260},{5,229},{6,262},{7,231},{8... | collective-permute-start | bytes 258056 | tf_op jit(solution)/shard_map/ppermute | solution.py:77
  84.8 1.4 %convolution_add_fusion.3 = f32[256,256]{1,0:T(8,128)S(1)} fusion(bf16[512,1024]{1,0:T(8,128)(2,1)} %param.7, bf16[256,256]{1,0:T(8,128)(2,1)} %param.6, bf16[256,512]{1,0:T(8,128)(2,1)S(1)} %get-tuple-element.6, bf16[256,512]{1,0:T(8,128)(2,1)S(1)} %get-tuple-element.5), kind=kOutput, calls=%fused_computation.10 | convolution fusion | flops 135397376 | bytes 1441792 | tf_op jit(solution)/shard_map/dot_general | solution.py:20
  86.3 11.0 %collective-permute-done.8 = f32[168,128]{1,0:T(8,128)S(1)} collective-permute-done((f32[168,128]{1,0:T(8,128)S(1)}, f32[168,128]{1,0:T(8,128)S(1)}, u32[]{:S(2)}, u32[]{:S(2)}) %collective-permute-start.8) | collective-permute-done | bytes 86048 | tf_op jit(solution)/shard_map/ppermute | solution.py:77
  97.2 1.9 %collective-permute-start.9 = (f32[168,128]{1,0:T(8,128)S(1)}, f32[168,128]{1,0:T(8,128)S(1)}, u32[]{:S(2)}, u32[]{:S(2)}) collective-permute-start(f32[168,128]{1,0:T(8,128)S(1)} %add.133), channel_id=1, source_target_pairs={{0,64},{1,129},{2,66},{3,131},{4,68},{5,133},{6,70},{7,135},{8,72}... | collective-permute-start | bytes 258056 | tf_op jit(solution)/shard_map/ppermute | solution.py:77
  99.2 0.0 copy-done.4
  99.2 0.0 copy-done.6
  99.2 0.9 fusion.1
  100.1 5.5 %collective-permute-done.9 = f32[168,128]{1,0:T(8,128)S(1)} collective-permute-done((f32[168,128]{1,0:T(8,128)S(1)}, f32[168,128]{1,0:T(8,128)S(1)}, u32[]{:S(2)}, u32[]{:S(2)}) %collective-permute-start.9) | collective-permute-done | bytes 86048 | tf_op jit(solution)/shard_map/ppermute | solution.py:77
  105.6 5.7 %collective-permute-start.10 = (f32[168,128]{1,0:T(8,128)S(1)}, f32[168,128]{1,0:T(8,128)S(1)}, u32[]{:S(2)}, u32[]{:S(2)}) collective-permute-start(f32[168,128]{1,0:T(8,128)S(1)} %add.134), channel_id=1, source_target_pairs={{0,128},{1,65},{2,130},{3,67},{4,132},{5,69},{6,134},{7,71},{8,136... | collective-permute-start | bytes 258056 | tf_op jit(solution)/shard_map/ppermute | solution.py:77
  111.3 0.0 collective-permute-done.1
  111.3 0.0 copy-done.2
  111.3 1.0 fusion.2
  112.3 3.5 %collective-permute-done.10 = f32[168,128]{1,0:T(8,128)S(1)} collective-permute-done((f32[168,128]{1,0:T(8,128)S(1)}, f32[168,128]{1,0:T(8,128)S(1)}, u32[]{:S(2)}, u32[]{:S(2)}) %collective-permute-start.10) | collective-permute-done | bytes 86048 | tf_op jit(solution)/shard_map/ppermute | solution.py:77
  115.9 0.5 slice_bitcast_fusion
  116.4 0.6 reshape.50
  117.0 0.6 reshape.51
  (46 shorter events, 0.5 us)
Async XLA Ops:
  0.6 11.3 %copy-start = (bf16[512,256]{1,0:T(8,128)(2,1)S(1)}, bf16[512,256]{1,0:T(8,128)(2,1)}, u32[]{:S(2)}) copy-start(bf16[512,256]{1,0:T(8,128)(2,1)} %param.9) | copy-start | bytes 786436
  0.6 11.3 %copy-start.7 = (bf16[256,256]{1,0:T(8,128)(2,1)S(1)}, bf16[256,256]{1,0:T(8,128)(2,1)}, u32[]{:S(2)}) copy-start(bf16[256,256]{1,0:T(8,128)(2,1)} %param.6) | copy-start | bytes 393220
  0.7 9.9 %collective-permute-start = (bf16[256,256]{1,0:T(8,128)(2,1)}, bf16[256,256]{1,0:T(8,128)(2,1)S(1)}, u32[]{:S(2)}, u32[]{:S(2)}) collective-permute-start(bf16[256,256]{1,0:T(8,128)(2,1)} %param.5), channel_id=1, source_target_pairs={{0,2},{1,3},{2,4},{3,5},{4,6},{5,7},{6,8},{7,9},{8,10},{9,11},{10,... | collective-permute-start | bytes 393224 | tf_op jit(solution)/shard_map/ppermute | solution.py:10
  11.9 0.9 copy-start.3
  12.4 1.5 %copy-start.5 = (bf16[256,512]{1,0:T(8,128)(2,1)}, bf16[256,512]{1,0:T(8,128)(2,1)S(1)}, u32[]{:S(2)}) copy-start(bf16[256,512]{1,0:T(8,128)(2,1)S(1)} %get-tuple-element.7) | copy-start | bytes 786436
  17.9 1.5 %copy-start.1 = (f32[32,168,128]{2,1,0:T(8,128)}, f32[32,168,128]{2,1,0:T(8,128)S(1)}, u32[]{:S(2)}) copy-start(f32[32,168,128]{2,1,0:T(8,128)S(1)} %slice_dynamic-update-slice_fusion) | copy-start | bytes 8257540
  19.5 5.0 %collective-permute-start.2 = (f32[16,168,128]{2,1,0:T(8,128)S(1)}, f32[16,168,128]{2,1,0:T(8,128)S(1)}, u32[]{:S(2)}, u32[]{:S(2)}) collective-permute-start(f32[16,168,128]{2,1,0:T(8,128)S(1)} %dynamic-slice_bitcast_fusion), channel_id=1, source_target_pairs={{0,1},{1,0},{2,3},{3,2},{4,5},{5,4},{6,7},{7,6},{8,9},{9,8},{10,11... | collective-permute-start | bytes 4128776 | tf_op jit(solution)/shard_map/ppermute | solution.py:62
  26.1 12.8 %collective-permute-start.3 = (f32[8,168,128]{2,1,0:T(8,128)S(1)}, f32[8,168,128]{2,1,0:T(8,128)S(1)}, u32[]{:S(2)}, u32[]{:S(2)}) collective-permute-start(f32[8,168,128]{2,1,0:T(8,128)S(1)} %dynamic-slice_bitcast_fusion.1), channel_id=1, source_target_pairs={{0,4},{1,29},{2,6},{3,31},{4,0},{5,9},{6,2},{7,11},{8,12},{9,5},{1... | collective-permute-start | bytes 2064392 | tf_op jit(solution)/shard_map/ppermute | solution.py:62
  39.0 13.7 %collective-permute-start.4 = (f32[4,168,128]{2,1,0:T(8,128)S(1)}, f32[4,168,128]{2,1,0:T(8,128)S(1)}, u32[]{:S(2)}, u32[]{:S(2)}) collective-permute-start(f32[4,168,128]{2,1,0:T(8,128)S(1)} %dynamic-slice_bitcast_fusion.2), channel_id=1, source_target_pairs={{0,8},{1,3},{2,10},{3,1},{4,12},{5,7},{6,14},{7,5},{8,0},{9,11},{1... | collective-permute-start | bytes 1032200 | tf_op jit(solution)/shard_map/ppermute | solution.py:62
  43.6 55.6 %copy-start.4 = (bf16[256,256]{1,0:T(8,128)(2,1)S(1)}, bf16[256,256]{1,0:T(8,128)(2,1)}, u32[]{:S(2)}) copy-start(bf16[256,256]{1,0:T(8,128)(2,1)} %param.5) | copy-start | bytes 393220
  43.6 55.6 %copy-start.6 = (bf16[256,512]{1,0:T(8,128)(2,1)S(1)}, bf16[256,512]{1,0:T(8,128)(2,1)}, u32[]{:S(2)}) copy-start(bf16[256,512]{1,0:T(8,128)(2,1)} %copy-done.5) | copy-start | bytes 786436
  52.8 58.5 %copy-start.2 = (bf16[512,1024]{1,0:T(8,128)(2,1)S(1)}, bf16[512,1024]{1,0:T(8,128)(2,1)}, u32[]{:S(2)}) copy-start(bf16[512,1024]{1,0:T(8,128)(2,1)} %param.7) | copy-start | bytes 3145732
  52.8 8.9 %collective-permute-start.5 = (f32[2,168,128]{2,1,0:T(8,128)S(1)}, f32[2,168,128]{2,1,0:T(8,128)S(1)}, u32[]{:S(2)}, u32[]{:S(2)}) collective-permute-start(f32[2,168,128]{2,1,0:T(8,128)S(1)} %dynamic-slice_bitcast_fusion.3), channel_id=1, source_target_pairs={{0,2},{1,9},{2,0},{3,11},{4,6},{5,29},{6,4},{7,31},{8,10},{9,1},{1... | collective-permute-start | bytes 516104 | tf_op jit(solution)/shard_map/ppermute | solution.py:62
  61.8 10.3 %collective-permute-start.6 = (f32[1,168,128]{2,1,0:T(8,128)S(1)}, f32[1,168,128]{2,1,0:T(8,128)S(1)}, u32[]{:S(2)}, u32[]{:S(2)}) collective-permute-start(f32[1,168,128]{2,1,0:T(8,128)S(1)} %constant_dynamic-slice_fusion), channel_id=1, source_target_pairs={{0,16},{1,17},{2,18},{3,19},{4,20},{5,21},{6,22},{7,23},{8,24},{9,... | collective-permute-start | bytes 258056 | tf_op jit(solution)/shard_map/ppermute | solution.py:62
  72.1 7.9 %collective-permute-start.7 = (f32[168,128]{1,0:T(8,128)S(1)}, f32[168,128]{1,0:T(8,128)S(1)}, u32[]{:S(2)}, u32[]{:S(2)}) collective-permute-start(f32[168,128]{1,0:T(8,128)S(1)} %add_bitcast_fusion), channel_id=1, source_target_pairs={{0,32},{1,257},{2,34},{3,259},{4,36},{5,261},{6,38},{7,263},{8,40}... | collective-permute-start | bytes 258056 | tf_op jit(solution)/shard_map/ppermute | solution.py:77
  76.5 34.8 %collective-permute-start.1 = (bf16[256,1024]{1,0:T(8,128)(2,1)S(1)}, bf16[256,1024]{1,0:T(8,128)(2,1)S(1)}, u32[]{:S(2)}, u32[]{:S(2)}) collective-permute-start(bf16[256,1024]{1,0:T(8,128)(2,1)S(1)} %pad_maximum_fusion.2), channel_id=1, source_target_pairs={{2,0},{3,1},{4,2},{5,3},{6,4},{7,5},{8,6},{9,7},{10,8},{11,9},{12,... | collective-permute-start | bytes 1572872 | tf_op jit(solution)/shard_map/ppermute | solution.py:10
  80.1 17.2 %collective-permute-start.8 = (f32[168,128]{1,0:T(8,128)S(1)}, f32[168,128]{1,0:T(8,128)S(1)}, u32[]{:S(2)}, u32[]{:S(2)}) collective-permute-start(f32[168,128]{1,0:T(8,128)S(1)} %add.132), channel_id=1, source_target_pairs={{0,256},{1,225},{2,258},{3,227},{4,260},{5,229},{6,262},{7,231},{8... | collective-permute-start | bytes 258056 | tf_op jit(solution)/shard_map/ppermute | solution.py:77
  97.2 8.3 %collective-permute-start.9 = (f32[168,128]{1,0:T(8,128)S(1)}, f32[168,128]{1,0:T(8,128)S(1)}, u32[]{:S(2)}, u32[]{:S(2)}) collective-permute-start(f32[168,128]{1,0:T(8,128)S(1)} %add.133), channel_id=1, source_target_pairs={{0,64},{1,129},{2,66},{3,131},{4,68},{5,133},{6,70},{7,135},{8,72}... | collective-permute-start | bytes 258056 | tf_op jit(solution)/shard_map/ppermute | solution.py:77
  105.6 10.3 %collective-permute-start.10 = (f32[168,128]{1,0:T(8,128)S(1)}, f32[168,128]{1,0:T(8,128)S(1)}, u32[]{:S(2)}, u32[]{:S(2)}) collective-permute-start(f32[168,128]{1,0:T(8,128)S(1)} %add.134), channel_id=1, source_target_pairs={{0,128},{1,65},{2,130},{3,67},{4,132},{5,69},{6,134},{7,71},{8,136... | collective-permute-start | bytes 258056 | tf_op jit(solution)/shard_map/ppermute | solution.py:77

commit v6 on v5

--- a/solution.py
+++ b/solution.py
@@ -77,6 +77,24 @@
         array = array + lax.ppermute(array, axes, pairs)
     return array
 
+def quad_sum(array, axis, pairs):
+    count = lax.axis_size(axis)
+    where = lax.axis_index(axis)
+    for lo, hi in pairs:
+        masks = [1 << lo, 1 << hi, (1 << lo) | (1 << hi)]
+        got = [lax.ppermute(array, axis, [(i, i ^ m) for i in range(count)]) for m in masks]
+        q = ((where >> lo) & 1) + 2 * ((where >> hi) & 1)
+        by_mask = [array] + got
+        vals = []
+        for k in range(4):
+            x = k ^ q
+            v = jnp.where(x == 1, by_mask[1], by_mask[0])
+            v = jnp.where(x == 2, by_mask[2], v)
+            vals.append(jnp.where(x == 3, by_mask[3], v))
+        array = (vals[0] + vals[1]) + (vals[2] + vals[3])
+    return array
+
+
 def per_device(signal, cotangent, w_taps, gate_bias, w_out):
     width = signal.shape[1]
     units = w_out.shape[0]
@@ -129,7 +147,7 @@
         axis=1,
     )
     mine = halving_scatter(packed, "seq", ([0, 2, 3, 1, 4], [0, 2, 1, 3, 4]), (4, 8))
-    mine = butterfly_sum(mine, ("grp", "seq"), ([0, 3, 1, 2], [3, 0, 2, 1]), (1, 8), groups)
+    mine = quad_sum(mine, "grp", [(0, 3), (1, 2)])
     grad_taps = mine[:taps_r].reshape(rows_taps, part_taps.shape[1])
     grad_out = mine[taps_r : taps_r + out_r].reshape(rows_out, part_out.shape[1])
     grad_bias = mine[taps_r + out_r, :share_bias]

time: 118 us -> 118 us (level)
  waiting for transfers between devices: 55.5 us -> 43.4 us
  starting transfers between devices: 43.9 us -> 51.7 us
  other arithmetic: 3.5 us -> 5.97 us
    ppermute x4 -> x6, waiting for transfers between devices: 20 us -> 9.68 us  [quad_sum(): lax.ppermute(array, axis, [(i, i ^ m) for i in range(count)])]
    ppermute x4 -> x6, starting transfers between devices: 16.7 us -> 25.9 us  [quad_sum(): lax.ppermute(array, axis, [(i, i ^ m) for i in range(count)])]
    ppermute x5, waiting for transfers between devices: 32.2 us -> 30.4 us  [halving_scatter(): buf = keep + lax.ppermute(send, axis, pairs)]
    ppermute x2, starting transfers between devices: 8.63 us -> 7.07 us  [from_behind(): return lax.ppermute(array, axis, pairs)]
    add x4, other arithmetic: 1.61 us -> 3.12 us  [halving_scatter(): buf = keep + lax.ppermute(send, axis, pairs)]
  transfers between devices with their start and end apart: 11 -> 13, of which waited for: 9 -> 10; matrix products, arithmetic and copies ran while one was open for 4% -> 4% of each run, Pallas kernels for 0% -> 0%
where the time goes in v6:
time: 118 us; the launch traced here: 117 us
  starting transfers between devices  51.7 us (44%)
  waiting for transfers between devices  43.4 us (37%)
  matrix products  7.4 us (6%)
  local copies, waits for them, and re-layouts  6.68 us (6%)
  other arithmetic  5.97 us (5%)
  between operations  1.4 us (1%)
    ppermute x5, waiting for transfers between devices, halving_scatter(): buf = keep + lax.ppermute(send, axis, pairs)  30.4 us
    ppermute x6, starting transfers between devices, quad_sum(): lax.ppermute(array, axis, [(i, i ^ m) for i in range(count)])  25.9 us
    ppermute x5, starting transfers between devices, halving_scatter(): buf = keep + lax.ppermute(send, axis, pairs)  18.7 us
    ppermute x6, waiting for transfers between devices, quad_sum(): lax.ppermute(array, axis, [(i, i ^ m) for i in range(count)])  9.68 us
    ppermute x2, starting transfers between devices, from_behind(): return lax.ppermute(array, axis, pairs)  7.07 us
    ppermute x2, waiting for transfers between devices, from_behind(): return lax.ppermute(array, axis, pairs)  3.33 us
    add x4, other arithmetic, halving_scatter(): buf = keep + lax.ppermute(send, axis, pairs)  3.12 us
    dot_general x3, matrix products, contract_cols(): lax.dot_general(left, right, (((1,), (1,)), ((), ())), preferred_element_...  2.83 us
  transfers between devices with their start and end apart: 13, of which 10 were waited for; matrix products, arithmetic and copies ran while one was open for 4% of the time, Pallas kernels for 0%

profile of v6, /device:TPU:56, one launch (start us, length us, event | category | flops | bytes accessed | tf_op | source)
XLA Modules:
  0.0 116.5 jit_solution(17093772660230049288)
XLA Ops:
  0.6 0.0 copy-start
  0.6 0.0 copy-start.6
  0.7 5.1 %collective-permute-start = (bf16[256,256]{1,0:T(8,128)(2,1)}, bf16[256,256]{1,0:T(8,128)(2,1)S(1)}, u32[]{:S(2)}, u32[]{:S(2)}) collective-permute-start(bf16[256,256]{1,0:T(8,128)(2,1)} %param.5), channel_id=1, source_target_pairs={{0,2},{1,3},{2,4},{3,5},{4,6},{5,7},{6,8},{7,9},{8,10},{9,11},{10,... | collective-permute-start | bytes 393224 | tf_op jit(solution)/shard_map/ppermute | solution.py:10
  5.7 1.4 %fusion.9 = f32[256,1024]{1,0:T(8,128)S(1)} fusion(bf16[256,256]{1,0:T(8,128)(2,1)} %param.5, bf16[512,1024]{1,0:T(8,128)(2,1)} %param.7), kind=kOutput, calls=%fused_computation.28 | convolution fusion | flops 134217728 | bytes 1703936 | tf_op jit(solution)/shard_map/dot_general | solution.py:102
  7.2 3.3 %collective-permute-done = bf16[256,256]{1,0:T(8,128)(2,1)S(1)} collective-permute-done((bf16[256,256]{1,0:T(8,128)(2,1)}, bf16[256,256]{1,0:T(8,128)(2,1)S(1)}, u32[]{:S(2)}, u32[]{:S(2)}) %collective-permute-start) | collective-permute-done | bytes 131104 | tf_op jit(solution)/shard_map/ppermute | solution.py:10
  10.5 1.3 %fusion = f32[256,1024]{1,0:T(8,128)S(1)} fusion(f32[256,1024]{1,0:T(8,128)S(1)} %fusion.9, bf16[256,256]{1,0:T(8,128)(2,1)S(1)} %collective-permute-done, f32[1024]{0:T(1024)} %param.8, bf16[512,1024]{1,0:T(8,128)(2,1)} %param.7), kind=kOutput, calls=%fused_computation.7 | convolution fusion | flops 134742016 | bytes 2756608 | tf_op jit(solution)/shard_map/dot_general | solution.py:105
  11.9 0.0 copy-done
  11.9 0.0 copy-done.6
  11.9 0.0 copy-start.3
  11.9 0.5 multiply_convert_fusion.1
  12.4 0.0 copy-start.4
  12.4 0.1 convert_reduce_fusion
  12.5 0.3 copy-done.3
  12.8 0.3 convolution_bitcast_fusion
  13.2 0.1 reshape.45
  13.2 0.7 pad_slice_fusion
  13.9 0.3 fusion.11
  14.2 0.3 convolution_bitcast_fusion.1
  14.6 0.0 copy-done.4
  14.6 1.5 %pad_maximum_fusion.1 = f32[512,1024]{1,0:T(8,128)} fusion(f32[256,1024]{1,0:T(8,128)S(1)} %convolution_bitcast_fusion, f32[256,1024]{1,0:T(8,128)S(1)} %convolution_bitcast_fusion.1), kind=kLoop, calls=%fused_computation.1 | loop fusion | flops 524288 | bytes 4194304 | tf_op jit(solution)/shard_map/concatenate | solution.py:124
  16.1 1.7 %reshape.43 = f32[32,128,128]{2,1,0:T(8,128)S(1)} reshape(f32[512,1024]{1,0:T(8,128)} %pad_maximum_fusion.1) | data formatting | bytes 4194304 | tf_op jit(solution)/shard_map/reshape | solution.py:143
  17.8 1.1 pad_maximum_fusion
  19.4 0.0 copy-start.1
  19.4 1.5 %copy-done.1 = f32[32,168,128]{2,1,0:T(8,128)} copy-done((f32[32,168,128]{2,1,0:T(8,128)}, f32[32,168,128]{2,1,0:T(8,128)S(1)}, u32[]{:S(2)}) %copy-start.1) | copy-done | bytes 2752536
  21.0 0.1 dynamic-slice_bitcast_fusion
  21.1 1.9 %collective-permute-start.2 = (f32[16,168,128]{2,1,0:T(8,128)S(1)}, f32[16,168,128]{2,1,0:T(8,128)}, u32[]{:S(2)}, u32[]{:S(2)}) collective-permute-start(f32[16,168,128]{2,1,0:T(8,128)S(1)} %dynamic-slice_bitcast_fusion), channel_id=1, source_target_pairs={{0,1},{1,0},{2,3},{3,2},{4,5},{5,4},{6,7},{7,6},{8,9},{9,8},{10,11... | collective-permute-start | bytes 4128776 | tf_op jit(solution)/shard_map/ppermute | solution.py:62
  23.0 3.2 %collective-permute-done.2 = f32[16,168,128]{2,1,0:T(8,128)} collective-permute-done((f32[16,168,128]{2,1,0:T(8,128)S(1)}, f32[16,168,128]{2,1,0:T(8,128)}, u32[]{:S(2)}, u32[]{:S(2)}) %collective-permute-start.2) | collective-permute-done | bytes 1376288 | tf_op jit(solution)/shard_map/ppermute | solution.py:62
  26.2 1.9 %bitcast_add_fusion = f32[16,168,128]{2,1,0:T(8,128)S(1)} fusion(f32[16,168,128]{2,1,0:T(8,128)} %collective-permute-done.2, f32[2,16,168,128]{3,2,1,0:T(8,128)} %bitcast.42, s32[]{:T(128)S(6)} %select_n.214), kind=kLoop, calls=%fused_computation.2 | loop fusion | flops 344064 | bytes 4128772 | tf_op jit(solution)/shard_map/add | solution.py:62
  28.1 0.0 copy-start.7
  28.1 0.1 dynamic-slice_bitcast_fusion.1
  28.2 3.3 %collective-permute-start.3 = (f32[8,168,128]{2,1,0:T(8,128)S(1)}, f32[8,168,128]{2,1,0:T(8,128)}, u32[]{:S(2)}, u32[]{:S(2)}) collective-permute-start(f32[8,168,128]{2,1,0:T(8,128)S(1)} %dynamic-slice_bitcast_fusion.1), channel_id=1, source_target_pairs={{0,4},{1,29},{2,6},{3,31},{4,0},{5,9},{6,2},{7,11},{8,12},{9,5},{1... | collective-permute-start | bytes 2064392 | tf_op jit(solution)/shard_map/ppermute | solution.py:62
  31.5 9.7 %collective-permute-done.3 = f32[8,168,128]{2,1,0:T(8,128)} collective-permute-done((f32[8,168,128]{2,1,0:T(8,128)S(1)}, f32[8,168,128]{2,1,0:T(8,128)}, u32[]{:S(2)}, u32[]{:S(2)}) %collective-permute-start.3) | collective-permute-done | bytes 688160 | tf_op jit(solution)/shard_map/ppermute | solution.py:62
  41.1 1.2 %bitcast_add_fusion.1 = f32[8,168,128]{2,1,0:T(8,128)S(1)} fusion(f32[8,168,128]{2,1,0:T(8,128)} %collective-permute-done.3, f32[2,8,168,128]{3,2,1,0:T(8,128)S(1)} %bitcast.40, s32[]{:T(128)S(6)} %select_n.216), kind=kLoop, calls=%fused_computation.14 | loop fusion | flops 172032 | bytes 2064388 | tf_op jit(solution)/shard_map/add | solution.py:62
  42.3 0.0 copy-start.5
  42.3 4.7 %collective-permute-start.4 = (f32[4,168,128]{2,1,0:T(8,128)S(1)}, f32[4,168,128]{2,1,0:T(8,128)S(1)}, u32[]{:S(2)}, u32[]{:S(2)}) collective-permute-start(f32[4,168,128]{2,1,0:T(8,128)S(1)} %dynamic-slice_bitcast_fusion.2), channel_id=1, source_target_pairs={{0,8},{1,3},{2,10},{3,1},{4,12},{5,7},{6,14},{7,5},{8,0},{9,11},{1... | collective-permute-start | bytes 1032200 | tf_op jit(solution)/shard_map/ppermute | solution.py:62
  47.1 9.1 %collective-permute-done.4 = f32[4,168,128]{2,1,0:T(8,128)S(1)} collective-permute-done((f32[4,168,128]{2,1,0:T(8,128)S(1)}, f32[4,168,128]{2,1,0:T(8,128)S(1)}, u32[]{:S(2)}, u32[]{:S(2)}) %collective-permute-start.4) | collective-permute-done | bytes 344096 | tf_op jit(solution)/shard_map/ppermute | solution.py:62
  56.2 0.0 copy-start.2
  56.3 4.2 %collective-permute-start.5 = (f32[2,168,128]{2,1,0:T(8,128)S(1)}, f32[2,168,128]{2,1,0:T(8,128)S(1)}, u32[]{:S(2)}, u32[]{:S(2)}) collective-permute-start(f32[2,168,128]{2,1,0:T(8,128)S(1)} %dynamic-slice_bitcast_fusion.3), channel_id=1, source_target_pairs={{0,2},{1,9},{2,0},{3,11},{4,6},{5,29},{6,4},{7,31},{8,10},{9,1},{1... | collective-permute-start | bytes 516104 | tf_op jit(solution)/shard_map/ppermute | solution.py:62
  60.5 1.4 %convolution_add_fusion.3 = f32[256,256]{1,0:T(8,128)S(1)} fusion(bf16[512,1024]{1,0:T(8,128)(2,1)} %param.7, bf16[256,256]{1,0:T(8,128)(2,1)S(1)} %copy-done.7, bf16[256,512]{1,0:T(8,128)(2,1)S(1)} %get-tuple-element.6, bf16[256,512]{1,0:T(8,128)(2,1)S(1)} %get-tuple-element.5), kind=kOutput, calls=%fused_computation.10 | convolution fusion | flops 135397376 | bytes 1441792 | tf_op jit(solution)/shard_map/dot_general | solution.py:20
  61.9 3.4 %collective-permute-done.5 = f32[2,168,128]{2,1,0:T(8,128)S(1)} collective-permute-done((f32[2,168,128]{2,1,0:T(8,128)S(1)}, f32[2,168,128]{2,1,0:T(8,128)S(1)}, u32[]{:S(2)}, u32[]{:S(2)}) %collective-permute-start.5) | collective-permute-done | bytes 172064 | tf_op jit(solution)/shard_map/ppermute | solution.py:62
  65.3 4.6 %collective-permute-start.6 = (f32[1,168,128]{2,1,0:T(8,128)S(1)}, f32[1,168,128]{2,1,0:T(8,128)S(1)}, u32[]{:S(2)}, u32[]{:S(2)}) collective-permute-start(f32[1,168,128]{2,1,0:T(8,128)S(1)} %constant_dynamic-slice_fusion), channel_id=1, source_target_pairs={{0,16},{1,17},{2,18},{3,19},{4,20},{5,21},{6,22},{7,23},{8,24},{9,... | collective-permute-start | bytes 258056 | tf_op jit(solution)/shard_map/ppermute | solution.py:62
  69.9 0.1 pad_maximum_fusion.2
  69.9 2.0 %collective-permute-start.1 = (bf16[256,1024]{1,0:T(8,128)(2,1)S(1)}, bf16[256,1024]{1,0:T(8,128)(2,1)S(1)}, u32[]{:S(2)}, u32[]{:S(2)}) collective-permute-start(bf16[256,1024]{1,0:T(8,128)(2,1)S(1)} %pad_maximum_fusion.2), channel_id=1, source_target_pairs={{2,0},{3,1},{4,2},{5,3},{6,4},{7,5},{8,6},{9,7},{10,8},{11,9},{12,... | collective-permute-start | bytes 1572872 | tf_op jit(solution)/shard_map/ppermute | solution.py:10
  72.0 5.1 %collective-permute-done.6 = f32[1,168,128]{2,1,0:T(8,128)S(1)} collective-permute-done((f32[1,168,128]{2,1,0:T(8,128)S(1)}, f32[1,168,128]{2,1,0:T(8,128)S(1)}, u32[]{:S(2)}, u32[]{:S(2)}) %collective-permute-start.6) | collective-permute-done | bytes 86048 | tf_op jit(solution)/shard_map/ppermute | solution.py:62
  77.1 5.2 %collective-permute-start.7 = (f32[168,128]{1,0:T(8,128)S(1)}, f32[168,128]{1,0:T(8,128)S(1)}, u32[]{:S(2)}, u32[]{:S(2)}) collective-permute-start(f32[168,128]{1,0:T(8,128)S(1)} %add_bitcast_fusion), channel_id=1, source_target_pairs={{0,288},{32,256},{64,352},{96,320},{128,416},{160,384},{192,480},{... | collective-permute-start | bytes 258056 | tf_op jit(solution)/shard_map/ppermute | solution.py:85
  82.3 2.4 %collective-permute-start.8 = (f32[168,128]{1,0:T(8,128)S(1)}, f32[168,128]{1,0:T(8,128)S(1)}, u32[]{:S(2)}, u32[]{:S(2)}) collective-permute-start(f32[168,128]{1,0:T(8,128)S(1)} %add_bitcast_fusion), channel_id=1, source_target_pairs={{0,256},{32,288},{64,320},{96,352},{128,384},{160,416},{192,448},{... | collective-permute-start | bytes 258056 | tf_op jit(solution)/shard_map/ppermute | solution.py:85
  84.7 2.6 %collective-permute-start.9 = (f32[168,128]{1,0:T(8,128)S(1)}, f32[168,128]{1,0:T(8,128)S(1)}, u32[]{:S(2)}, u32[]{:S(2)}) collective-permute-start(f32[168,128]{1,0:T(8,128)S(1)} %add_bitcast_fusion), channel_id=1, source_target_pairs={{0,32},{32,0},{64,96},{96,64},{128,160},{160,128},{192,224},{224,1... | collective-permute-start | bytes 258056 | tf_op jit(solution)/shard_map/ppermute | solution.py:85
  87.3 0.9 fusion.1
  88.2 3.2 %collective-permute-done.7 = f32[168,128]{1,0:T(8,128)S(1)} collective-permute-done((f32[168,128]{1,0:T(8,128)S(1)}, f32[168,128]{1,0:T(8,128)S(1)}, u32[]{:S(2)}, u32[]{:S(2)}) %collective-permute-start.7) | collective-permute-done | bytes 86048 | tf_op jit(solution)/shard_map/ppermute | solution.py:85
  91.4 1.3 %collective-permute-done.8 = f32[168,128]{1,0:T(8,128)S(1)} collective-permute-done((f32[168,128]{1,0:T(8,128)S(1)}, f32[168,128]{1,0:T(8,128)S(1)}, u32[]{:S(2)}, u32[]{:S(2)}) %collective-permute-start.8) | collective-permute-done | bytes 86048 | tf_op jit(solution)/shard_map/ppermute | solution.py:85
  92.7 0.0 collective-permute-done.9
  92.7 0.1 add_add_fusion.1
  92.7 9.5 %collective-permute-start.10 = (f32[168,128]{1,0:T(8,128)S(1)}, f32[168,128]{1,0:T(8,128)S(1)}, u32[]{:S(2)}, u32[]{:S(2)}) collective-permute-start(f32[168,128]{1,0:T(8,128)S(1)} %add_add_fusion.1), channel_id=1, source_target_pairs={{0,192},{32,224},{64,128},{96,160},{128,64},{160,96},{192,0},{224,... | collective-permute-start | bytes 258056 | tf_op jit(solution)/shard_map/ppermute | solution.py:85
  102.2 2.0 %collective-permute-start.11 = (f32[168,128]{1,0:T(8,128)S(1)}, f32[168,128]{1,0:T(8,128)S(1)}, u32[]{:S(2)}, u32[]{:S(2)}) collective-permute-start(f32[168,128]{1,0:T(8,128)S(1)} %add_add_fusion.1), channel_id=1, source_target_pairs={{0,128},{32,160},{64,192},{96,224},{128,0},{160,32},{192,64},{224,... | collective-permute-start | bytes 258056 | tf_op jit(solution)/shard_map/ppermute | solution.py:85
  104.2 4.2 %collective-permute-start.12 = (f32[168,128]{1,0:T(8,128)S(1)}, f32[168,128]{1,0:T(8,128)S(1)}, u32[]{:S(2)}, u32[]{:S(2)}) collective-permute-start(f32[168,128]{1,0:T(8,128)S(1)} %add_add_fusion.1), channel_id=1, source_target_pairs={{0,64},{32,96},{64,0},{96,32},{128,192},{160,224},{192,128},{224,1... | collective-permute-start | bytes 258056 | tf_op jit(solution)/shard_map/ppermute | solution.py:85
  108.4 0.0 collective-permute-done.1
  108.4 0.0 copy-done.2
  108.5 1.0 fusion.2
  109.5 0.0 collective-permute-done.10
  109.5 3.1 %collective-permute-done.11 = f32[168,128]{1,0:T(8,128)S(1)} collective-permute-done((f32[168,128]{1,0:T(8,128)S(1)}, f32[168,128]{1,0:T(8,128)S(1)}, u32[]{:S(2)}, u32[]{:S(2)}) %collective-permute-start.11) | collective-permute-done | bytes 86048 | tf_op jit(solution)/shard_map/ppermute | solution.py:85
  112.5 2.2 %collective-permute-done.12 = f32[168,128]{1,0:T(8,128)S(1)} collective-permute-done((f32[168,128]{1,0:T(8,128)S(1)}, f32[168,128]{1,0:T(8,128)S(1)}, u32[]{:S(2)}, u32[]{:S(2)}) %collective-permute-start.12) | collective-permute-done | bytes 86048 | tf_op jit(solution)/shard_map/ppermute | solution.py:85
  114.8 0.5 slice_bitcast_fusion
  115.3 0.6 reshape.50
  115.9 0.6 reshape.51
  (44 shorter events, 0.5 us)
Async XLA Ops:
  0.6 11.3 %copy-start = (bf16[512,256]{1,0:T(8,128)(2,1)S(1)}, bf16[512,256]{1,0:T(8,128)(2,1)}, u32[]{:S(2)}) copy-start(bf16[512,256]{1,0:T(8,128)(2,1)} %param.9) | copy-start | bytes 786436
  0.6 11.3 %copy-start.6 = (bf16[256,256]{1,0:T(8,128)(2,1)S(1)}, bf16[256,256]{1,0:T(8,128)(2,1)}, u32[]{:S(2)}) copy-start(bf16[256,256]{1,0:T(8,128)(2,1)} %param.6) | copy-start | bytes 393220
  0.7 9.9 %collective-permute-start = (bf16[256,256]{1,0:T(8,128)(2,1)}, bf16[256,256]{1,0:T(8,128)(2,1)S(1)}, u32[]{:S(2)}, u32[]{:S(2)}) collective-permute-start(bf16[256,256]{1,0:T(8,128)(2,1)} %param.5), channel_id=1, source_target_pairs={{0,2},{1,3},{2,4},{3,5},{4,6},{5,7},{6,8},{7,9},{8,10},{9,11},{10,... | collective-permute-start | bytes 393224 | tf_op jit(solution)/shard_map/ppermute | solution.py:10
  11.9 0.9 copy-start.3
  12.4 2.2 %copy-start.4 = (bf16[256,512]{1,0:T(8,128)(2,1)}, bf16[256,512]{1,0:T(8,128)(2,1)S(1)}, u32[]{:S(2)}) copy-start(bf16[256,512]{1,0:T(8,128)(2,1)S(1)} %get-tuple-element.7) | copy-start | bytes 786436
  19.4 1.6 %copy-start.1 = (f32[32,168,128]{2,1,0:T(8,128)}, f32[32,168,128]{2,1,0:T(8,128)S(1)}, u32[]{:S(2)}) copy-start(f32[32,168,128]{2,1,0:T(8,128)S(1)} %slice_dynamic-update-slice_fusion) | copy-start | bytes 8257540
  21.1 5.2 %collective-permute-start.2 = (f32[16,168,128]{2,1,0:T(8,128)S(1)}, f32[16,168,128]{2,1,0:T(8,128)}, u32[]{:S(2)}, u32[]{:S(2)}) collective-permute-start(f32[16,168,128]{2,1,0:T(8,128)S(1)} %dynamic-slice_bitcast_fusion), channel_id=1, source_target_pairs={{0,1},{1,0},{2,3},{3,2},{4,5},{5,4},{6,7},{7,6},{8,9},{9,8},{10,11... | collective-permute-start | bytes 4128776 | tf_op jit(solution)/shard_map/ppermute | solution.py:62
  28.1 32.4 %copy-start.7 = (bf16[256,256]{1,0:T(8,128)(2,1)S(1)}, bf16[256,256]{1,0:T(8,128)(2,1)}, u32[]{:S(2)}) copy-start(bf16[256,256]{1,0:T(8,128)(2,1)} %param.6) | copy-start | bytes 393220
  28.2 12.9 %collective-permute-start.3 = (f32[8,168,128]{2,1,0:T(8,128)S(1)}, f32[8,168,128]{2,1,0:T(8,128)}, u32[]{:S(2)}, u32[]{:S(2)}) collective-permute-start(f32[8,168,128]{2,1,0:T(8,128)S(1)} %dynamic-slice_bitcast_fusion.1), channel_id=1, source_target_pairs={{0,4},{1,29},{2,6},{3,31},{4,0},{5,9},{6,2},{7,11},{8,12},{9,5},{1... | collective-permute-start | bytes 2064392 | tf_op jit(solution)/shard_map/ppermute | solution.py:62
  42.3 45.0 %copy-start.5 = (bf16[256,512]{1,0:T(8,128)(2,1)S(1)}, bf16[256,512]{1,0:T(8,128)(2,1)}, u32[]{:S(2)}) copy-start(bf16[256,512]{1,0:T(8,128)(2,1)} %copy-done.4) | copy-start | bytes 786436
  42.3 13.9 %collective-permute-start.4 = (f32[4,168,128]{2,1,0:T(8,128)S(1)}, f32[4,168,128]{2,1,0:T(8,128)S(1)}, u32[]{:S(2)}, u32[]{:S(2)}) collective-permute-start(f32[4,168,128]{2,1,0:T(8,128)S(1)} %dynamic-slice_bitcast_fusion.2), channel_id=1, source_target_pairs={{0,8},{1,3},{2,10},{3,1},{4,12},{5,7},{6,14},{7,5},{8,0},{9,11},{1... | collective-permute-start | bytes 1032200 | tf_op jit(solution)/shard_map/ppermute | solution.py:62
  56.2 52.2 %copy-start.2 = (bf16[512,1024]{1,0:T(8,128)(2,1)S(1)}, bf16[512,1024]{1,0:T(8,128)(2,1)}, u32[]{:S(2)}) copy-start(bf16[512,1024]{1,0:T(8,128)(2,1)} %param.7) | copy-start | bytes 3145732
  56.3 8.9 %collective-permute-start.5 = (f32[2,168,128]{2,1,0:T(8,128)S(1)}, f32[2,168,128]{2,1,0:T(8,128)S(1)}, u32[]{:S(2)}, u32[]{:S(2)}) collective-permute-start(f32[2,168,128]{2,1,0:T(8,128)S(1)} %dynamic-slice_bitcast_fusion.3), channel_id=1, source_target_pairs={{0,2},{1,9},{2,0},{3,11},{4,6},{5,29},{6,4},{7,31},{8,10},{9,1},{1... | collective-permute-start | bytes 516104 | tf_op jit(solution)/shard_map/ppermute | solution.py:62
  65.3 11.8 %collective-permute-start.6 = (f32[1,168,128]{2,1,0:T(8,128)S(1)}, f32[1,168,128]{2,1,0:T(8,128)S(1)}, u32[]{:S(2)}, u32[]{:S(2)}) collective-permute-start(f32[1,168,128]{2,1,0:T(8,128)S(1)} %constant_dynamic-slice_fusion), channel_id=1, source_target_pairs={{0,16},{1,17},{2,18},{3,19},{4,20},{5,21},{6,22},{7,23},{8,24},{9,... | collective-permute-start | bytes 258056 | tf_op jit(solution)/shard_map/ppermute | solution.py:62
  69.9 38.5 %collective-permute-start.1 = (bf16[256,1024]{1,0:T(8,128)(2,1)S(1)}, bf16[256,1024]{1,0:T(8,128)(2,1)S(1)}, u32[]{:S(2)}, u32[]{:S(2)}) collective-permute-start(bf16[256,1024]{1,0:T(8,128)(2,1)S(1)} %pad_maximum_fusion.2), channel_id=1, source_target_pairs={{2,0},{3,1},{4,2},{5,3},{6,4},{7,5},{8,6},{9,7},{10,8},{11,9},{12,... | collective-permute-start | bytes 1572872 | tf_op jit(solution)/shard_map/ppermute | solution.py:10
  77.1 14.3 %collective-permute-start.7 = (f32[168,128]{1,0:T(8,128)S(1)}, f32[168,128]{1,0:T(8,128)S(1)}, u32[]{:S(2)}, u32[]{:S(2)}) collective-permute-start(f32[168,128]{1,0:T(8,128)S(1)} %add_bitcast_fusion), channel_id=1, source_target_pairs={{0,288},{32,256},{64,352},{96,320},{128,416},{160,384},{192,480},{... | collective-permute-start | bytes 258056 | tf_op jit(solution)/shard_map/ppermute | solution.py:85
  82.3 10.4 %collective-permute-start.8 = (f32[168,128]{1,0:T(8,128)S(1)}, f32[168,128]{1,0:T(8,128)S(1)}, u32[]{:S(2)}, u32[]{:S(2)}) collective-permute-start(f32[168,128]{1,0:T(8,128)S(1)} %add_bitcast_fusion), channel_id=1, source_target_pairs={{0,256},{32,288},{64,320},{96,352},{128,384},{160,416},{192,448},{... | collective-permute-start | bytes 258056 | tf_op jit(solution)/shard_map/ppermute | solution.py:85
  84.7 7.9 %collective-permute-start.9 = (f32[168,128]{1,0:T(8,128)S(1)}, f32[168,128]{1,0:T(8,128)S(1)}, u32[]{:S(2)}, u32[]{:S(2)}) collective-permute-start(f32[168,128]{1,0:T(8,128)S(1)} %add_bitcast_fusion), channel_id=1, source_target_pairs={{0,32},{32,0},{64,96},{96,64},{128,160},{160,128},{192,224},{224,1... | collective-permute-start | bytes 258056 | tf_op jit(solution)/shard_map/ppermute | solution.py:85
  92.7 16.7 %collective-permute-start.10 = (f32[168,128]{1,0:T(8,128)S(1)}, f32[168,128]{1,0:T(8,128)S(1)}, u32[]{:S(2)}, u32[]{:S(2)}) collective-permute-start(f32[168,128]{1,0:T(8,128)S(1)} %add_add_fusion.1), channel_id=1, source_target_pairs={{0,192},{32,224},{64,128},{96,160},{128,64},{160,96},{192,0},{224,... | collective-permute-start | bytes 258056 | tf_op jit(solution)/shard_map/ppermute | solution.py:85
  102.2 10.3 %collective-permute-start.11 = (f32[168,128]{1,0:T(8,128)S(1)}, f32[168,128]{1,0:T(8,128)S(1)}, u32[]{:S(2)}, u32[]{:S(2)}) collective-permute-start(f32[168,128]{1,0:T(8,128)S(1)} %add_add_fusion.1), channel_id=1, source_target_pairs={{0,128},{32,160},{64,192},{96,224},{128,0},{160,32},{192,64},{224,... | collective-permute-start | bytes 258056 | tf_op jit(solution)/shard_map/ppermute | solution.py:85
  104.2 10.5 %collective-permute-start.12 = (f32[168,128]{1,0:T(8,128)S(1)}, f32[168,128]{1,0:T(8,128)S(1)}, u32[]{:S(2)}, u32[]{:S(2)}) collective-permute-start(f32[168,128]{1,0:T(8,128)S(1)} %add_add_fusion.1), channel_id=1, source_target_pairs={{0,64},{32,96},{64,0},{96,32},{128,192},{160,224},{192,128},{224,1... | collective-permute-start | bytes 258056 | tf_op jit(solution)/shard_map/ppermute | solution.py:85

commit v7 on v5

--- a/solution.py
+++ b/solution.py
@@ -31,12 +31,9 @@
     return relabel(index, rotate, size, -1)
 
 
-def halving_scatter(shares, axis, orders, ring):
-    count = shares.shape[0]
+def share_rows(count, orders, ring):
     bits = count.bit_length() - 1
-    rest = shares.shape[1:]
     rotate, size = ring
-    where = lax.axis_index(axis)
     rows = []
     for c, order in enumerate(orders):
         for p in range(count // 2):
@@ -44,7 +41,16 @@
             for t, b in enumerate(order[1:]):
                 v |= ((p >> (bits - 2 - t)) & 1) << b
             rows.append(unlabel(v, rotate, size) if c else v)
-    buf = jnp.concatenate([shares[s : s + 1] for s in rows])
+    return rows
+
+
+def halving_scatter(shares, axis, orders, ring):
+    count = shares.shape[0]
+    bits = count.bit_length() - 1
+    rest = shares.shape[1:]
+    rotate, size = ring
+    where = lax.axis_index(axis)
+    buf = shares
     core = where & 1
     mine = jnp.where(core == 1, relabel(where, rotate, size), where)
     for step in range(bits):
@@ -102,16 +108,24 @@
         ],
         axis=1,
     ).astype(jnp.bfloat16)
-    part_out = reduced_row_axes(hidden_state, cotangent)
-    part_taps = jnp.concatenate(
-        [reduced_row_axes(lagged_input, grad_pre), reduced_row_axes(signal, grad_pre)], axis=0
-    )
+    groups = lax.axis_size("seq")
+    orders = ([0, 2, 3, 1, 4], [0, 2, 1, 3, 4])
+    ring = (4, 8)
+    rows = share_rows(groups, orders, ring)
+
+    def in_share_order(array):
+        step = array.shape[1] // groups
+        return jnp.concatenate([array[:, s * step : (s + 1) * step] for s in rows], axis=1)
+
+    part_out = reduced_row_axes(in_share_order(hidden_state), cotangent)
+    inputs = jnp.concatenate([lagged_input, signal], axis=1)
+    part_taps = reduced_row_axes(in_share_order(inputs), grad_pre)
     part_bias = jnp.sum(grad_pre.astype(jnp.float32), axis=0)
+    part_bias = in_share_order(part_bias[None])[0]
     later_pre = from_behind(grad_pre, ("grp", "seq"), -2)
     tapped_signal = contract_cols(later_pre, w_taps[:width])
     nearby = cotangent.astype(jnp.float32) + contract_cols(grad_pre, w_taps[width:])
     grad_in = (nearby + tapped_signal).astype(jnp.bfloat16)
-    groups = lax.axis_size("seq")
     lanes = 128
     rows_taps = part_taps.shape[0] // groups
     rows_out = part_out.shape[0] // groups
@@ -128,7 +142,7 @@
         ],
         axis=1,
     )
-    mine = halving_scatter(packed, "seq", ([0, 2, 3, 1, 4], [0, 2, 1, 3, 4]), (4, 8))
+    mine = halving_scatter(packed, "seq", orders, ring)
     mine = butterfly_sum(mine, ("grp", "seq"), ([0, 3, 1, 2], [3, 0, 2, 1]), (1, 8), groups)
     grad_taps = mine[:taps_r].reshape(rows_taps, part_taps.shape[1])
     grad_out = mine[taps_r : taps_r + out_r].reshape(rows_out, part_out.shape[1])

time: 118 us -> 135 us (1.14)
  local copies, waits for them, and re-layouts: 6.02 us -> 19.7 us
  other arithmetic: 3.5 us -> 6.53 us
    concatenate x1 -> x6, local copies, waits for them, and re-layouts: 0.01 us -> 12.1 us  [the longest x4 9.73 us: in_share_order(): jnp.concatenate([array[:, s * step:(s + 1) * step] for s in rows], axis=1)]
    slice x0 -> x6, local copies, waits for them, and re-layouts: none -> 3.16 us  [in_share_order(): array[:, s * step:(s + 1) * step]]
    add x4, other arithmetic: 1.61 us -> 3.69 us  [halving_scatter(): buf = keep + lax.ppermute(send, axis, pairs)]
    reshape x3 -> x0, local copies, waits for them, and re-layouts: 1.84 us -> none  [the longest x1 1.71 us: per_device(): part_taps.reshape(groups, taps_r, lanes)]
    concatenate x1, other arithmetic: 0.2 us -> 1.97 us  [per_device(): jnp.concatenate([part_taps.reshape(groups, taps_r, lanes), part_out.resha...]
    dot_general x3 -> x2, matrix products: 0.93 us -> 2.68 us  [reduced_row_axes(): lax.dot_general(left, right, (((0,), (0,)), ((), ())), preferred_element_...]
where the time goes in v7:
time: 135 us; the launch traced here: 134 us
  waiting for transfers between devices  55.9 us (41%)
  starting transfers between devices  43.8 us (32%)
  local copies, waits for them, and re-layouts  19.7 us (15%)
  matrix products  7.08 us (5%)
  other arithmetic  6.53 us (5%)
    ppermute x5, waiting for transfers between devices, halving_scatter(): buf = keep + lax.ppermute(send, axis, pairs)  32.6 us
    ppermute x4, waiting for transfers between devices, butterfly_sum(): array = array + lax.ppermute(array, axes, pairs)  21.1 us
    ppermute x5, starting transfers between devices, halving_scatter(): buf = keep + lax.ppermute(send, axis, pairs)  18.5 us
    ppermute x4, starting transfers between devices, butterfly_sum(): array = array + lax.ppermute(array, axes, pairs)  16.8 us
    concatenate x4, local copies, waits for them, and re-layouts, in_share_order(): jnp.concatenate([array[:, s * step:(s + 1) * step] for s in rows], axis=1)  9.73 us
    ppermute x2, starting transfers between devices, from_behind(): return lax.ppermute(array, axis, pairs)  8.52 us
    add x4, other arithmetic, halving_scatter(): buf = keep + lax.ppermute(send, axis, pairs)  3.69 us
    slice x6, local copies, waits for them, and re-layouts, in_share_order(): array[:, s * step:(s + 1) * step]  3.16 us
  transfers between devices with their start and end apart: 11, of which 9 were waited for; matrix products, arithmetic and copies ran while one was open for 4% of the time, Pallas kernels for 0%

profile of v7, /device:TPU:56, one launch (start us, length us, event | category | flops | bytes accessed | tf_op | source)
XLA Modules:
  0.0 134.2 jit_solution(18345287168142248882)
XLA Ops:
  0.6 0.0 copy-start
  0.6 0.0 copy-start.1
  0.7 0.0 copy-start.3
  0.7 5.1 %collective-permute-start = (bf16[256,256]{1,0:T(8,128)(2,1)}, bf16[256,256]{1,0:T(8,128)(2,1)S(1)}, u32[]{:S(2)}, u32[]{:S(2)}) collective-permute-start(bf16[256,256]{1,0:T(8,128)(2,1)} %param.5), channel_id=1, source_target_pairs={{0,2},{1,3},{2,4},{3,5},{4,6},{5,7},{6,8},{7,9},{8,10},{9,11},{10,... | collective-permute-start | bytes 393224 | tf_op jit(solution)/shard_map/ppermute | solution.py:10
  5.8 1.4 %fusion.9 = f32[256,1024]{1,0:T(8,128)S(1)} fusion(bf16[256,256]{1,0:T(8,128)(2,1)} %param.5, bf16[512,1024]{1,0:T(8,128)(2,1)} %param.7), kind=kOutput, calls=%fused_computation.25 | convolution fusion | flops 134217728 | bytes 1703936 | tf_op jit(solution)/shard_map/dot_general | solution.py:90
  7.2 0.0 copy-start.17
  7.3 1.2 fusion.14
  8.4 2.1 %collective-permute-done = bf16[256,256]{1,0:T(8,128)(2,1)S(1)} collective-permute-done((bf16[256,256]{1,0:T(8,128)(2,1)}, bf16[256,256]{1,0:T(8,128)(2,1)S(1)}, u32[]{:S(2)}, u32[]{:S(2)}) %collective-permute-start) | collective-permute-done | bytes 131104 | tf_op jit(solution)/shard_map/ppermute | solution.py:10
  10.6 0.3 fusion
  10.9 0.4 multiply_convert_fusion.1
  11.4 0.1 convert_reduce_fusion
  11.5 0.1 fusion.17
  11.5 0.1 fusion.16
  11.6 1.1 fusion.13
  12.7 0.4 fusion.12
  13.2 0.1 concatenate.28
  13.3 0.5 broadcast.22
  13.8 0.7 reduce.3
  14.5 0.1 reshape_squeeze.3
  14.6 3.7 %concatenate.26 = bf16[256,512]{1,0:T(8,128)(2,1)S(1)} concatenate(bf16[256,16]{1,0:T(8,128)(2,1)} %get-tuple-element.39, bf16[256,16]{1,0:T(8,128)(2,1)} %get-tuple-element.38, bf16[256,16]{1,0:T(8,128)(2,1)} %get-tuple-element.37, bf16[256,16]{1,0:T(8,128)(2,1)} %get-tuple-element.36, bf16[256,16]{1,0:T(8,128)(2,1)} %get-tuple-element.35, bf16[256,16]{1,0:T(8,128)(2,1)} %get-tuple-element.34, ...), dimensions={1} | concatenate | bytes 524288 | tf_op jit(solution)/shard_map/concatenate | solution.py:118
  18.3 1.3 fusion.18
  19.6 0.8 concatenate.27
  20.4 0.3 fusion.15
  20.9 5.4 %concatenate.24 = bf16[256,512]{1,0:T(8,128)(2,1)} concatenate(bf16[256,16]{1,0:T(8,128)(2,1)S(1)} %get-tuple-element.71, bf16[256,16]{1,0:T(8,128)(2,1)S(1)} %copy-done.15, bf16[256,16]{1,0:T(8,128)(2,1)S(1)} %get-tuple-element.70, bf16[256,16]{1,0:T(8,128)(2,1)S(1)} %copy-done.14, bf16[256,16]{1,0:T(8,128)(2,1)S(1)} %get-tuple-element.69, bf16[256,16]{1,0:T(8,128)(2,1)S(1)} %copy-done.13, ...), dimensions={1} | concatenate | bytes 524288 | tf_op jit(solution)/shard_map/concatenate | solution.py:118
  26.3 1.4 %fusion.11 = f32[512,1024]{1,0:T(8,128)S(1)} fusion(bf16[256,512]{1,0:T(8,128)(2,1)} %concatenate.24, bf16[256,512]{1,0:T(8,128)(2,1)S(1)} %get-tuple-element.6, bf16[256,512]{1,0:T(8,128)(2,1)S(1)} %get-tuple-element.5), kind=kOutput, calls=%fused_computation.35 | convolution fusion | flops 269484032 | bytes 2883584 | tf_op jit(solution)/shard_map/dot_general | solution.py:14
  27.7 1.5 %concatenate.25 = f32[2,16,128,128]{3,2,1,0:T(8,128)} reshape(f32[512,1024]{1,0:T(8,128)S(1)} %fusion.11) | data formatting | bytes 4194304 | tf_op jit(solution)/shard_map/concatenate | solution.py:137
  29.2 2.0 %pad_maximum_fusion = f32[2,16,168,128]{3,2,1,0:T(8,128)S(1)} fusion(f32[2,16,8,128]{3,2,1,0:T(8,128)S(1)} %bitcast.41, f32[2,16,32,128]{3,2,1,0:T(8,128)} %concatenate.27, f32[2,16,128,128]{3,2,1,0:T(8,128)} %concatenate.25), kind=kLoop, calls=%fused_computation | loop fusion | flops 1376256 | bytes 5505024 | tf_op jit(solution)/shard_map/concatenate | solution.py:137
  31.2 1.2 dynamic-slice_bitcast_fusion
  32.4 1.9 %collective-permute-start.2 = (f32[16,168,128]{2,1,0:T(8,128)}, f32[16,168,128]{2,1,0:T(8,128)}, u32[]{:S(2)}, u32[]{:S(2)}) collective-permute-start(f32[16,168,128]{2,1,0:T(8,128)} %dynamic-slice_bitcast_fusion), channel_id=1, source_target_pairs={{0,1},{1,0},{2,3},{3,2},{4,5},{5,4},{6,7},{7,6},{8,9},{9,8},{10,11... | collective-permute-start | bytes 4128776 | tf_op jit(solution)/shard_map/ppermute | solution.py:68
  34.3 3.4 %collective-permute-done.2 = f32[16,168,128]{2,1,0:T(8,128)} collective-permute-done((f32[16,168,128]{2,1,0:T(8,128)}, f32[16,168,128]{2,1,0:T(8,128)}, u32[]{:S(2)}, u32[]{:S(2)}) %collective-permute-start.2) | collective-permute-done | bytes 1376288 | tf_op jit(solution)/shard_map/ppermute | solution.py:68
  37.8 1.5 %bitcast_add_fusion = f32[16,168,128]{2,1,0:T(8,128)S(1)} fusion(f32[16,168,128]{2,1,0:T(8,128)} %collective-permute-done.2, f32[2,16,168,128]{3,2,1,0:T(8,128)S(1)} %pad_maximum_fusion, s32[]{:T(128)S(6)} %select_n.66), kind=kLoop, calls=%fused_computation.1 | loop fusion | flops 344064 | bytes 4128772 | tf_op jit(solution)/shard_map/add | solution.py:68
  39.3 0.0 copy-start.2
  39.3 1.1 copy-done.2
  40.4 3.3 %collective-permute-start.3 = (f32[8,168,128]{2,1,0:T(8,128)S(1)}, f32[8,168,128]{2,1,0:T(8,128)S(1)}, u32[]{:S(2)}, u32[]{:S(2)}) collective-permute-start(f32[8,168,128]{2,1,0:T(8,128)S(1)} %dynamic-slice_bitcast_fusion.1), channel_id=1, source_target_pairs={{0,4},{1,29},{2,6},{3,31},{4,0},{5,9},{6,2},{7,11},{8,12},{9,5},{1... | collective-permute-start | bytes 2064392 | tf_op jit(solution)/shard_map/ppermute | solution.py:68
  43.7 9.5 %collective-permute-done.3 = f32[8,168,128]{2,1,0:T(8,128)S(1)} collective-permute-done((f32[8,168,128]{2,1,0:T(8,128)S(1)}, f32[8,168,128]{2,1,0:T(8,128)S(1)}, u32[]{:S(2)}, u32[]{:S(2)}) %collective-permute-start.3) | collective-permute-done | bytes 688160 | tf_op jit(solution)/shard_map/ppermute | solution.py:68
  53.2 1.2 bitcast_add_fusion.1
  54.4 0.0 copy-start.4
  54.4 0.0 copy-start.18
  54.5 4.7 %collective-permute-start.4 = (f32[4,168,128]{2,1,0:T(8,128)S(1)}, f32[4,168,128]{2,1,0:T(8,128)}, u32[]{:S(2)}, u32[]{:S(2)}) collective-permute-start(f32[4,168,128]{2,1,0:T(8,128)S(1)} %dynamic-slice_bitcast_fusion.2), channel_id=1, source_target_pairs={{0,8},{1,3},{2,10},{3,1},{4,12},{5,7},{6,14},{7,5},{8,0},{9,11},{1... | collective-permute-start | bytes 1032200 | tf_op jit(solution)/shard_map/ppermute | solution.py:68
  59.2 9.2 %collective-permute-done.4 = f32[4,168,128]{2,1,0:T(8,128)} collective-permute-done((f32[4,168,128]{2,1,0:T(8,128)S(1)}, f32[4,168,128]{2,1,0:T(8,128)}, u32[]{:S(2)}, u32[]{:S(2)}) %collective-permute-start.4) | collective-permute-done | bytes 344096 | tf_op jit(solution)/shard_map/ppermute | solution.py:68
  68.4 1.0 bitcast_add_fusion.2
  69.5 4.0 %collective-permute-start.5 = (f32[2,168,128]{2,1,0:T(8,128)S(1)}, f32[2,168,128]{2,1,0:T(8,128)S(1)}, u32[]{:S(2)}, u32[]{:S(2)}) collective-permute-start(f32[2,168,128]{2,1,0:T(8,128)S(1)} %dynamic-slice_bitcast_fusion.3), channel_id=1, source_target_pairs={{0,2},{1,9},{2,0},{3,11},{4,6},{5,29},{6,4},{7,31},{8,10},{9,1},{1... | collective-permute-start | bytes 516104 | tf_op jit(solution)/shard_map/ppermute | solution.py:68
  73.5 4.8 %collective-permute-done.5 = f32[2,168,128]{2,1,0:T(8,128)S(1)} collective-permute-done((f32[2,168,128]{2,1,0:T(8,128)S(1)}, f32[2,168,128]{2,1,0:T(8,128)S(1)}, u32[]{:S(2)}, u32[]{:S(2)}) %collective-permute-start.5) | collective-permute-done | bytes 172064 | tf_op jit(solution)/shard_map/ppermute | solution.py:68
  78.3 4.6 %collective-permute-start.6 = (f32[1,168,128]{2,1,0:T(8,128)S(1)}, f32[1,168,128]{2,1,0:T(8,128)S(1)}, u32[]{:S(2)}, u32[]{:S(2)}) collective-permute-start(f32[1,168,128]{2,1,0:T(8,128)S(1)} %constant_dynamic-slice_fusion), channel_id=1, source_target_pairs={{0,16},{1,17},{2,18},{3,19},{4,20},{5,21},{6,22},{7,23},{8,24},{9,... | collective-permute-start | bytes 258056 | tf_op jit(solution)/shard_map/ppermute | solution.py:68
  82.9 5.7 %collective-permute-done.6 = f32[1,168,128]{2,1,0:T(8,128)S(1)} collective-permute-done((f32[1,168,128]{2,1,0:T(8,128)S(1)}, f32[1,168,128]{2,1,0:T(8,128)S(1)}, u32[]{:S(2)}, u32[]{:S(2)}) %collective-permute-start.6) | collective-permute-done | bytes 86048 | tf_op jit(solution)/shard_map/ppermute | solution.py:68
  88.7 4.3 %collective-permute-start.7 = (f32[168,128]{1,0:T(8,128)S(1)}, f32[168,128]{1,0:T(8,128)S(1)}, u32[]{:S(2)}, u32[]{:S(2)}) collective-permute-start(f32[168,128]{1,0:T(8,128)S(1)} %add_bitcast_fusion), channel_id=1, source_target_pairs={{0,32},{1,257},{2,34},{3,259},{4,36},{5,261},{6,38},{7,263},{8,40}... | collective-permute-start | bytes 258056 | tf_op jit(solution)/shard_map/ppermute | solution.py:83
  92.9 0.0 copy-done.6
  93.0 0.0 copy-done.8
  93.0 0.1 pad_maximum_fusion.1
  93.0 3.5 %collective-permute-start.1 = (bf16[256,1024]{1,0:T(8,128)(2,1)S(1)}, bf16[256,1024]{1,0:T(8,128)(2,1)S(1)}, u32[]{:S(2)}, u32[]{:S(2)}) collective-permute-start(bf16[256,1024]{1,0:T(8,128)(2,1)S(1)} %pad_maximum_fusion.1), channel_id=1, source_target_pairs={{2,0},{3,1},{4,2},{5,3},{6,4},{7,5},{8,6},{9,7},{10,8},{11,9},{12,... | collective-permute-start | bytes 1572872 | tf_op jit(solution)/shard_map/ppermute | solution.py:10
  96.5 0.0 collective-permute-done.7
  96.5 4.9 %collective-permute-start.8 = (f32[168,128]{1,0:T(8,128)S(1)}, f32[168,128]{1,0:T(8,128)S(1)}, u32[]{:S(2)}, u32[]{:S(2)}) collective-permute-start(f32[168,128]{1,0:T(8,128)S(1)} %add.132), channel_id=1, source_target_pairs={{0,256},{1,225},{2,258},{3,227},{4,260},{5,229},{6,262},{7,231},{8... | collective-permute-start | bytes 258056 | tf_op jit(solution)/shard_map/ppermute | solution.py:83
  101.4 0.3 convolution_add_fusion.3
  101.7 12.3 %collective-permute-done.8 = f32[168,128]{1,0:T(8,128)S(1)} collective-permute-done((f32[168,128]{1,0:T(8,128)S(1)}, f32[168,128]{1,0:T(8,128)S(1)}, u32[]{:S(2)}, u32[]{:S(2)}) %collective-permute-start.8) | collective-permute-done | bytes 86048 | tf_op jit(solution)/shard_map/ppermute | solution.py:83
  114.0 1.9 %collective-permute-start.9 = (f32[168,128]{1,0:T(8,128)S(1)}, f32[168,128]{1,0:T(8,128)S(1)}, u32[]{:S(2)}, u32[]{:S(2)}) collective-permute-start(f32[168,128]{1,0:T(8,128)S(1)} %add.133), channel_id=1, source_target_pairs={{0,64},{1,129},{2,66},{3,131},{4,68},{5,133},{6,70},{7,135},{8,72}... | collective-permute-start | bytes 258056 | tf_op jit(solution)/shard_map/ppermute | solution.py:83
  116.0 0.9 fusion.1
  116.8 5.3 %collective-permute-done.9 = f32[168,128]{1,0:T(8,128)S(1)} collective-permute-done((f32[168,128]{1,0:T(8,128)S(1)}, f32[168,128]{1,0:T(8,128)S(1)}, u32[]{:S(2)}, u32[]{:S(2)}) %collective-permute-start.9) | collective-permute-done | bytes 86048 | tf_op jit(solution)/shard_map/ppermute | solution.py:83
  122.1 5.7 %collective-permute-start.10 = (f32[168,128]{1,0:T(8,128)S(1)}, f32[168,128]{1,0:T(8,128)S(1)}, u32[]{:S(2)}, u32[]{:S(2)}) collective-permute-start(f32[168,128]{1,0:T(8,128)S(1)} %add.134), channel_id=1, source_target_pairs={{0,128},{1,65},{2,130},{3,67},{4,132},{5,69},{6,134},{7,71},{8,136... | collective-permute-start | bytes 258056 | tf_op jit(solution)/shard_map/ppermute | solution.py:83
  127.8 0.0 collective-permute-done.1
  127.9 1.0 fusion.2
  128.9 3.6 %collective-permute-done.10 = f32[168,128]{1,0:T(8,128)S(1)} collective-permute-done((f32[168,128]{1,0:T(8,128)S(1)}, f32[168,128]{1,0:T(8,128)S(1)}, u32[]{:S(2)}, u32[]{:S(2)}) %collective-permute-start.10) | collective-permute-done | bytes 86048 | tf_op jit(solution)/shard_map/ppermute | solution.py:83
  132.4 0.5 slice_bitcast_fusion
  133.0 0.6 reshape.42
  133.6 0.6 reshape.43
  (43 shorter events, 0.3 us)
Async XLA Ops:
  0.6 10.2 %copy-start = (bf16[512,256]{1,0:T(8,128)(2,1)S(1)}, bf16[512,256]{1,0:T(8,128)(2,1)}, u32[]{:S(2)}) copy-start(bf16[512,256]{1,0:T(8,128)(2,1)} %param.9) | copy-start | bytes 786436
  0.6 6.6 %copy-start.1 = (bf16[256,256]{1,0:T(8,128)(2,1)S(1)}, bf16[256,256]{1,0:T(8,128)(2,1)}, u32[]{:S(2)}) copy-start(bf16[256,256]{1,0:T(8,128)(2,1)} %param.5) | copy-start | bytes 393220
  0.7 9.9 %copy-start.3 = (bf16[512,1024]{1,0:T(8,128)(2,1)S(1)}, bf16[512,1024]{1,0:T(8,128)(2,1)}, u32[]{:S(2)}) copy-start(bf16[512,1024]{1,0:T(8,128)(2,1)} %param.7) | copy-start | bytes 3145732
  0.7 9.9 %copy-start.19 = (f32[1024]{0:T(1024)S(1)}, f32[1024]{0:T(1024)}, u32[]{:S(2)}) copy-start(f32[1024]{0:T(1024)} %param.8) | copy-start | bytes 12292
  0.7 9.9 %collective-permute-start = (bf16[256,256]{1,0:T(8,128)(2,1)}, bf16[256,256]{1,0:T(8,128)(2,1)S(1)}, u32[]{:S(2)}, u32[]{:S(2)}) collective-permute-start(bf16[256,256]{1,0:T(8,128)(2,1)} %param.5), channel_id=1, source_target_pairs={{0,2},{1,3},{2,4},{3,5},{4,6},{5,7},{6,8},{7,9},{8,10},{9,11},{10,... | collective-permute-start | bytes 393224 | tf_op jit(solution)/shard_map/ppermute | solution.py:10
  7.2 3.6 %copy-start.17 = (bf16[256,256]{1,0:T(8,128)(2,1)S(1)}, bf16[256,256]{1,0:T(8,128)(2,1)}, u32[]{:S(2)}) copy-start(bf16[256,256]{1,0:T(8,128)(2,1)} %param.6) | copy-start | bytes 393220
  11.3 14.9 %copy-start.5 = (bf16[256,512]{1,0:T(8,128)(2,1)}, bf16[256,512]{1,0:T(8,128)(2,1)S(1)}, u32[]{:S(2)}) copy-start(bf16[256,512]{1,0:T(8,128)(2,1)S(1)} %get-tuple-element.5) | copy-start | bytes 786436
  11.4 14.9 %copy-start.7 = (bf16[256,512]{1,0:T(8,128)(2,1)}, bf16[256,512]{1,0:T(8,128)(2,1)S(1)}, u32[]{:S(2)}) copy-start(bf16[256,512]{1,0:T(8,128)(2,1)S(1)} %get-tuple-element.6) | copy-start | bytes 786436
  18.2 2.5 %copy-start.9 = (bf16[256,16]{1,0:T(8,128)(2,1)S(1)}, bf16[256,16]{1,0:T(8,128)(2,1)}, u32[]{:S(2)}) copy-start(bf16[256,16]{1,0:T(8,128)(2,1)} %get-tuple-element.48) | copy-start | bytes 24580
  18.2 2.5 %copy-start.10 = (bf16[256,16]{1,0:T(8,128)(2,1)S(1)}, bf16[256,16]{1,0:T(8,128)(2,1)}, u32[]{:S(2)}) copy-start(bf16[256,16]{1,0:T(8,128)(2,1)} %get-tuple-element.49) | copy-start | bytes 24580
  18.3 2.5 %copy-start.11 = (bf16[256,16]{1,0:T(8,128)(2,1)S(1)}, bf16[256,16]{1,0:T(8,128)(2,1)}, u32[]{:S(2)}) copy-start(bf16[256,16]{1,0:T(8,128)(2,1)} %get-tuple-element.50) | copy-start | bytes 24580
  18.3 2.5 %copy-start.12 = (bf16[256,16]{1,0:T(8,128)(2,1)S(1)}, bf16[256,16]{1,0:T(8,128)(2,1)}, u32[]{:S(2)}) copy-start(bf16[256,16]{1,0:T(8,128)(2,1)} %get-tuple-element.51) | copy-start | bytes 24580
  18.3 2.5 %copy-start.13 = (bf16[256,16]{1,0:T(8,128)(2,1)S(1)}, bf16[256,16]{1,0:T(8,128)(2,1)}, u32[]{:S(2)}) copy-start(bf16[256,16]{1,0:T(8,128)(2,1)} %get-tuple-element.52) | copy-start | bytes 24580
  18.3 2.5 %copy-start.14 = (bf16[256,16]{1,0:T(8,128)(2,1)S(1)}, bf16[256,16]{1,0:T(8,128)(2,1)}, u32[]{:S(2)}) copy-start(bf16[256,16]{1,0:T(8,128)(2,1)} %get-tuple-element.53) | copy-start | bytes 24580
  18.3 2.5 %copy-start.15 = (bf16[256,16]{1,0:T(8,128)(2,1)S(1)}, bf16[256,16]{1,0:T(8,128)(2,1)}, u32[]{:S(2)}) copy-start(bf16[256,16]{1,0:T(8,128)(2,1)} %get-tuple-element.54) | copy-start | bytes 24580
  18.3 2.5 %copy-start.16 = (bf16[256,16]{1,0:T(8,128)(2,1)S(1)}, bf16[256,16]{1,0:T(8,128)(2,1)}, u32[]{:S(2)}) copy-start(bf16[256,16]{1,0:T(8,128)(2,1)} %get-tuple-element.55) | copy-start | bytes 24580
  32.4 5.4 %collective-permute-start.2 = (f32[16,168,128]{2,1,0:T(8,128)}, f32[16,168,128]{2,1,0:T(8,128)}, u32[]{:S(2)}, u32[]{:S(2)}) collective-permute-start(f32[16,168,128]{2,1,0:T(8,128)} %dynamic-slice_bitcast_fusion), channel_id=1, source_target_pairs={{0,1},{1,0},{2,3},{3,2},{4,5},{5,4},{6,7},{7,6},{8,9},{9,8},{10,11... | collective-permute-start | bytes 4128776 | tf_op jit(solution)/shard_map/ppermute | solution.py:68
  39.3 1.1 copy-start.2
  40.4 12.8 %collective-permute-start.3 = (f32[8,168,128]{2,1,0:T(8,128)S(1)}, f32[8,168,128]{2,1,0:T(8,128)S(1)}, u32[]{:S(2)}, u32[]{:S(2)}) collective-permute-start(f32[8,168,128]{2,1,0:T(8,128)S(1)} %dynamic-slice_bitcast_fusion.1), channel_id=1, source_target_pairs={{0,4},{1,29},{2,6},{3,31},{4,0},{5,9},{6,2},{7,11},{8,12},{9,5},{1... | collective-permute-start | bytes 2064392 | tf_op jit(solution)/shard_map/ppermute | solution.py:68
  43.7 49.3 %copy-start.6 = (bf16[256,512]{1,0:T(8,128)(2,1)S(1)}, bf16[256,512]{1,0:T(8,128)(2,1)}, u32[]{:S(2)}) copy-start(bf16[256,512]{1,0:T(8,128)(2,1)} %copy-done.5) | copy-start | bytes 786436
  43.7 49.3 %copy-start.8 = (bf16[256,512]{1,0:T(8,128)(2,1)S(1)}, bf16[256,512]{1,0:T(8,128)(2,1)}, u32[]{:S(2)}) copy-start(bf16[256,512]{1,0:T(8,128)(2,1)} %copy-done.7) | copy-start | bytes 786436
  54.4 47.0 %copy-start.4 = (bf16[512,1024]{1,0:T(8,128)(2,1)S(1)}, bf16[512,1024]{1,0:T(8,128)(2,1)}, u32[]{:S(2)}) copy-start(bf16[512,1024]{1,0:T(8,128)(2,1)} %param.7) | copy-start | bytes 3145732
  54.4 47.0 %copy-start.18 = (bf16[256,256]{1,0:T(8,128)(2,1)S(1)}, bf16[256,256]{1,0:T(8,128)(2,1)}, u32[]{:S(2)}) copy-start(bf16[256,256]{1,0:T(8,128)(2,1)} %param.6) | copy-start | bytes 393220
  54.5 14.0 %collective-permute-start.4 = (f32[4,168,128]{2,1,0:T(8,128)S(1)}, f32[4,168,128]{2,1,0:T(8,128)}, u32[]{:S(2)}, u32[]{:S(2)}) collective-permute-start(f32[4,168,128]{2,1,0:T(8,128)S(1)} %dynamic-slice_bitcast_fusion.2), channel_id=1, source_target_pairs={{0,8},{1,3},{2,10},{3,1},{4,12},{5,7},{6,14},{7,5},{8,0},{9,11},{1... | collective-permute-start | bytes 1032200 | tf_op jit(solution)/shard_map/ppermute | solution.py:68
  69.5 8.8 %collective-permute-start.5 = (f32[2,168,128]{2,1,0:T(8,128)S(1)}, f32[2,168,128]{2,1,0:T(8,128)S(1)}, u32[]{:S(2)}, u32[]{:S(2)}) collective-permute-start(f32[2,168,128]{2,1,0:T(8,128)S(1)} %dynamic-slice_bitcast_fusion.3), channel_id=1, source_target_pairs={{0,2},{1,9},{2,0},{3,11},{4,6},{5,29},{6,4},{7,31},{8,10},{9,1},{1... | collective-permute-start | bytes 516104 | tf_op jit(solution)/shard_map/ppermute | solution.py:68
  78.3 10.3 %collective-permute-start.6 = (f32[1,168,128]{2,1,0:T(8,128)S(1)}, f32[1,168,128]{2,1,0:T(8,128)S(1)}, u32[]{:S(2)}, u32[]{:S(2)}) collective-permute-start(f32[1,168,128]{2,1,0:T(8,128)S(1)} %constant_dynamic-slice_fusion), channel_id=1, source_target_pairs={{0,16},{1,17},{2,18},{3,19},{4,20},{5,21},{6,22},{7,23},{8,24},{9,... | collective-permute-start | bytes 258056 | tf_op jit(solution)/shard_map/ppermute | solution.py:68
  88.7 7.8 %collective-permute-start.7 = (f32[168,128]{1,0:T(8,128)S(1)}, f32[168,128]{1,0:T(8,128)S(1)}, u32[]{:S(2)}, u32[]{:S(2)}) collective-permute-start(f32[168,128]{1,0:T(8,128)S(1)} %add_bitcast_fusion), channel_id=1, source_target_pairs={{0,32},{1,257},{2,34},{3,259},{4,36},{5,261},{6,38},{7,263},{8,40}... | collective-permute-start | bytes 258056 | tf_op jit(solution)/shard_map/ppermute | solution.py:83
  93.0 34.8 %collective-permute-start.1 = (bf16[256,1024]{1,0:T(8,128)(2,1)S(1)}, bf16[256,1024]{1,0:T(8,128)(2,1)S(1)}, u32[]{:S(2)}, u32[]{:S(2)}) collective-permute-start(bf16[256,1024]{1,0:T(8,128)(2,1)S(1)} %pad_maximum_fusion.1), channel_id=1, source_target_pairs={{2,0},{3,1},{4,2},{5,3},{6,4},{7,5},{8,6},{9,7},{10,8},{11,9},{12,... | collective-permute-start | bytes 1572872 | tf_op jit(solution)/shard_map/ppermute | solution.py:10
  96.5 17.5 %collective-permute-start.8 = (f32[168,128]{1,0:T(8,128)S(1)}, f32[168,128]{1,0:T(8,128)S(1)}, u32[]{:S(2)}, u32[]{:S(2)}) collective-permute-start(f32[168,128]{1,0:T(8,128)S(1)} %add.132), channel_id=1, source_target_pairs={{0,256},{1,225},{2,258},{3,227},{4,260},{5,229},{6,262},{7,231},{8... | collective-permute-start | bytes 258056 | tf_op jit(solution)/shard_map/ppermute | solution.py:83
  114.0 8.1 %collective-permute-start.9 = (f32[168,128]{1,0:T(8,128)S(1)}, f32[168,128]{1,0:T(8,128)S(1)}, u32[]{:S(2)}, u32[]{:S(2)}) collective-permute-start(f32[168,128]{1,0:T(8,128)S(1)} %add.133), channel_id=1, source_target_pairs={{0,64},{1,129},{2,66},{3,131},{4,68},{5,133},{6,70},{7,135},{8,72}... | collective-permute-start | bytes 258056 | tf_op jit(solution)/shard_map/ppermute | solution.py:83
  122.1 10.3 %collective-permute-start.10 = (f32[168,128]{1,0:T(8,128)S(1)}, f32[168,128]{1,0:T(8,128)S(1)}, u32[]{:S(2)}, u32[]{:S(2)}) collective-permute-start(f32[168,128]{1,0:T(8,128)S(1)} %add.134), channel_id=1, source_target_pairs={{0,128},{1,65},{2,130},{3,67},{4,132},{5,69},{6,134},{7,71},{8,136... | collective-permute-start | bytes 258056 | tf_op jit(solution)/shard_map/ppermute | solution.py:83

commit v8 on v5

--- a/solution.py
+++ b/solution.py
@@ -108,9 +108,6 @@
     )
     part_bias = jnp.sum(grad_pre.astype(jnp.float32), axis=0)
     later_pre = from_behind(grad_pre, ("grp", "seq"), -2)
-    tapped_signal = contract_cols(later_pre, w_taps[:width])
-    nearby = cotangent.astype(jnp.float32) + contract_cols(grad_pre, w_taps[width:])
-    grad_in = (nearby + tapped_signal).astype(jnp.bfloat16)
     groups = lax.axis_size("seq")
     lanes = 128
     rows_taps = part_taps.shape[0] // groups
@@ -128,6 +125,10 @@
         ],
         axis=1,
     )
+    later_pre, packed = lax.optimization_barrier((later_pre, packed))
+    tapped_signal = contract_cols(later_pre, w_taps[:width])
+    nearby = cotangent.astype(jnp.float32) + contract_cols(grad_pre, w_taps[width:])
+    grad_in = (nearby + tapped_signal).astype(jnp.bfloat16)
     mine = halving_scatter(packed, "seq", ([0, 2, 3, 1, 4], [0, 2, 1, 3, 4]), (4, 8))
     mine = butterfly_sum(mine, ("grp", "seq"), ([0, 3, 1, 2], [3, 0, 2, 1]), (1, 8), groups)
     grad_taps = mine[:taps_r].reshape(rows_taps, part_taps.shape[1])

time: 118 us -> 128 us (1.085)
  the two profiles are of different devices: /device:TPU:56 before, /device:TPU:2 now
where the time goes in v8:
time: 128 us; the launch traced here: 127 us
  waiting for transfers between devices  73.6 us (57%)
  starting transfers between devices  31.8 us (25%)
  matrix products  8.47 us (7%)
  local copies, waits for them, and re-layouts  6.52 us (5%)
  other arithmetic  5.27 us (4%)
  between operations  1.32 us (1%)
    ppermute x5, waiting for transfers between devices, halving_scatter(): buf = keep + lax.ppermute(send, axis, pairs)  40.5 us
    ppermute x2, waiting for transfers between devices, from_behind(): return lax.ppermute(array, axis, pairs)  19.5 us
    ppermute x4, waiting for transfers between devices, butterfly_sum(): array = array + lax.ppermute(array, axes, pairs)  13.6 us
    ppermute x4, starting transfers between devices, butterfly_sum(): array = array + lax.ppermute(array, axes, pairs)  12.7 us
    ppermute x5, starting transfers between devices, halving_scatter(): buf = keep + lax.ppermute(send, axis, pairs)  9.74 us
    ppermute x2, starting transfers between devices, from_behind(): return lax.ppermute(array, axis, pairs)  9.32 us
    dot_general x3, matrix products, contract_cols(): lax.dot_general(left, right, (((1,), (1,)), ((), ())), preferred_element_...  3.89 us
    add x4, other arithmetic, halving_scatter(): buf = keep + lax.ppermute(send, axis, pairs)  2.59 us
  transfers between devices with their start and end apart: 11, of which 11 were waited for; matrix products, arithmetic and copies ran while one was open for 8% of the time, Pallas kernels for 0%

profile of v8, /device:TPU:2, one launch (start us, length us, event | category | flops | bytes accessed | tf_op | source)
XLA Modules:
  0.0 127.0 jit_solution(4494020958194160671)
XLA Ops:
  0.6 0.0 copy-start
  0.6 0.0 copy-start.8
  0.7 4.2 %collective-permute-start = (bf16[256,256]{1,0:T(8,128)(2,1)}, bf16[256,256]{1,0:T(8,128)(2,1)S(1)}, u32[]{:S(2)}, u32[]{:S(2)}) collective-permute-start(bf16[256,256]{1,0:T(8,128)(2,1)} %param.5), channel_id=1, source_target_pairs={{0,2},{1,3},{2,4},{3,5},{4,6},{5,7},{6,8},{7,9},{8,10},{9,11},{10,... | collective-permute-start | bytes 393224 | tf_op jit(solution)/shard_map/ppermute | solution.py:10
  4.8 1.4 %fusion.9 = f32[256,1024]{1,0:T(8,128)S(1)} fusion(bf16[256,256]{1,0:T(8,128)(2,1)} %param.5, bf16[512,1024]{1,0:T(8,128)(2,1)} %param.7), kind=kOutput, calls=%fused_computation.28 | convolution fusion | flops 134217728 | bytes 1703936 | tf_op jit(solution)/shard_map/dot_general | solution.py:84
  6.3 13.0 %collective-permute-done = bf16[256,256]{1,0:T(8,128)(2,1)S(1)} collective-permute-done((bf16[256,256]{1,0:T(8,128)(2,1)}, bf16[256,256]{1,0:T(8,128)(2,1)S(1)}, u32[]{:S(2)}, u32[]{:S(2)}) %collective-permute-start) | collective-permute-done | bytes 131104 | tf_op jit(solution)/shard_map/ppermute | solution.py:10
  19.3 1.3 %fusion = f32[256,1024]{1,0:T(8,128)S(1)} fusion(f32[256,1024]{1,0:T(8,128)S(1)} %fusion.9, bf16[256,256]{1,0:T(8,128)(2,1)S(1)} %collective-permute-done, f32[1024]{0:T(1024)} %param.8, bf16[512,1024]{1,0:T(8,128)(2,1)} %param.7), kind=kOutput, calls=%fused_computation.7 | convolution fusion | flops 134742016 | bytes 2756608 | tf_op jit(solution)/shard_map/dot_general | solution.py:87
  20.6 0.0 copy-done
  20.6 0.0 copy-done.8
  20.6 0.0 copy-start.4
  20.7 0.4 multiply_convert_fusion.1
  21.1 0.0 copy-start.6
  21.1 0.0 copy-start.9
  21.1 0.9 pad_maximum_fusion.2
  22.0 0.0 copy-done.4
  22.0 0.3 convolution_bitcast_fusion
  22.4 5.2 %collective-permute-start.1 = (bf16[256,1024]{1,0:T(8,128)(2,1)}, bf16[256,1024]{1,0:T(8,128)(2,1)}, u32[]{:S(2)}, u32[]{:S(2)}) collective-permute-start(bf16[256,1024]{1,0:T(8,128)(2,1)} %pad_maximum_fusion.2), channel_id=1, source_target_pairs={{2,0},{3,1},{4,2},{5,3},{6,4},{7,5},{8,6},{9,7},{10,8},{11,9},{12,... | collective-permute-start | bytes 1572872 | tf_op jit(solution)/shard_map/ppermute | solution.py:10
  27.5 0.3 convolution_bitcast_fusion.1
  27.9 0.0 copy-done.6
  27.9 0.0 copy-done.9
  27.9 0.3 fusion.11
  28.1 0.1 convert_reduce_fusion
  28.2 0.1 reshape.45
  28.3 0.8 reshape.44
  29.2 1.4 %pad_maximum_fusion.1 = f32[512,1024]{1,0:T(8,128)} fusion(f32[256,1024]{1,0:T(8,128)S(1)} %convolution_bitcast_fusion, f32[256,1024]{1,0:T(8,128)S(1)} %convolution_bitcast_fusion.1), kind=kLoop, calls=%fused_computation.1 | loop fusion | flops 524288 | bytes 4194304 | tf_op jit(solution)/shard_map/concatenate | solution.py:106
  30.6 1.8 %reshape.43 = f32[32,128,128]{2,1,0:T(8,128)S(1)} reshape(f32[512,1024]{1,0:T(8,128)} %pad_maximum_fusion.1) | data formatting | bytes 4194304 | tf_op jit(solution)/shard_map/reshape | solution.py:122
  32.4 0.0 copy-done.3
  32.4 0.2 pad_maximum_fusion
  32.6 6.5 %collective-permute-done.1 = bf16[256,1024]{1,0:T(8,128)(2,1)} collective-permute-done((bf16[256,1024]{1,0:T(8,128)(2,1)}, bf16[256,1024]{1,0:T(8,128)(2,1)}, u32[]{:S(2)}, u32[]{:S(2)}) %collective-permute-start.1) | collective-permute-done | bytes 524320 | tf_op jit(solution)/shard_map/ppermute | solution.py:10
  39.7 0.0 copy-start.1
  39.7 1.5 %copy-done.1 = f32[32,168,128]{2,1,0:T(8,128)} copy-done((f32[32,168,128]{2,1,0:T(8,128)}, f32[32,168,128]{2,1,0:T(8,128)S(1)}, u32[]{:S(2)}) %copy-start.1) | copy-done | bytes 2752536
  41.2 0.1 dynamic-slice_bitcast_fusion
  41.3 1.9 %collective-permute-start.2 = (f32[16,168,128]{2,1,0:T(8,128)S(1)}, f32[16,168,128]{2,1,0:T(8,128)S(1)}, u32[]{:S(2)}, u32[]{:S(2)}) collective-permute-start(f32[16,168,128]{2,1,0:T(8,128)S(1)} %dynamic-slice_bitcast_fusion), channel_id=1, source_target_pairs={{0,1},{1,0},{2,3},{3,2},{4,5},{5,4},{6,7},{7,6},{8,9},{9,8},{10,11... | collective-permute-start | bytes 4128776 | tf_op jit(solution)/shard_map/ppermute | solution.py:62
  43.2 3.1 %collective-permute-done.2 = f32[16,168,128]{2,1,0:T(8,128)S(1)} collective-permute-done((f32[16,168,128]{2,1,0:T(8,128)S(1)}, f32[16,168,128]{2,1,0:T(8,128)S(1)}, u32[]{:S(2)}, u32[]{:S(2)}) %collective-permute-start.2) | collective-permute-done | bytes 1376288 | tf_op jit(solution)/shard_map/ppermute | solution.py:62
  46.3 1.5 %bitcast_add_fusion = f32[16,168,128]{2,1,0:T(8,128)S(1)} fusion(f32[16,168,128]{2,1,0:T(8,128)S(1)} %collective-permute-done.2, f32[2,16,168,128]{3,2,1,0:T(8,128)} %bitcast.42, s32[]{:T(128)S(6)} %select_n.66), kind=kLoop, calls=%fused_computation.2 | loop fusion | flops 344064 | bytes 4128772 | tf_op jit(solution)/shard_map/add | solution.py:62
  47.8 0.1 dynamic-slice_bitcast_fusion.1
  47.8 1.9 %collective-permute-start.3 = (f32[8,168,128]{2,1,0:T(8,128)S(1)}, f32[8,168,128]{2,1,0:T(8,128)S(1)}, u32[]{:S(2)}, u32[]{:S(2)}) collective-permute-start(f32[8,168,128]{2,1,0:T(8,128)S(1)} %dynamic-slice_bitcast_fusion.1), channel_id=1, source_target_pairs={{0,4},{1,29},{2,6},{3,31},{4,0},{5,9},{6,2},{7,11},{8,12},{9,5},{1... | collective-permute-start | bytes 2064392 | tf_op jit(solution)/shard_map/ppermute | solution.py:62
  49.8 10.9 %collective-permute-done.3 = f32[8,168,128]{2,1,0:T(8,128)S(1)} collective-permute-done((f32[8,168,128]{2,1,0:T(8,128)S(1)}, f32[8,168,128]{2,1,0:T(8,128)S(1)}, u32[]{:S(2)}, u32[]{:S(2)}) %collective-permute-start.3) | collective-permute-done | bytes 688160 | tf_op jit(solution)/shard_map/ppermute | solution.py:62
  60.7 0.1 bitcast_add_fusion.1
  60.8 0.0 copy-start.5
  60.8 0.0 copy-start.7
  60.8 2.1 %collective-permute-start.4 = (f32[4,168,128]{2,1,0:T(8,128)S(1)}, f32[4,168,128]{2,1,0:T(8,128)}, u32[]{:S(2)}, u32[]{:S(2)}) collective-permute-start(f32[4,168,128]{2,1,0:T(8,128)S(1)} %dynamic-slice_bitcast_fusion.2), channel_id=1, source_target_pairs={{0,8},{1,3},{2,10},{3,1},{4,12},{5,7},{6,14},{7,5},{8,0},{9,11},{1... | collective-permute-start | bytes 1032200 | tf_op jit(solution)/shard_map/ppermute | solution.py:62
  62.9 0.0 copy-start.2
  62.9 11.3 %collective-permute-done.4 = f32[4,168,128]{2,1,0:T(8,128)} collective-permute-done((f32[4,168,128]{2,1,0:T(8,128)S(1)}, f32[4,168,128]{2,1,0:T(8,128)}, u32[]{:S(2)}, u32[]{:S(2)}) %collective-permute-start.4) | collective-permute-done | bytes 344096 | tf_op jit(solution)/shard_map/ppermute | solution.py:62
  74.2 1.0 bitcast_add_fusion.2
  75.3 1.9 %collective-permute-start.5 = (f32[2,168,128]{2,1,0:T(8,128)S(1)}, f32[2,168,128]{2,1,0:T(8,128)S(1)}, u32[]{:S(2)}, u32[]{:S(2)}) collective-permute-start(f32[2,168,128]{2,1,0:T(8,128)S(1)} %dynamic-slice_bitcast_fusion.3), channel_id=1, source_target_pairs={{0,2},{1,9},{2,0},{3,11},{4,6},{5,29},{6,4},{7,31},{8,10},{9,1},{1... | collective-permute-start | bytes 516104 | tf_op jit(solution)/shard_map/ppermute | solution.py:62
  77.2 6.9 %collective-permute-done.5 = f32[2,168,128]{2,1,0:T(8,128)S(1)} collective-permute-done((f32[2,168,128]{2,1,0:T(8,128)S(1)}, f32[2,168,128]{2,1,0:T(8,128)S(1)}, u32[]{:S(2)}, u32[]{:S(2)}) %collective-permute-start.5) | collective-permute-done | bytes 172064 | tf_op jit(solution)/shard_map/ppermute | solution.py:62
  84.1 1.9 %collective-permute-start.6 = (f32[1,168,128]{2,1,0:T(8,128)S(1)}, f32[1,168,128]{2,1,0:T(8,128)S(1)}, u32[]{:S(2)}, u32[]{:S(2)}) collective-permute-start(f32[1,168,128]{2,1,0:T(8,128)S(1)} %constant_dynamic-slice_fusion), channel_id=1, source_target_pairs={{0,16},{1,17},{2,18},{3,19},{4,20},{5,21},{6,22},{7,23},{8,24},{9,... | collective-permute-start | bytes 258056 | tf_op jit(solution)/shard_map/ppermute | solution.py:62
  86.1 8.4 %collective-permute-done.6 = f32[1,168,128]{2,1,0:T(8,128)S(1)} collective-permute-done((f32[1,168,128]{2,1,0:T(8,128)S(1)}, f32[1,168,128]{2,1,0:T(8,128)S(1)}, u32[]{:S(2)}, u32[]{:S(2)}) %collective-permute-start.6) | collective-permute-done | bytes 86048 | tf_op jit(solution)/shard_map/ppermute | solution.py:62
  94.4 1.9 %collective-permute-start.7 = (f32[168,128]{1,0:T(8,128)S(1)}, f32[168,128]{1,0:T(8,128)S(1)}, u32[]{:S(2)}, u32[]{:S(2)}) collective-permute-start(f32[168,128]{1,0:T(8,128)S(1)} %add_bitcast_fusion), channel_id=1, source_target_pairs={{0,32},{1,257},{2,34},{3,259},{4,36},{5,261},{6,38},{7,263},{8,40}... | collective-permute-start | bytes 258056 | tf_op jit(solution)/shard_map/ppermute | solution.py:77
  96.4 4.5 %collective-permute-done.7 = f32[168,128]{1,0:T(8,128)S(1)} collective-permute-done((f32[168,128]{1,0:T(8,128)S(1)}, f32[168,128]{1,0:T(8,128)S(1)}, u32[]{:S(2)}, u32[]{:S(2)}) %collective-permute-start.7) | collective-permute-done | bytes 86048 | tf_op jit(solution)/shard_map/ppermute | solution.py:77
  100.8 1.9 %collective-permute-start.8 = (f32[168,128]{1,0:T(8,128)S(1)}, f32[168,128]{1,0:T(8,128)S(1)}, u32[]{:S(2)}, u32[]{:S(2)}) collective-permute-start(f32[168,128]{1,0:T(8,128)S(1)} %add.132), channel_id=1, source_target_pairs={{0,256},{1,225},{2,258},{3,227},{4,260},{5,229},{6,262},{7,231},{8... | collective-permute-start | bytes 258056 | tf_op jit(solution)/shard_map/ppermute | solution.py:77
  102.8 1.4 %convolution_add_fusion.3 = f32[256,256]{1,0:T(8,128)S(1)} fusion(bf16[512,1024]{1,0:T(8,128)(2,1)} %param.7, bf16[256,256]{1,0:T(8,128)(2,1)} %param.6, bf16[256,512]{1,0:T(8,128)(2,1)S(1)} %get-tuple-element.10, bf16[256,512]{1,0:T(8,128)(2,1)S(1)} %get-tuple-element.9), kind=kOutput, calls=%fused_computation.10 | convolution fusion | flops 135397376 | bytes 1441792 | tf_op jit(solution)/shard_map/dot_general | solution.py:20
  104.2 3.0 %collective-permute-done.8 = f32[168,128]{1,0:T(8,128)S(1)} collective-permute-done((f32[168,128]{1,0:T(8,128)S(1)}, f32[168,128]{1,0:T(8,128)S(1)}, u32[]{:S(2)}, u32[]{:S(2)}) %collective-permute-start.8) | collective-permute-done | bytes 86048 | tf_op jit(solution)/shard_map/ppermute | solution.py:77
  107.2 1.9 %collective-permute-start.9 = (f32[168,128]{1,0:T(8,128)S(1)}, f32[168,128]{1,0:T(8,128)S(1)}, u32[]{:S(2)}, u32[]{:S(2)}) collective-permute-start(f32[168,128]{1,0:T(8,128)S(1)} %add.133), channel_id=1, source_target_pairs={{0,64},{1,129},{2,66},{3,131},{4,68},{5,133},{6,70},{7,135},{8,72}... | collective-permute-start | bytes 258056 | tf_op jit(solution)/shard_map/ppermute | solution.py:77
  109.2 0.0 copy-done.5
  109.2 0.0 copy-done.7
  109.2 0.9 fusion.1
  110.1 4.8 %collective-permute-done.9 = f32[168,128]{1,0:T(8,128)S(1)} collective-permute-done((f32[168,128]{1,0:T(8,128)S(1)}, f32[168,128]{1,0:T(8,128)S(1)}, u32[]{:S(2)}, u32[]{:S(2)}) %collective-permute-start.9) | collective-permute-done | bytes 86048 | tf_op jit(solution)/shard_map/ppermute | solution.py:77
  114.9 7.0 %collective-permute-start.10 = (f32[168,128]{1,0:T(8,128)S(1)}, f32[168,128]{1,0:T(8,128)S(1)}, u32[]{:S(2)}, u32[]{:S(2)}) collective-permute-start(f32[168,128]{1,0:T(8,128)S(1)} %add.134), channel_id=1, source_target_pairs={{0,128},{1,65},{2,130},{3,67},{4,132},{5,69},{6,134},{7,71},{8,136... | collective-permute-start | bytes 258056 | tf_op jit(solution)/shard_map/ppermute | solution.py:77
  121.9 2.0 %fusion.2 = bf16[256,256]{1,0:T(8,128)(2,1)} fusion(f32[256,256]{1,0:T(8,128)S(1)} %convolution_add_fusion.3, bf16[256,1024]{1,0:T(8,128)(2,1)} %collective-permute-done.1, bf16[512,1024]{1,0:T(8,128)(2,1)S(1)} %copy-done.2), kind=kOutput, calls=%fused_computation.12 | convolution fusion | flops 134348800 | bytes 1441792 | tf_op jit(solution)/shard_map/dot_general | solution.py:20
  123.9 1.3 %collective-permute-done.10 = f32[168,128]{1,0:T(8,128)S(1)} collective-permute-done((f32[168,128]{1,0:T(8,128)S(1)}, f32[168,128]{1,0:T(8,128)S(1)}, u32[]{:S(2)}, u32[]{:S(2)}) %collective-permute-start.10) | collective-permute-done | bytes 86048 | tf_op jit(solution)/shard_map/ppermute | solution.py:77
  125.2 0.5 slice_bitcast_fusion
  125.7 0.6 reshape.50
  126.4 0.6 reshape.51
  (46 shorter events, 0.5 us)
Async XLA Ops:
  0.6 20.0 %copy-start = (bf16[512,256]{1,0:T(8,128)(2,1)S(1)}, bf16[512,256]{1,0:T(8,128)(2,1)}, u32[]{:S(2)}) copy-start(bf16[512,256]{1,0:T(8,128)(2,1)} %param.9) | copy-start | bytes 786436
  0.6 20.0 %copy-start.8 = (bf16[256,256]{1,0:T(8,128)(2,1)S(1)}, bf16[256,256]{1,0:T(8,128)(2,1)}, u32[]{:S(2)}) copy-start(bf16[256,256]{1,0:T(8,128)(2,1)} %param.6) | copy-start | bytes 393220
  0.7 18.6 %collective-permute-start = (bf16[256,256]{1,0:T(8,128)(2,1)}, bf16[256,256]{1,0:T(8,128)(2,1)S(1)}, u32[]{:S(2)}, u32[]{:S(2)}) collective-permute-start(bf16[256,256]{1,0:T(8,128)(2,1)} %param.5), channel_id=1, source_target_pairs={{0,2},{1,3},{2,4},{3,5},{4,6},{5,7},{6,8},{7,9},{8,10},{9,11},{10,... | collective-permute-start | bytes 393224 | tf_op jit(solution)/shard_map/ppermute | solution.py:10
  20.6 1.4 %copy-start.4 = (bf16[256,256]{1,0:T(8,128)(2,1)S(1)}, bf16[256,256]{1,0:T(8,128)(2,1)}, u32[]{:S(2)}) copy-start(bf16[256,256]{1,0:T(8,128)(2,1)} %param.5) | copy-start | bytes 393220
  21.1 6.7 %copy-start.6 = (bf16[256,512]{1,0:T(8,128)(2,1)}, bf16[256,512]{1,0:T(8,128)(2,1)S(1)}, u32[]{:S(2)}) copy-start(bf16[256,512]{1,0:T(8,128)(2,1)S(1)} %get-tuple-element.11) | copy-start | bytes 786436
  21.1 6.7 %copy-start.9 = (bf16[256,256]{1,0:T(8,128)(2,1)S(1)}, bf16[256,256]{1,0:T(8,128)(2,1)}, u32[]{:S(2)}) copy-start(bf16[256,256]{1,0:T(8,128)(2,1)} %param.6) | copy-start | bytes 393220
  22.4 16.8 %collective-permute-start.1 = (bf16[256,1024]{1,0:T(8,128)(2,1)}, bf16[256,1024]{1,0:T(8,128)(2,1)}, u32[]{:S(2)}, u32[]{:S(2)}) collective-permute-start(bf16[256,1024]{1,0:T(8,128)(2,1)} %pad_maximum_fusion.2), channel_id=1, source_target_pairs={{2,0},{3,1},{4,2},{5,3},{6,4},{7,5},{8,6},{9,7},{10,8},{11,9},{12,... | collective-permute-start | bytes 1572872 | tf_op jit(solution)/shard_map/ppermute | solution.py:10
  30.6 1.8 %copy-start.3 = (f32[32,32,128]{2,1,0:T(8,128)S(1)}, f32[32,32,128]{2,1,0:T(8,128)}, u32[]{:S(2)}) copy-start(f32[32,32,128]{2,1,0:T(8,128)} %reshape.44) | copy-start | bytes 1572868
  39.7 1.5 %copy-start.1 = (f32[32,168,128]{2,1,0:T(8,128)}, f32[32,168,128]{2,1,0:T(8,128)S(1)}, u32[]{:S(2)}) copy-start(f32[32,168,128]{2,1,0:T(8,128)S(1)} %slice_dynamic-update-slice_fusion) | copy-start | bytes 8257540
  41.3 5.0 %collective-permute-start.2 = (f32[16,168,128]{2,1,0:T(8,128)S(1)}, f32[16,168,128]{2,1,0:T(8,128)S(1)}, u32[]{:S(2)}, u32[]{:S(2)}) collective-permute-start(f32[16,168,128]{2,1,0:T(8,128)S(1)} %dynamic-slice_bitcast_fusion), channel_id=1, source_target_pairs={{0,1},{1,0},{2,3},{3,2},{4,5},{5,4},{6,7},{7,6},{8,9},{9,8},{10,11... | collective-permute-start | bytes 4128776 | tf_op jit(solution)/shard_map/ppermute | solution.py:62
  47.8 12.8 %collective-permute-start.3 = (f32[8,168,128]{2,1,0:T(8,128)S(1)}, f32[8,168,128]{2,1,0:T(8,128)S(1)}, u32[]{:S(2)}, u32[]{:S(2)}) collective-permute-start(f32[8,168,128]{2,1,0:T(8,128)S(1)} %dynamic-slice_bitcast_fusion.1), channel_id=1, source_target_pairs={{0,4},{1,29},{2,6},{3,31},{4,0},{5,9},{6,2},{7,11},{8,12},{9,5},{1... | collective-permute-start | bytes 2064392 | tf_op jit(solution)/shard_map/ppermute | solution.py:62
  60.8 48.4 %copy-start.5 = (bf16[256,256]{1,0:T(8,128)(2,1)S(1)}, bf16[256,256]{1,0:T(8,128)(2,1)}, u32[]{:S(2)}) copy-start(bf16[256,256]{1,0:T(8,128)(2,1)} %param.5) | copy-start | bytes 393220
  60.8 48.4 %copy-start.7 = (bf16[256,512]{1,0:T(8,128)(2,1)S(1)}, bf16[256,512]{1,0:T(8,128)(2,1)}, u32[]{:S(2)}) copy-start(bf16[256,512]{1,0:T(8,128)(2,1)} %copy-done.6) | copy-start | bytes 786436
  60.8 13.4 %collective-permute-start.4 = (f32[4,168,128]{2,1,0:T(8,128)S(1)}, f32[4,168,128]{2,1,0:T(8,128)}, u32[]{:S(2)}, u32[]{:S(2)}) collective-permute-start(f32[4,168,128]{2,1,0:T(8,128)S(1)} %dynamic-slice_bitcast_fusion.2), channel_id=1, source_target_pairs={{0,8},{1,3},{2,10},{3,1},{4,12},{5,7},{6,14},{7,5},{8,0},{9,11},{1... | collective-permute-start | bytes 1032200 | tf_op jit(solution)/shard_map/ppermute | solution.py:62
  62.9 59.0 %copy-start.2 = (bf16[512,1024]{1,0:T(8,128)(2,1)S(1)}, bf16[512,1024]{1,0:T(8,128)(2,1)}, u32[]{:S(2)}) copy-start(bf16[512,1024]{1,0:T(8,128)(2,1)} %param.7) | copy-start | bytes 3145732
  75.3 8.8 %collective-permute-start.5 = (f32[2,168,128]{2,1,0:T(8,128)S(1)}, f32[2,168,128]{2,1,0:T(8,128)S(1)}, u32[]{:S(2)}, u32[]{:S(2)}) collective-permute-start(f32[2,168,128]{2,1,0:T(8,128)S(1)} %dynamic-slice_bitcast_fusion.3), channel_id=1, source_target_pairs={{0,2},{1,9},{2,0},{3,11},{4,6},{5,29},{6,4},{7,31},{8,10},{9,1},{1... | collective-permute-start | bytes 516104 | tf_op jit(solution)/shard_map/ppermute | solution.py:62
  84.1 10.3 %collective-permute-start.6 = (f32[1,168,128]{2,1,0:T(8,128)S(1)}, f32[1,168,128]{2,1,0:T(8,128)S(1)}, u32[]{:S(2)}, u32[]{:S(2)}) collective-permute-start(f32[1,168,128]{2,1,0:T(8,128)S(1)} %constant_dynamic-slice_fusion), channel_id=1, source_target_pairs={{0,16},{1,17},{2,18},{3,19},{4,20},{5,21},{6,22},{7,23},{8,24},{9,... | collective-permute-start | bytes 258056 | tf_op jit(solution)/shard_map/ppermute | solution.py:62
  94.4 6.4 %collective-permute-start.7 = (f32[168,128]{1,0:T(8,128)S(1)}, f32[168,128]{1,0:T(8,128)S(1)}, u32[]{:S(2)}, u32[]{:S(2)}) collective-permute-start(f32[168,128]{1,0:T(8,128)S(1)} %add_bitcast_fusion), channel_id=1, source_target_pairs={{0,32},{1,257},{2,34},{3,259},{4,36},{5,261},{6,38},{7,263},{8,40}... | collective-permute-start | bytes 258056 | tf_op jit(solution)/shard_map/ppermute | solution.py:77
  100.8 6.4 %collective-permute-start.8 = (f32[168,128]{1,0:T(8,128)S(1)}, f32[168,128]{1,0:T(8,128)S(1)}, u32[]{:S(2)}, u32[]{:S(2)}) collective-permute-start(f32[168,128]{1,0:T(8,128)S(1)} %add.132), channel_id=1, source_target_pairs={{0,256},{1,225},{2,258},{3,227},{4,260},{5,229},{6,262},{7,231},{8... | collective-permute-start | bytes 258056 | tf_op jit(solution)/shard_map/ppermute | solution.py:77
  107.2 7.6 %collective-permute-start.9 = (f32[168,128]{1,0:T(8,128)S(1)}, f32[168,128]{1,0:T(8,128)S(1)}, u32[]{:S(2)}, u32[]{:S(2)}) collective-permute-start(f32[168,128]{1,0:T(8,128)S(1)} %add.133), channel_id=1, source_target_pairs={{0,64},{1,129},{2,66},{3,131},{4,68},{5,133},{6,70},{7,135},{8,72}... | collective-permute-start | bytes 258056 | tf_op jit(solution)/shard_map/ppermute | solution.py:77
  114.9 10.3 %collective-permute-start.10 = (f32[168,128]{1,0:T(8,128)S(1)}, f32[168,128]{1,0:T(8,128)S(1)}, u32[]{:S(2)}, u32[]{:S(2)}) collective-permute-start(f32[168,128]{1,0:T(8,128)S(1)} %add.134), channel_id=1, source_target_pairs={{0,128},{1,65},{2,130},{3,67},{4,132},{5,69},{6,134},{7,71},{8,136... | collective-permute-start | bytes 258056 | tf_op jit(solution)/shard_map/ppermute | solution.py:77

commit v9 on v5

--- a/solution.py
+++ b/solution.py
@@ -44,7 +44,7 @@
             for t, b in enumerate(order[1:]):
                 v |= ((p >> (bits - 2 - t)) & 1) << b
             rows.append(unlabel(v, rotate, size) if c else v)
-    buf = jnp.concatenate([shares[s : s + 1] for s in rows])
+    buf = jnp.take(shares, jnp.array(rows, jnp.int32), axis=0)
     core = where & 1
     mine = jnp.where(core == 1, relabel(where, rotate, size), where)
     for step in range(bits):

time: 118 us -> 124 us (1.051)
  other arithmetic: 3.5 us -> 6.81 us
  local copies, waits for them, and re-layouts: 6.02 us -> 8.87 us
    gather x0 -> x1, local copies, waits for them, and re-layouts: none -> 2.5 us  [halving_scatter(): buf = jnp.take(shares, jnp.array(rows, jnp.int32), axis=0)]
    concatenate x1, other arithmetic: 0.2 us -> 1.75 us  [per_device(): jnp.concatenate([part_taps.reshape(groups, taps_r, lanes), part_out.resha...]
where the time goes in v9:
time: 124 us; the launch traced here: 123 us
  waiting for transfers between devices  54.5 us (44%)
  starting transfers between devices  44.7 us (36%)
  local copies, waits for them, and re-layouts  8.87 us (7%)
  matrix products  6.91 us (6%)
  other arithmetic  6.81 us (5%)
    ppermute x5, waiting for transfers between devices, halving_scatter(): buf = keep + lax.ppermute(send, axis, pairs)  32.5 us
    ppermute x4, waiting for transfers between devices, butterfly_sum(): array = array + lax.ppermute(array, axes, pairs)  19.3 us
    ppermute x5, starting transfers between devices, halving_scatter(): buf = keep + lax.ppermute(send, axis, pairs)  18.5 us
    ppermute x4, starting transfers between devices, butterfly_sum(): array = array + lax.ppermute(array, axes, pairs)  17.5 us
    ppermute x2, starting transfers between devices, from_behind(): return lax.ppermute(array, axis, pairs)  8.63 us
    add x4, other arithmetic, halving_scatter(): buf = keep + lax.ppermute(send, axis, pairs)  2.71 us
    dot_general x3, matrix products, contract_cols(): lax.dot_general(left, right, (((1,), (1,)), ((), ())), preferred_element_...  2.69 us
    ppermute x2, waiting for transfers between devices, from_behind(): return lax.ppermute(array, axis, pairs)  2.67 us
  transfers between devices with their start and end apart: 11, of which 9 were waited for; matrix products, arithmetic and copies ran while one was open for 4% of the time, Pallas kernels for 0%

profile of v9, /device:TPU:56, one launch (start us, length us, event | category | flops | bytes accessed | tf_op | source)
XLA Modules:
  0.0 122.9 jit_solution(18034453728481076981)
XLA Ops:
  0.6 0.0 copy-start
  0.6 0.0 copy-start.2
  0.7 0.0 copy-start.10
  0.7 5.1 %collective-permute-start = (bf16[256,256]{1,0:T(8,128)(2,1)}, bf16[256,256]{1,0:T(8,128)(2,1)S(1)}, u32[]{:S(2)}, u32[]{:S(2)}) collective-permute-start(bf16[256,256]{1,0:T(8,128)(2,1)} %param.6), channel_id=1, source_target_pairs={{0,2},{1,3},{2,4},{3,5},{4,6},{5,7},{6,8},{7,9},{8,10},{9,11},{10,... | collective-permute-start | bytes 393224 | tf_op jit(solution)/shard_map/ppermute | solution.py:10
  5.7 1.4 %fusion.9 = f32[256,1024]{1,0:T(8,128)S(1)} fusion(bf16[256,256]{1,0:T(8,128)(2,1)} %param.6, bf16[512,1024]{1,0:T(8,128)(2,1)} %param.8), kind=kOutput, calls=%fused_computation.29 | convolution fusion | flops 134217728 | bytes 1703936 | tf_op jit(solution)/shard_map/dot_general | solution.py:84
  7.2 0.7 pad_clamp_fusion
  7.9 2.7 %collective-permute-done = bf16[256,256]{1,0:T(8,128)(2,1)S(1)} collective-permute-done((bf16[256,256]{1,0:T(8,128)(2,1)}, bf16[256,256]{1,0:T(8,128)(2,1)S(1)}, u32[]{:S(2)}, u32[]{:S(2)}) %collective-permute-start) | collective-permute-done | bytes 131104 | tf_op jit(solution)/shard_map/ppermute | solution.py:10
  10.5 0.0 copy-done.2
  10.6 1.0 fusion
  11.6 0.0 copy-done
  11.6 0.0 copy-done.10
  11.6 0.0 copy-start.4
  11.6 0.4 multiply_convert_fusion.1
  12.0 0.0 copy-done.8
  12.0 0.0 copy-start.6
  12.1 0.0 copy-start.9
  12.1 0.1 convert_reduce_fusion
  12.2 0.3 copy-done.4
  12.5 0.3 convolution_bitcast_fusion
  12.8 0.1 reshape.51
  12.9 0.3 fusion.11
  13.2 0.0 copy-done.6
  13.2 0.0 copy-done.9
  13.3 0.3 convolution_bitcast_fusion.1
  13.6 1.5 %pad_maximum_fusion.1 = f32[512,1024]{1,0:T(8,128)} fusion(f32[256,1024]{1,0:T(8,128)S(1)} %convolution_bitcast_fusion, f32[256,1024]{1,0:T(8,128)S(1)} %convolution_bitcast_fusion.1), kind=kLoop, calls=%fused_computation.2 | loop fusion | flops 524288 | bytes 4194304 | tf_op jit(solution)/shard_map/concatenate | solution.py:106
  15.1 1.7 %reshape.49 = f32[32,128,128]{2,1,0:T(8,128)S(1)} reshape(f32[512,1024]{1,0:T(8,128)} %pad_maximum_fusion.1) | data formatting | bytes 4194304 | tf_op jit(solution)/shard_map/reshape | solution.py:125
  16.8 1.7 %pad_maximum_fusion = f32[32,168,128]{2,1,0:T(8,128)} fusion(f32[32,8,128]{2,1,0:T(8,128)S(1)} %pad_slice_fusion, f32[32,32,128]{2,1,0:T(8,128)S(1)} %reshape.50, f32[32,128,128]{2,1,0:T(8,128)S(1)} %reshape.49), kind=kLoop, calls=%fused_computation.1 | loop fusion | flops 1376256 | bytes 5505024 | tf_op jit(solution)/shard_map/concatenate | solution.py:123
  18.5 2.5 %gather_fusion = f32[32,168,128]{2,1,0:T(8,128)S(1)} fusion(f32[32,168,128]{2,1,0:T(8,128)} %pad_maximum_fusion, s32[1024]{0:T(1024)S(1)} %pad_clamp_fusion), kind=kCustom, calls=%fused_computation | custom fusion | bytes 5505152 | tf_op jit(solution)/shard_map/jit(_take)/gather | solution.py:47
  21.1 1.2 dynamic-slice_bitcast_fusion
  22.2 1.9 %collective-permute-start.2 = (f32[16,168,128]{2,1,0:T(8,128)}, f32[16,168,128]{2,1,0:T(8,128)}, u32[]{:S(2)}, u32[]{:S(2)}) collective-permute-start(f32[16,168,128]{2,1,0:T(8,128)} %dynamic-slice_bitcast_fusion), channel_id=1, source_target_pairs={{0,1},{1,0},{2,3},{3,2},{4,5},{5,4},{6,7},{7,6},{8,9},{9,8},{10,11... | collective-permute-start | bytes 4128776 | tf_op jit(solution)/shard_map/ppermute | solution.py:62
  24.2 3.4 %collective-permute-done.2 = f32[16,168,128]{2,1,0:T(8,128)} collective-permute-done((f32[16,168,128]{2,1,0:T(8,128)}, f32[16,168,128]{2,1,0:T(8,128)}, u32[]{:S(2)}, u32[]{:S(2)}) %collective-permute-start.2) | collective-permute-done | bytes 1376288 | tf_op jit(solution)/shard_map/ppermute | solution.py:62
  27.6 1.5 %bitcast_add_fusion = f32[16,168,128]{2,1,0:T(8,128)S(1)} fusion(f32[16,168,128]{2,1,0:T(8,128)} %collective-permute-done.2, f32[2,16,168,128]{3,2,1,0:T(8,128)S(1)} %bitcast.40, s32[]{:T(128)S(6)} %select_n.78), kind=kLoop, calls=%fused_computation.3 | loop fusion | flops 344064 | bytes 4128772 | tf_op jit(solution)/shard_map/add | solution.py:62
  29.1 0.0 copy-start.1
  29.1 1.1 copy-done.1
  30.2 3.3 %collective-permute-start.3 = (f32[8,168,128]{2,1,0:T(8,128)S(1)}, f32[8,168,128]{2,1,0:T(8,128)S(1)}, u32[]{:S(2)}, u32[]{:S(2)}) collective-permute-start(f32[8,168,128]{2,1,0:T(8,128)S(1)} %dynamic-slice_bitcast_fusion.1), channel_id=1, source_target_pairs={{0,4},{1,29},{2,6},{3,31},{4,0},{5,9},{6,2},{7,11},{8,12},{9,5},{1... | collective-permute-start | bytes 2064392 | tf_op jit(solution)/shard_map/ppermute | solution.py:62
  33.5 9.6 %collective-permute-done.3 = f32[8,168,128]{2,1,0:T(8,128)S(1)} collective-permute-done((f32[8,168,128]{2,1,0:T(8,128)S(1)}, f32[8,168,128]{2,1,0:T(8,128)S(1)}, u32[]{:S(2)}, u32[]{:S(2)}) %collective-permute-start.3) | collective-permute-done | bytes 688160 | tf_op jit(solution)/shard_map/ppermute | solution.py:62
  43.0 1.2 bitcast_add_fusion.1
  44.2 0.0 copy-start.3
  44.3 4.7 %collective-permute-start.4 = (f32[4,168,128]{2,1,0:T(8,128)S(1)}, f32[4,168,128]{2,1,0:T(8,128)S(1)}, u32[]{:S(2)}, u32[]{:S(2)}) collective-permute-start(f32[4,168,128]{2,1,0:T(8,128)S(1)} %dynamic-slice_bitcast_fusion.2), channel_id=1, source_target_pairs={{0,8},{1,3},{2,10},{3,1},{4,12},{5,7},{6,14},{7,5},{8,0},{9,11},{1... | collective-permute-start | bytes 1032200 | tf_op jit(solution)/shard_map/ppermute | solution.py:62
  49.0 9.1 %collective-permute-done.4 = f32[4,168,128]{2,1,0:T(8,128)S(1)} collective-permute-done((f32[4,168,128]{2,1,0:T(8,128)S(1)}, f32[4,168,128]{2,1,0:T(8,128)S(1)}, u32[]{:S(2)}, u32[]{:S(2)}) %collective-permute-start.4) | collective-permute-done | bytes 344096 | tf_op jit(solution)/shard_map/ppermute | solution.py:62
  58.2 4.0 %collective-permute-start.5 = (f32[2,168,128]{2,1,0:T(8,128)S(1)}, f32[2,168,128]{2,1,0:T(8,128)S(1)}, u32[]{:S(2)}, u32[]{:S(2)}) collective-permute-start(f32[2,168,128]{2,1,0:T(8,128)S(1)} %dynamic-slice_bitcast_fusion.3), channel_id=1, source_target_pairs={{0,2},{1,9},{2,0},{3,11},{4,6},{5,29},{6,4},{7,31},{8,10},{9,1},{1... | collective-permute-start | bytes 516104 | tf_op jit(solution)/shard_map/ppermute | solution.py:62
  62.2 0.0 copy-start.5
  62.3 0.0 copy-start.7
  62.3 4.7 %collective-permute-done.5 = f32[2,168,128]{2,1,0:T(8,128)S(1)} collective-permute-done((f32[2,168,128]{2,1,0:T(8,128)S(1)}, f32[2,168,128]{2,1,0:T(8,128)S(1)}, u32[]{:S(2)}, u32[]{:S(2)}) %collective-permute-start.5) | collective-permute-done | bytes 172064 | tf_op jit(solution)/shard_map/ppermute | solution.py:62
  67.0 4.6 %collective-permute-start.6 = (f32[1,168,128]{2,1,0:T(8,128)S(1)}, f32[1,168,128]{2,1,0:T(8,128)S(1)}, u32[]{:S(2)}, u32[]{:S(2)}) collective-permute-start(f32[1,168,128]{2,1,0:T(8,128)S(1)} %constant_dynamic-slice_fusion), channel_id=1, source_target_pairs={{0,16},{1,17},{2,18},{3,19},{4,20},{5,21},{6,22},{7,23},{8,24},{9,... | collective-permute-start | bytes 258056 | tf_op jit(solution)/shard_map/ppermute | solution.py:62
  71.7 5.7 %collective-permute-done.6 = f32[1,168,128]{2,1,0:T(8,128)S(1)} collective-permute-done((f32[1,168,128]{2,1,0:T(8,128)S(1)}, f32[1,168,128]{2,1,0:T(8,128)S(1)}, u32[]{:S(2)}, u32[]{:S(2)}) %collective-permute-start.6) | collective-permute-done | bytes 86048 | tf_op jit(solution)/shard_map/ppermute | solution.py:62
  77.4 4.3 %collective-permute-start.7 = (f32[168,128]{1,0:T(8,128)S(1)}, f32[168,128]{1,0:T(8,128)S(1)}, u32[]{:S(2)}, u32[]{:S(2)}) collective-permute-start(f32[168,128]{1,0:T(8,128)S(1)} %add_bitcast_fusion), channel_id=1, source_target_pairs={{0,32},{1,257},{2,34},{3,259},{4,36},{5,261},{6,38},{7,263},{8,40}... | collective-permute-start | bytes 258056 | tf_op jit(solution)/shard_map/ppermute | solution.py:77
  81.6 0.1 pad_maximum_fusion.2
  81.7 3.6 %collective-permute-start.1 = (bf16[256,1024]{1,0:T(8,128)(2,1)S(1)}, bf16[256,1024]{1,0:T(8,128)(2,1)S(1)}, u32[]{:S(2)}, u32[]{:S(2)}) collective-permute-start(bf16[256,1024]{1,0:T(8,128)(2,1)S(1)} %pad_maximum_fusion.2), channel_id=1, source_target_pairs={{2,0},{3,1},{4,2},{5,3},{6,4},{7,5},{8,6},{9,7},{10,8},{11,9},{12,... | collective-permute-start | bytes 1572872 | tf_op jit(solution)/shard_map/ppermute | solution.py:10
  85.3 0.0 collective-permute-done.7
  85.3 4.8 %collective-permute-start.8 = (f32[168,128]{1,0:T(8,128)S(1)}, f32[168,128]{1,0:T(8,128)S(1)}, u32[]{:S(2)}, u32[]{:S(2)}) collective-permute-start(f32[168,128]{1,0:T(8,128)S(1)} %add.142), channel_id=1, source_target_pairs={{0,256},{1,225},{2,258},{3,227},{4,260},{5,229},{6,262},{7,231},{8... | collective-permute-start | bytes 258056 | tf_op jit(solution)/shard_map/ppermute | solution.py:77
  90.1 0.0 copy-done.3
  90.1 1.2 %convolution_add_fusion.3 = f32[256,256]{1,0:T(8,128)S(1)} fusion(bf16[512,1024]{1,0:T(8,128)(2,1)S(1)} %copy-done.3, bf16[256,256]{1,0:T(8,128)(2,1)} %param.7, bf16[256,512]{1,0:T(8,128)(2,1)S(1)} %get-tuple-element.6, bf16[256,512]{1,0:T(8,128)(2,1)S(1)} %get-tuple-element.5), kind=kOutput, calls=%fused_computation.11 | convolution fusion | flops 135397376 | bytes 1441792 | tf_op jit(solution)/shard_map/dot_general | solution.py:20
  91.3 11.1 %collective-permute-done.8 = f32[168,128]{1,0:T(8,128)S(1)} collective-permute-done((f32[168,128]{1,0:T(8,128)S(1)}, f32[168,128]{1,0:T(8,128)S(1)}, u32[]{:S(2)}, u32[]{:S(2)}) %collective-permute-start.8) | collective-permute-done | bytes 86048 | tf_op jit(solution)/shard_map/ppermute | solution.py:77
  102.5 1.9 %collective-permute-start.9 = (f32[168,128]{1,0:T(8,128)S(1)}, f32[168,128]{1,0:T(8,128)S(1)}, u32[]{:S(2)}, u32[]{:S(2)}) collective-permute-start(f32[168,128]{1,0:T(8,128)S(1)} %add.143), channel_id=1, source_target_pairs={{0,64},{1,129},{2,66},{3,131},{4,68},{5,133},{6,70},{7,135},{8,72}... | collective-permute-start | bytes 258056 | tf_op jit(solution)/shard_map/ppermute | solution.py:77
  104.4 0.9 fusion.1
  105.3 5.5 %collective-permute-done.9 = f32[168,128]{1,0:T(8,128)S(1)} collective-permute-done((f32[168,128]{1,0:T(8,128)S(1)}, f32[168,128]{1,0:T(8,128)S(1)}, u32[]{:S(2)}, u32[]{:S(2)}) %collective-permute-start.9) | collective-permute-done | bytes 86048 | tf_op jit(solution)/shard_map/ppermute | solution.py:77
  110.8 6.6 %collective-permute-start.10 = (f32[168,128]{1,0:T(8,128)S(1)}, f32[168,128]{1,0:T(8,128)S(1)}, u32[]{:S(2)}, u32[]{:S(2)}) collective-permute-start(f32[168,128]{1,0:T(8,128)S(1)} %add.144), channel_id=1, source_target_pairs={{0,128},{1,65},{2,130},{3,67},{4,132},{5,69},{6,134},{7,71},{8,136... | collective-permute-start | bytes 258056 | tf_op jit(solution)/shard_map/ppermute | solution.py:77
  117.4 0.0 collective-permute-done.1
  117.4 1.0 fusion.2
  118.4 2.7 %collective-permute-done.10 = f32[168,128]{1,0:T(8,128)S(1)} collective-permute-done((f32[168,128]{1,0:T(8,128)S(1)}, f32[168,128]{1,0:T(8,128)S(1)}, u32[]{:S(2)}, u32[]{:S(2)}) %collective-permute-start.10) | collective-permute-done | bytes 86048 | tf_op jit(solution)/shard_map/ppermute | solution.py:77
  121.1 0.5 slice_bitcast_fusion
  121.6 0.6 reshape.55
  122.3 0.6 reshape.56
  (18 shorter events, 0.3 us)
Async XLA Ops:
  0.6 10.9 %copy-start = (bf16[512,256]{1,0:T(8,128)(2,1)S(1)}, bf16[512,256]{1,0:T(8,128)(2,1)}, u32[]{:S(2)}) copy-start(bf16[512,256]{1,0:T(8,128)(2,1)} %param.10) | copy-start | bytes 786436
  0.6 9.9 %copy-start.2 = (bf16[512,1024]{1,0:T(8,128)(2,1)S(1)}, bf16[512,1024]{1,0:T(8,128)(2,1)}, u32[]{:S(2)}) copy-start(bf16[512,1024]{1,0:T(8,128)(2,1)} %param.8) | copy-start | bytes 3145732
  0.7 10.9 %copy-start.10 = (bf16[256,256]{1,0:T(8,128)(2,1)S(1)}, bf16[256,256]{1,0:T(8,128)(2,1)}, u32[]{:S(2)}) copy-start(bf16[256,256]{1,0:T(8,128)(2,1)} %param.7) | copy-start | bytes 393220
  0.7 9.9 %collective-permute-start = (bf16[256,256]{1,0:T(8,128)(2,1)}, bf16[256,256]{1,0:T(8,128)(2,1)S(1)}, u32[]{:S(2)}, u32[]{:S(2)}) collective-permute-start(bf16[256,256]{1,0:T(8,128)(2,1)} %param.6), channel_id=1, source_target_pairs={{0,2},{1,3},{2,4},{3,5},{4,6},{5,7},{6,8},{7,9},{8,10},{9,11},{10,... | collective-permute-start | bytes 393224 | tf_op jit(solution)/shard_map/ppermute | solution.py:10
  10.6 1.5 %copy-start.8 = (bf16[256,256]{1,0:T(8,128)(2,1)}, bf16[256,256]{1,0:T(8,128)(2,1)S(1)}, u32[]{:S(2)}) copy-start(bf16[256,256]{1,0:T(8,128)(2,1)S(1)} %collective-permute-done) | copy-start | bytes 393220
  11.6 0.9 copy-start.4
  12.0 1.2 copy-start.6
  12.1 1.2 copy-start.9
  22.2 5.4 %collective-permute-start.2 = (f32[16,168,128]{2,1,0:T(8,128)}, f32[16,168,128]{2,1,0:T(8,128)}, u32[]{:S(2)}, u32[]{:S(2)}) collective-permute-start(f32[16,168,128]{2,1,0:T(8,128)} %dynamic-slice_bitcast_fusion), channel_id=1, source_target_pairs={{0,1},{1,0},{2,3},{3,2},{4,5},{5,4},{6,7},{7,6},{8,9},{9,8},{10,11... | collective-permute-start | bytes 4128776 | tf_op jit(solution)/shard_map/ppermute | solution.py:62
  29.1 1.1 copy-start.1
  30.2 12.8 %collective-permute-start.3 = (f32[8,168,128]{2,1,0:T(8,128)S(1)}, f32[8,168,128]{2,1,0:T(8,128)S(1)}, u32[]{:S(2)}, u32[]{:S(2)}) collective-permute-start(f32[8,168,128]{2,1,0:T(8,128)S(1)} %dynamic-slice_bitcast_fusion.1), channel_id=1, source_target_pairs={{0,4},{1,29},{2,6},{3,31},{4,0},{5,9},{6,2},{7,11},{8,12},{9,5},{1... | collective-permute-start | bytes 2064392 | tf_op jit(solution)/shard_map/ppermute | solution.py:62
  44.2 45.9 %copy-start.3 = (bf16[512,1024]{1,0:T(8,128)(2,1)S(1)}, bf16[512,1024]{1,0:T(8,128)(2,1)}, u32[]{:S(2)}) copy-start(bf16[512,1024]{1,0:T(8,128)(2,1)} %param.8) | copy-start | bytes 3145732
  44.3 13.9 %collective-permute-start.4 = (f32[4,168,128]{2,1,0:T(8,128)S(1)}, f32[4,168,128]{2,1,0:T(8,128)S(1)}, u32[]{:S(2)}, u32[]{:S(2)}) collective-permute-start(f32[4,168,128]{2,1,0:T(8,128)S(1)} %dynamic-slice_bitcast_fusion.2), channel_id=1, source_target_pairs={{0,8},{1,3},{2,10},{3,1},{4,12},{5,7},{6,14},{7,5},{8,0},{9,11},{1... | collective-permute-start | bytes 1032200 | tf_op jit(solution)/shard_map/ppermute | solution.py:62
  58.2 8.8 %collective-permute-start.5 = (f32[2,168,128]{2,1,0:T(8,128)S(1)}, f32[2,168,128]{2,1,0:T(8,128)S(1)}, u32[]{:S(2)}, u32[]{:S(2)}) collective-permute-start(f32[2,168,128]{2,1,0:T(8,128)S(1)} %dynamic-slice_bitcast_fusion.3), channel_id=1, source_target_pairs={{0,2},{1,9},{2,0},{3,11},{4,6},{5,29},{6,4},{7,31},{8,10},{9,1},{1... | collective-permute-start | bytes 516104 | tf_op jit(solution)/shard_map/ppermute | solution.py:62
  62.2 42.2 %copy-start.5 = (bf16[256,256]{1,0:T(8,128)(2,1)S(1)}, bf16[256,256]{1,0:T(8,128)(2,1)}, u32[]{:S(2)}) copy-start(bf16[256,256]{1,0:T(8,128)(2,1)} %param.6) | copy-start | bytes 393220
  62.3 42.2 %copy-start.7 = (bf16[256,512]{1,0:T(8,128)(2,1)S(1)}, bf16[256,512]{1,0:T(8,128)(2,1)}, u32[]{:S(2)}) copy-start(bf16[256,512]{1,0:T(8,128)(2,1)} %copy-done.6) | copy-start | bytes 786436
  67.0 10.3 %collective-permute-start.6 = (f32[1,168,128]{2,1,0:T(8,128)S(1)}, f32[1,168,128]{2,1,0:T(8,128)S(1)}, u32[]{:S(2)}, u32[]{:S(2)}) collective-permute-start(f32[1,168,128]{2,1,0:T(8,128)S(1)} %constant_dynamic-slice_fusion), channel_id=1, source_target_pairs={{0,16},{1,17},{2,18},{3,19},{4,20},{5,21},{6,22},{7,23},{8,24},{9,... | collective-permute-start | bytes 258056 | tf_op jit(solution)/shard_map/ppermute | solution.py:62
  77.4 7.9 %collective-permute-start.7 = (f32[168,128]{1,0:T(8,128)S(1)}, f32[168,128]{1,0:T(8,128)S(1)}, u32[]{:S(2)}, u32[]{:S(2)}) collective-permute-start(f32[168,128]{1,0:T(8,128)S(1)} %add_bitcast_fusion), channel_id=1, source_target_pairs={{0,32},{1,257},{2,34},{3,259},{4,36},{5,261},{6,38},{7,263},{8,40}... | collective-permute-start | bytes 258056 | tf_op jit(solution)/shard_map/ppermute | solution.py:77
  81.7 35.7 %collective-permute-start.1 = (bf16[256,1024]{1,0:T(8,128)(2,1)S(1)}, bf16[256,1024]{1,0:T(8,128)(2,1)S(1)}, u32[]{:S(2)}, u32[]{:S(2)}) collective-permute-start(bf16[256,1024]{1,0:T(8,128)(2,1)S(1)} %pad_maximum_fusion.2), channel_id=1, source_target_pairs={{2,0},{3,1},{4,2},{5,3},{6,4},{7,5},{8,6},{9,7},{10,8},{11,9},{12,... | collective-permute-start | bytes 1572872 | tf_op jit(solution)/shard_map/ppermute | solution.py:10
  85.3 17.2 %collective-permute-start.8 = (f32[168,128]{1,0:T(8,128)S(1)}, f32[168,128]{1,0:T(8,128)S(1)}, u32[]{:S(2)}, u32[]{:S(2)}) collective-permute-start(f32[168,128]{1,0:T(8,128)S(1)} %add.142), channel_id=1, source_target_pairs={{0,256},{1,225},{2,258},{3,227},{4,260},{5,229},{6,262},{7,231},{8... | collective-permute-start | bytes 258056 | tf_op jit(solution)/shard_map/ppermute | solution.py:77
  102.5 8.3 %collective-permute-start.9 = (f32[168,128]{1,0:T(8,128)S(1)}, f32[168,128]{1,0:T(8,128)S(1)}, u32[]{:S(2)}, u32[]{:S(2)}) collective-permute-start(f32[168,128]{1,0:T(8,128)S(1)} %add.143), channel_id=1, source_target_pairs={{0,64},{1,129},{2,66},{3,131},{4,68},{5,133},{6,70},{7,135},{8,72}... | collective-permute-start | bytes 258056 | tf_op jit(solution)/shard_map/ppermute | solution.py:77
  110.8 10.3 %collective-permute-start.10 = (f32[168,128]{1,0:T(8,128)S(1)}, f32[168,128]{1,0:T(8,128)S(1)}, u32[]{:S(2)}, u32[]{:S(2)}) collective-permute-start(f32[168,128]{1,0:T(8,128)S(1)} %add.144), channel_id=1, source_target_pairs={{0,128},{1,65},{2,130},{3,67},{4,132},{5,69},{6,134},{7,71},{8,136... | collective-permute-start | bytes 258056 | tf_op jit(solution)/shard_map/ppermute | solution.py:77

commit v10 on v5

--- a/solution.py
+++ b/solution.py
@@ -129,7 +129,7 @@
         axis=1,
     )
     mine = halving_scatter(packed, "seq", ([0, 2, 3, 1, 4], [0, 2, 1, 3, 4]), (4, 8))
-    mine = butterfly_sum(mine, ("grp", "seq"), ([0, 3, 1, 2], [3, 0, 2, 1]), (1, 8), groups)
+    mine = butterfly_sum(mine, ("grp", "seq"), ([0, 1, 2, 3], [3, 0, 1, 2]), (1, 8), groups)
     grad_taps = mine[:taps_r].reshape(rows_taps, part_taps.shape[1])
     grad_out = mine[taps_r : taps_r + out_r].reshape(rows_out, part_out.shape[1])
     grad_bias = mine[taps_r + out_r, :share_bias]

time: 118 us -> 116 us (0.983)
  waiting for transfers between devices: 55.5 us -> 43.6 us
  starting transfers between devices: 43.9 us -> 53.3 us
    ppermute x4, waiting for transfers between devices: 20 us -> 8.09 us  [butterfly_sum(): array = array + lax.ppermute(array, axes, pairs)]
    ppermute x4, starting transfers between devices: 16.7 us -> 26.2 us  [butterfly_sum(): array = array + lax.ppermute(array, axes, pairs)]
where the time goes in v10:
time: 116 us; the launch traced here: 115 us
  starting transfers between devices  53.3 us (46%)
  waiting for transfers between devices  43.6 us (38%)
  matrix products  7.44 us (6%)
  local copies, waits for them, and re-layouts  6.02 us (5%)
  other arithmetic  3.5 us (3%)
  between operations  1.34 us (1%)
    ppermute x5, waiting for transfers between devices, halving_scatter(): buf = keep + lax.ppermute(send, axis, pairs)  32.2 us
    ppermute x4, starting transfers between devices, butterfly_sum(): array = array + lax.ppermute(array, axes, pairs)  26.2 us
    ppermute x5, starting transfers between devices, halving_scatter(): buf = keep + lax.ppermute(send, axis, pairs)  18.5 us
    ppermute x2, starting transfers between devices, from_behind(): return lax.ppermute(array, axis, pairs)  8.63 us
    ppermute x4, waiting for transfers between devices, butterfly_sum(): array = array + lax.ppermute(array, axes, pairs)  8.09 us
    ppermute x2, waiting for transfers between devices, from_behind(): return lax.ppermute(array, axis, pairs)  3.33 us
    dot_general x3, matrix products, contract_cols(): lax.dot_general(left, right, (((1,), (1,)), ((), ())), preferred_element_...  2.85 us
  transfers between devices with their start and end apart: 11, of which 9 were waited for; matrix products, arithmetic and copies ran while one was open for 4% of the time, Pallas kernels for 0%

profile of v10, /device:TPU:56, one launch (start us, length us, event | category | flops | bytes accessed | tf_op | source)
XLA Modules:
  0.0 115.3 jit_solution(14468853055618822656)
XLA Ops:
  0.6 0.0 copy-start
  0.6 0.0 copy-start.7
  0.7 5.1 %collective-permute-start = (bf16[256,256]{1,0:T(8,128)(2,1)}, bf16[256,256]{1,0:T(8,128)(2,1)S(1)}, u32[]{:S(2)}, u32[]{:S(2)}) collective-permute-start(bf16[256,256]{1,0:T(8,128)(2,1)} %param.5), channel_id=1, source_target_pairs={{0,2},{1,3},{2,4},{3,5},{4,6},{5,7},{6,8},{7,9},{8,10},{9,11},{10,... | collective-permute-start | bytes 393224 | tf_op jit(solution)/shard_map/ppermute | solution.py:10
  5.7 1.4 %fusion.9 = f32[256,1024]{1,0:T(8,128)S(1)} fusion(bf16[256,256]{1,0:T(8,128)(2,1)} %param.5, bf16[512,1024]{1,0:T(8,128)(2,1)} %param.7), kind=kOutput, calls=%fused_computation.28 | convolution fusion | flops 134217728 | bytes 1703936 | tf_op jit(solution)/shard_map/dot_general | solution.py:84
  7.2 3.3 %collective-permute-done = bf16[256,256]{1,0:T(8,128)(2,1)S(1)} collective-permute-done((bf16[256,256]{1,0:T(8,128)(2,1)}, bf16[256,256]{1,0:T(8,128)(2,1)S(1)}, u32[]{:S(2)}, u32[]{:S(2)}) %collective-permute-start) | collective-permute-done | bytes 131104 | tf_op jit(solution)/shard_map/ppermute | solution.py:10
  10.5 1.3 %fusion = f32[256,1024]{1,0:T(8,128)S(1)} fusion(f32[256,1024]{1,0:T(8,128)S(1)} %fusion.9, bf16[256,256]{1,0:T(8,128)(2,1)S(1)} %collective-permute-done, f32[1024]{0:T(1024)} %param.8, bf16[512,1024]{1,0:T(8,128)(2,1)} %param.7), kind=kOutput, calls=%fused_computation.7 | convolution fusion | flops 134742016 | bytes 2756608 | tf_op jit(solution)/shard_map/dot_general | solution.py:87
  11.9 0.0 copy-done
  11.9 0.0 copy-done.7
  11.9 0.0 copy-start.3
  11.9 0.5 multiply_convert_fusion.1
  12.4 0.0 copy-start.5
  12.4 0.1 convert_reduce_fusion
  12.5 0.3 copy-done.3
  12.8 0.3 convolution_bitcast_fusion
  13.2 0.1 reshape.45
  13.3 0.3 fusion.11
  13.6 0.3 convolution_bitcast_fusion.1
  13.9 0.0 copy-done.5
  13.9 1.5 %pad_maximum_fusion.1 = f32[512,1024]{1,0:T(8,128)} fusion(f32[256,1024]{1,0:T(8,128)S(1)} %convolution_bitcast_fusion, f32[256,1024]{1,0:T(8,128)S(1)} %convolution_bitcast_fusion.1), kind=kLoop, calls=%fused_computation.1 | loop fusion | flops 524288 | bytes 4194304 | tf_op jit(solution)/shard_map/concatenate | solution.py:106
  15.4 1.7 %reshape.43 = f32[32,128,128]{2,1,0:T(8,128)S(1)} reshape(f32[512,1024]{1,0:T(8,128)} %pad_maximum_fusion.1) | data formatting | bytes 4194304 | tf_op jit(solution)/shard_map/reshape | solution.py:125
  17.1 0.2 pad_maximum_fusion
  17.9 0.0 copy-start.1
  17.9 1.5 %copy-done.1 = f32[32,168,128]{2,1,0:T(8,128)} copy-done((f32[32,168,128]{2,1,0:T(8,128)}, f32[32,168,128]{2,1,0:T(8,128)S(1)}, u32[]{:S(2)}) %copy-start.1) | copy-done | bytes 2752536
  19.4 0.1 dynamic-slice_bitcast_fusion
  19.5 1.9 %collective-permute-start.2 = (f32[16,168,128]{2,1,0:T(8,128)S(1)}, f32[16,168,128]{2,1,0:T(8,128)S(1)}, u32[]{:S(2)}, u32[]{:S(2)}) collective-permute-start(f32[16,168,128]{2,1,0:T(8,128)S(1)} %dynamic-slice_bitcast_fusion), channel_id=1, source_target_pairs={{0,1},{1,0},{2,3},{3,2},{4,5},{5,4},{6,7},{7,6},{8,9},{9,8},{10,11... | collective-permute-start | bytes 4128776 | tf_op jit(solution)/shard_map/ppermute | solution.py:62
  21.4 3.1 %collective-permute-done.2 = f32[16,168,128]{2,1,0:T(8,128)S(1)} collective-permute-done((f32[16,168,128]{2,1,0:T(8,128)S(1)}, f32[16,168,128]{2,1,0:T(8,128)S(1)}, u32[]{:S(2)}, u32[]{:S(2)}) %collective-permute-start.2) | collective-permute-done | bytes 1376288 | tf_op jit(solution)/shard_map/ppermute | solution.py:62
  24.5 1.5 %bitcast_add_fusion = f32[16,168,128]{2,1,0:T(8,128)S(1)} fusion(f32[16,168,128]{2,1,0:T(8,128)S(1)} %collective-permute-done.2, f32[2,16,168,128]{3,2,1,0:T(8,128)} %bitcast.42, s32[]{:T(128)S(6)} %select_n.66), kind=kLoop, calls=%fused_computation.2 | loop fusion | flops 344064 | bytes 4128772 | tf_op jit(solution)/shard_map/add | solution.py:62
  26.0 0.1 dynamic-slice_bitcast_fusion.1
  26.1 3.3 %collective-permute-start.3 = (f32[8,168,128]{2,1,0:T(8,128)S(1)}, f32[8,168,128]{2,1,0:T(8,128)S(1)}, u32[]{:S(2)}, u32[]{:S(2)}) collective-permute-start(f32[8,168,128]{2,1,0:T(8,128)S(1)} %dynamic-slice_bitcast_fusion.1), channel_id=1, source_target_pairs={{0,4},{1,29},{2,6},{3,31},{4,0},{5,9},{6,2},{7,11},{8,12},{9,5},{1... | collective-permute-start | bytes 2064392 | tf_op jit(solution)/shard_map/ppermute | solution.py:62
  29.3 9.6 %collective-permute-done.3 = f32[8,168,128]{2,1,0:T(8,128)S(1)} collective-permute-done((f32[8,168,128]{2,1,0:T(8,128)S(1)}, f32[8,168,128]{2,1,0:T(8,128)S(1)}, u32[]{:S(2)}, u32[]{:S(2)}) %collective-permute-start.3) | collective-permute-done | bytes 688160 | tf_op jit(solution)/shard_map/ppermute | solution.py:62
  38.9 0.1 bitcast_add_fusion.1
  39.0 4.6 %collective-permute-start.4 = (f32[4,168,128]{2,1,0:T(8,128)S(1)}, f32[4,168,128]{2,1,0:T(8,128)S(1)}, u32[]{:S(2)}, u32[]{:S(2)}) collective-permute-start(f32[4,168,128]{2,1,0:T(8,128)S(1)} %dynamic-slice_bitcast_fusion.2), channel_id=1, source_target_pairs={{0,8},{1,3},{2,10},{3,1},{4,12},{5,7},{6,14},{7,5},{8,0},{9,11},{1... | collective-permute-start | bytes 1032200 | tf_op jit(solution)/shard_map/ppermute | solution.py:62
  43.6 0.0 copy-start.4
  43.6 0.0 copy-start.6
  43.6 9.1 %collective-permute-done.4 = f32[4,168,128]{2,1,0:T(8,128)S(1)} collective-permute-done((f32[4,168,128]{2,1,0:T(8,128)S(1)}, f32[4,168,128]{2,1,0:T(8,128)S(1)}, u32[]{:S(2)}, u32[]{:S(2)}) %collective-permute-start.4) | collective-permute-done | bytes 344096 | tf_op jit(solution)/shard_map/ppermute | solution.py:62
  52.8 0.0 copy-start.2
  52.8 4.2 %collective-permute-start.5 = (f32[2,168,128]{2,1,0:T(8,128)S(1)}, f32[2,168,128]{2,1,0:T(8,128)S(1)}, u32[]{:S(2)}, u32[]{:S(2)}) collective-permute-start(f32[2,168,128]{2,1,0:T(8,128)S(1)} %dynamic-slice_bitcast_fusion.3), channel_id=1, source_target_pairs={{0,2},{1,9},{2,0},{3,11},{4,6},{5,29},{6,4},{7,31},{8,10},{9,1},{1... | collective-permute-start | bytes 516104 | tf_op jit(solution)/shard_map/ppermute | solution.py:62
  57.0 4.8 %collective-permute-done.5 = f32[2,168,128]{2,1,0:T(8,128)S(1)} collective-permute-done((f32[2,168,128]{2,1,0:T(8,128)S(1)}, f32[2,168,128]{2,1,0:T(8,128)S(1)}, u32[]{:S(2)}, u32[]{:S(2)}) %collective-permute-start.5) | collective-permute-done | bytes 172064 | tf_op jit(solution)/shard_map/ppermute | solution.py:62
  61.8 4.6 %collective-permute-start.6 = (f32[1,168,128]{2,1,0:T(8,128)S(1)}, f32[1,168,128]{2,1,0:T(8,128)S(1)}, u32[]{:S(2)}, u32[]{:S(2)}) collective-permute-start(f32[1,168,128]{2,1,0:T(8,128)S(1)} %constant_dynamic-slice_fusion), channel_id=1, source_target_pairs={{0,16},{1,17},{2,18},{3,19},{4,20},{5,21},{6,22},{7,23},{8,24},{9,... | collective-permute-start | bytes 258056 | tf_op jit(solution)/shard_map/ppermute | solution.py:62
  66.4 5.7 %collective-permute-done.6 = f32[1,168,128]{2,1,0:T(8,128)S(1)} collective-permute-done((f32[1,168,128]{2,1,0:T(8,128)S(1)}, f32[1,168,128]{2,1,0:T(8,128)S(1)}, u32[]{:S(2)}, u32[]{:S(2)}) %collective-permute-start.6) | collective-permute-done | bytes 86048 | tf_op jit(solution)/shard_map/ppermute | solution.py:62
  72.1 4.3 %collective-permute-start.7 = (f32[168,128]{1,0:T(8,128)S(1)}, f32[168,128]{1,0:T(8,128)S(1)}, u32[]{:S(2)}, u32[]{:S(2)}) collective-permute-start(f32[168,128]{1,0:T(8,128)S(1)} %add_bitcast_fusion), channel_id=1, source_target_pairs={{0,32},{1,257},{2,34},{3,259},{4,36},{5,261},{6,38},{7,263},{8,40}... | collective-permute-start | bytes 258056 | tf_op jit(solution)/shard_map/ppermute | solution.py:77
  76.4 0.1 pad_maximum_fusion.2
  76.5 3.6 %collective-permute-start.1 = (bf16[256,1024]{1,0:T(8,128)(2,1)S(1)}, bf16[256,1024]{1,0:T(8,128)(2,1)S(1)}, u32[]{:S(2)}, u32[]{:S(2)}) collective-permute-start(bf16[256,1024]{1,0:T(8,128)(2,1)S(1)} %pad_maximum_fusion.2), channel_id=1, source_target_pairs={{2,0},{3,1},{4,2},{5,3},{6,4},{7,5},{8,6},{9,7},{10,8},{11,9},{12,... | collective-permute-start | bytes 1572872 | tf_op jit(solution)/shard_map/ppermute | solution.py:10
  80.0 0.0 collective-permute-done.7
  80.1 10.5 %collective-permute-start.8 = (f32[168,128]{1,0:T(8,128)S(1)}, f32[168,128]{1,0:T(8,128)S(1)}, u32[]{:S(2)}, u32[]{:S(2)}) collective-permute-start(f32[168,128]{1,0:T(8,128)S(1)} %add.132), channel_id=1, source_target_pairs={{0,64},{1,225},{2,66},{3,227},{4,68},{5,229},{6,70},{7,231},{8,72}... | collective-permute-start | bytes 258056 | tf_op jit(solution)/shard_map/ppermute | solution.py:77
  90.6 1.4 %convolution_add_fusion.3 = f32[256,256]{1,0:T(8,128)S(1)} fusion(bf16[512,1024]{1,0:T(8,128)(2,1)} %param.7, bf16[256,256]{1,0:T(8,128)(2,1)} %param.6, bf16[256,512]{1,0:T(8,128)(2,1)S(1)} %get-tuple-element.6, bf16[256,512]{1,0:T(8,128)(2,1)S(1)} %get-tuple-element.5), kind=kOutput, calls=%fused_computation.10 | convolution fusion | flops 135397376 | bytes 1441792 | tf_op jit(solution)/shard_map/dot_general | solution.py:20
  92.0 3.4 %collective-permute-done.8 = f32[168,128]{1,0:T(8,128)S(1)} collective-permute-done((f32[168,128]{1,0:T(8,128)S(1)}, f32[168,128]{1,0:T(8,128)S(1)}, u32[]{:S(2)}, u32[]{:S(2)}) %collective-permute-start.8) | collective-permute-done | bytes 86048 | tf_op jit(solution)/shard_map/ppermute | solution.py:77
  95.4 9.2 %collective-permute-start.9 = (f32[168,128]{1,0:T(8,128)S(1)}, f32[168,128]{1,0:T(8,128)S(1)}, u32[]{:S(2)}, u32[]{:S(2)}) collective-permute-start(f32[168,128]{1,0:T(8,128)S(1)} %add.133), channel_id=1, source_target_pairs={{0,128},{1,65},{2,130},{3,67},{4,132},{5,69},{6,134},{7,71},{8,136... | collective-permute-start | bytes 258056 | tf_op jit(solution)/shard_map/ppermute | solution.py:77
  104.6 0.0 copy-done.4
  104.6 0.0 copy-done.6
  104.6 0.9 fusion.1
  105.5 1.5 %collective-permute-done.9 = f32[168,128]{1,0:T(8,128)S(1)} collective-permute-done((f32[168,128]{1,0:T(8,128)S(1)}, f32[168,128]{1,0:T(8,128)S(1)}, u32[]{:S(2)}, u32[]{:S(2)}) %collective-permute-start.9) | collective-permute-done | bytes 86048 | tf_op jit(solution)/shard_map/ppermute | solution.py:77
  107.1 2.2 %collective-permute-start.10 = (f32[168,128]{1,0:T(8,128)S(1)}, f32[168,128]{1,0:T(8,128)S(1)}, u32[]{:S(2)}, u32[]{:S(2)}) collective-permute-start(f32[168,128]{1,0:T(8,128)S(1)} %add.134), channel_id=1, source_target_pairs={{0,256},{1,129},{2,258},{3,131},{4,260},{5,133},{6,262},{7,135},{8... | collective-permute-start | bytes 258056 | tf_op jit(solution)/shard_map/ppermute | solution.py:77
  109.3 0.0 collective-permute-done.1
  109.3 0.0 copy-done.2
  109.3 1.0 fusion.2
  110.3 3.2 %collective-permute-done.10 = f32[168,128]{1,0:T(8,128)S(1)} collective-permute-done((f32[168,128]{1,0:T(8,128)S(1)}, f32[168,128]{1,0:T(8,128)S(1)}, u32[]{:S(2)}, u32[]{:S(2)}) %collective-permute-start.10) | collective-permute-done | bytes 86048 | tf_op jit(solution)/shard_map/ppermute | solution.py:77
  113.5 0.5 slice_bitcast_fusion
  114.0 0.6 reshape.50
  114.6 0.6 reshape.51
  (46 shorter events, 0.5 us)
Async XLA Ops:
  0.6 11.3 %copy-start = (bf16[512,256]{1,0:T(8,128)(2,1)S(1)}, bf16[512,256]{1,0:T(8,128)(2,1)}, u32[]{:S(2)}) copy-start(bf16[512,256]{1,0:T(8,128)(2,1)} %param.9) | copy-start | bytes 786436
  0.6 11.3 %copy-start.7 = (bf16[256,256]{1,0:T(8,128)(2,1)S(1)}, bf16[256,256]{1,0:T(8,128)(2,1)}, u32[]{:S(2)}) copy-start(bf16[256,256]{1,0:T(8,128)(2,1)} %param.6) | copy-start | bytes 393220
  0.7 9.9 %collective-permute-start = (bf16[256,256]{1,0:T(8,128)(2,1)}, bf16[256,256]{1,0:T(8,128)(2,1)S(1)}, u32[]{:S(2)}, u32[]{:S(2)}) collective-permute-start(bf16[256,256]{1,0:T(8,128)(2,1)} %param.5), channel_id=1, source_target_pairs={{0,2},{1,3},{2,4},{3,5},{4,6},{5,7},{6,8},{7,9},{8,10},{9,11},{10,... | collective-permute-start | bytes 393224 | tf_op jit(solution)/shard_map/ppermute | solution.py:10
  11.9 0.9 copy-start.3
  12.4 1.5 %copy-start.5 = (bf16[256,512]{1,0:T(8,128)(2,1)}, bf16[256,512]{1,0:T(8,128)(2,1)S(1)}, u32[]{:S(2)}) copy-start(bf16[256,512]{1,0:T(8,128)(2,1)S(1)} %get-tuple-element.7) | copy-start | bytes 786436
  17.9 1.5 %copy-start.1 = (f32[32,168,128]{2,1,0:T(8,128)}, f32[32,168,128]{2,1,0:T(8,128)S(1)}, u32[]{:S(2)}) copy-start(f32[32,168,128]{2,1,0:T(8,128)S(1)} %slice_dynamic-update-slice_fusion) | copy-start | bytes 8257540
  19.5 5.0 %collective-permute-start.2 = (f32[16,168,128]{2,1,0:T(8,128)S(1)}, f32[16,168,128]{2,1,0:T(8,128)S(1)}, u32[]{:S(2)}, u32[]{:S(2)}) collective-permute-start(f32[16,168,128]{2,1,0:T(8,128)S(1)} %dynamic-slice_bitcast_fusion), channel_id=1, source_target_pairs={{0,1},{1,0},{2,3},{3,2},{4,5},{5,4},{6,7},{7,6},{8,9},{9,8},{10,11... | collective-permute-start | bytes 4128776 | tf_op jit(solution)/shard_map/ppermute | solution.py:62
  26.1 12.8 %collective-permute-start.3 = (f32[8,168,128]{2,1,0:T(8,128)S(1)}, f32[8,168,128]{2,1,0:T(8,128)S(1)}, u32[]{:S(2)}, u32[]{:S(2)}) collective-permute-start(f32[8,168,128]{2,1,0:T(8,128)S(1)} %dynamic-slice_bitcast_fusion.1), channel_id=1, source_target_pairs={{0,4},{1,29},{2,6},{3,31},{4,0},{5,9},{6,2},{7,11},{8,12},{9,5},{1... | collective-permute-start | bytes 2064392 | tf_op jit(solution)/shard_map/ppermute | solution.py:62
  39.0 13.7 %collective-permute-start.4 = (f32[4,168,128]{2,1,0:T(8,128)S(1)}, f32[4,168,128]{2,1,0:T(8,128)S(1)}, u32[]{:S(2)}, u32[]{:S(2)}) collective-permute-start(f32[4,168,128]{2,1,0:T(8,128)S(1)} %dynamic-slice_bitcast_fusion.2), channel_id=1, source_target_pairs={{0,8},{1,3},{2,10},{3,1},{4,12},{5,7},{6,14},{7,5},{8,0},{9,11},{1... | collective-permute-start | bytes 1032200 | tf_op jit(solution)/shard_map/ppermute | solution.py:62
  43.6 61.0 %copy-start.4 = (bf16[256,256]{1,0:T(8,128)(2,1)S(1)}, bf16[256,256]{1,0:T(8,128)(2,1)}, u32[]{:S(2)}) copy-start(bf16[256,256]{1,0:T(8,128)(2,1)} %param.5) | copy-start | bytes 393220
  43.6 61.0 %copy-start.6 = (bf16[256,512]{1,0:T(8,128)(2,1)S(1)}, bf16[256,512]{1,0:T(8,128)(2,1)}, u32[]{:S(2)}) copy-start(bf16[256,512]{1,0:T(8,128)(2,1)} %copy-done.5) | copy-start | bytes 786436
  52.8 56.5 %copy-start.2 = (bf16[512,1024]{1,0:T(8,128)(2,1)S(1)}, bf16[512,1024]{1,0:T(8,128)(2,1)}, u32[]{:S(2)}) copy-start(bf16[512,1024]{1,0:T(8,128)(2,1)} %param.7) | copy-start | bytes 3145732
  52.8 8.9 %collective-permute-start.5 = (f32[2,168,128]{2,1,0:T(8,128)S(1)}, f32[2,168,128]{2,1,0:T(8,128)S(1)}, u32[]{:S(2)}, u32[]{:S(2)}) collective-permute-start(f32[2,168,128]{2,1,0:T(8,128)S(1)} %dynamic-slice_bitcast_fusion.3), channel_id=1, source_target_pairs={{0,2},{1,9},{2,0},{3,11},{4,6},{5,29},{6,4},{7,31},{8,10},{9,1},{1... | collective-permute-start | bytes 516104 | tf_op jit(solution)/shard_map/ppermute | solution.py:62
  61.8 10.3 %collective-permute-start.6 = (f32[1,168,128]{2,1,0:T(8,128)S(1)}, f32[1,168,128]{2,1,0:T(8,128)S(1)}, u32[]{:S(2)}, u32[]{:S(2)}) collective-permute-start(f32[1,168,128]{2,1,0:T(8,128)S(1)} %constant_dynamic-slice_fusion), channel_id=1, source_target_pairs={{0,16},{1,17},{2,18},{3,19},{4,20},{5,21},{6,22},{7,23},{8,24},{9,... | collective-permute-start | bytes 258056 | tf_op jit(solution)/shard_map/ppermute | solution.py:62
  72.1 7.9 %collective-permute-start.7 = (f32[168,128]{1,0:T(8,128)S(1)}, f32[168,128]{1,0:T(8,128)S(1)}, u32[]{:S(2)}, u32[]{:S(2)}) collective-permute-start(f32[168,128]{1,0:T(8,128)S(1)} %add_bitcast_fusion), channel_id=1, source_target_pairs={{0,32},{1,257},{2,34},{3,259},{4,36},{5,261},{6,38},{7,263},{8,40}... | collective-permute-start | bytes 258056 | tf_op jit(solution)/shard_map/ppermute | solution.py:77
  76.5 32.8 %collective-permute-start.1 = (bf16[256,1024]{1,0:T(8,128)(2,1)S(1)}, bf16[256,1024]{1,0:T(8,128)(2,1)S(1)}, u32[]{:S(2)}, u32[]{:S(2)}) collective-permute-start(bf16[256,1024]{1,0:T(8,128)(2,1)S(1)} %pad_maximum_fusion.2), channel_id=1, source_target_pairs={{2,0},{3,1},{4,2},{5,3},{6,4},{7,5},{8,6},{9,7},{10,8},{11,9},{12,... | collective-permute-start | bytes 1572872 | tf_op jit(solution)/shard_map/ppermute | solution.py:10
  80.1 15.3 %collective-permute-start.8 = (f32[168,128]{1,0:T(8,128)S(1)}, f32[168,128]{1,0:T(8,128)S(1)}, u32[]{:S(2)}, u32[]{:S(2)}) collective-permute-start(f32[168,128]{1,0:T(8,128)S(1)} %add.132), channel_id=1, source_target_pairs={{0,64},{1,225},{2,66},{3,227},{4,68},{5,229},{6,70},{7,231},{8,72}... | collective-permute-start | bytes 258056 | tf_op jit(solution)/shard_map/ppermute | solution.py:77
  95.4 11.7 %collective-permute-start.9 = (f32[168,128]{1,0:T(8,128)S(1)}, f32[168,128]{1,0:T(8,128)S(1)}, u32[]{:S(2)}, u32[]{:S(2)}) collective-permute-start(f32[168,128]{1,0:T(8,128)S(1)} %add.133), channel_id=1, source_target_pairs={{0,128},{1,65},{2,130},{3,67},{4,132},{5,69},{6,134},{7,71},{8,136... | collective-permute-start | bytes 258056 | tf_op jit(solution)/shard_map/ppermute | solution.py:77
  107.1 6.4 %collective-permute-start.10 = (f32[168,128]{1,0:T(8,128)S(1)}, f32[168,128]{1,0:T(8,128)S(1)}, u32[]{:S(2)}, u32[]{:S(2)}) collective-permute-start(f32[168,128]{1,0:T(8,128)S(1)} %add.134), channel_id=1, source_target_pairs={{0,256},{1,129},{2,258},{3,131},{4,260},{5,133},{6,262},{7,135},{8... | collective-permute-start | bytes 258056 | tf_op jit(solution)/shard_map/ppermute | solution.py:77

commit v11 on v10

--- a/solution.py
+++ b/solution.py
@@ -129,7 +129,7 @@
         axis=1,
     )
     mine = halving_scatter(packed, "seq", ([0, 2, 3, 1, 4], [0, 2, 1, 3, 4]), (4, 8))
-    mine = butterfly_sum(mine, ("grp", "seq"), ([0, 1, 2, 3], [3, 0, 1, 2]), (1, 8), groups)
+    mine = butterfly_sum(mine, ("grp", "seq"), ([0, 1, 2, 3], [2, 3, 0, 1]), (1, 8), groups)
     grad_taps = mine[:taps_r].reshape(rows_taps, part_taps.shape[1])
     grad_out = mine[taps_r : taps_r + out_r].reshape(rows_out, part_out.shape[1])
     grad_bias = mine[taps_r + out_r, :share_bias]

time: 116 us -> 118 us (1.017)
  waiting for transfers between devices: 43.6 us -> 53.2 us
  starting transfers between devices: 53.3 us -> 45.5 us
    ppermute x4, waiting for transfers between devices: 8.09 us -> 17.6 us  [butterfly_sum(): array = array + lax.ppermute(array, axes, pairs)]
    ppermute x4, starting transfers between devices: 26.2 us -> 18.3 us  [butterfly_sum(): array = array + lax.ppermute(array, axes, pairs)]
where the time goes in v11:
time: 118 us; the launch traced here: 117 us
  waiting for transfers between devices  53.2 us (45%)
  starting transfers between devices  45.5 us (39%)
  matrix products  7.43 us (6%)
  local copies, waits for them, and re-layouts  6.02 us (5%)
  other arithmetic  3.5 us (3%)
  between operations  1.34 us (1%)
    ppermute x5, waiting for transfers between devices, halving_scatter(): buf = keep + lax.ppermute(send, axis, pairs)  32.2 us
    ppermute x5, starting transfers between devices, halving_scatter(): buf = keep + lax.ppermute(send, axis, pairs)  18.5 us
    ppermute x4, starting transfers between devices, butterfly_sum(): array = array + lax.ppermute(array, axes, pairs)  18.3 us
    ppermute x4, waiting for transfers between devices, butterfly_sum(): array = array + lax.ppermute(array, axes, pairs)  17.6 us
    ppermute x2, starting transfers between devices, from_behind(): return lax.ppermute(array, axis, pairs)  8.63 us
    ppermute x2, waiting for transfers between devices, from_behind(): return lax.ppermute(array, axis, pairs)  3.33 us
    dot_general x3, matrix products, contract_cols(): lax.dot_general(left, right, (((1,), (1,)), ((), ())), preferred_element_...  2.85 us
  transfers between devices with their start and end apart: 11, of which 9 were waited for; matrix products, arithmetic and copies ran while one was open for 4% of the time, Pallas kernels for 0%

profile of v11, /device:TPU:56, one launch (start us, length us, event | category | flops | bytes accessed | tf_op | source)
XLA Modules:
  0.0 116.9 jit_solution(827767677666452894)
XLA Ops:
  0.6 0.0 copy-start
  0.6 0.0 copy-start.7
  0.7 5.1 %collective-permute-start = (bf16[256,256]{1,0:T(8,128)(2,1)}, bf16[256,256]{1,0:T(8,128)(2,1)S(1)}, u32[]{:S(2)}, u32[]{:S(2)}) collective-permute-start(bf16[256,256]{1,0:T(8,128)(2,1)} %param.5), channel_id=1, source_target_pairs={{0,2},{1,3},{2,4},{3,5},{4,6},{5,7},{6,8},{7,9},{8,10},{9,11},{10,... | collective-permute-start | bytes 393224 | tf_op jit(solution)/shard_map/ppermute | solution.py:10
  5.7 1.4 %fusion.9 = f32[256,1024]{1,0:T(8,128)S(1)} fusion(bf16[256,256]{1,0:T(8,128)(2,1)} %param.5, bf16[512,1024]{1,0:T(8,128)(2,1)} %param.7), kind=kOutput, calls=%fused_computation.28 | convolution fusion | flops 134217728 | bytes 1703936 | tf_op jit(solution)/shard_map/dot_general | solution.py:84
  7.2 3.3 %collective-permute-done = bf16[256,256]{1,0:T(8,128)(2,1)S(1)} collective-permute-done((bf16[256,256]{1,0:T(8,128)(2,1)}, bf16[256,256]{1,0:T(8,128)(2,1)S(1)}, u32[]{:S(2)}, u32[]{:S(2)}) %collective-permute-start) | collective-permute-done | bytes 131104 | tf_op jit(solution)/shard_map/ppermute | solution.py:10
  10.5 1.3 %fusion = f32[256,1024]{1,0:T(8,128)S(1)} fusion(f32[256,1024]{1,0:T(8,128)S(1)} %fusion.9, bf16[256,256]{1,0:T(8,128)(2,1)S(1)} %collective-permute-done, f32[1024]{0:T(1024)} %param.8, bf16[512,1024]{1,0:T(8,128)(2,1)} %param.7), kind=kOutput, calls=%fused_computation.7 | convolution fusion | flops 134742016 | bytes 2756608 | tf_op jit(solution)/shard_map/dot_general | solution.py:87
  11.9 0.0 copy-done
  11.9 0.0 copy-done.7
  11.9 0.0 copy-start.3
  11.9 0.5 multiply_convert_fusion.1
  12.4 0.0 copy-start.5
  12.4 0.1 convert_reduce_fusion
  12.5 0.3 copy-done.3
  12.8 0.3 convolution_bitcast_fusion
  13.2 0.1 reshape.45
  13.3 0.3 fusion.11
  13.6 0.3 convolution_bitcast_fusion.1
  13.9 0.0 copy-done.5
  13.9 1.5 %pad_maximum_fusion.1 = f32[512,1024]{1,0:T(8,128)} fusion(f32[256,1024]{1,0:T(8,128)S(1)} %convolution_bitcast_fusion, f32[256,1024]{1,0:T(8,128)S(1)} %convolution_bitcast_fusion.1), kind=kLoop, calls=%fused_computation.1 | loop fusion | flops 524288 | bytes 4194304 | tf_op jit(solution)/shard_map/concatenate | solution.py:106
  15.4 1.7 %reshape.43 = f32[32,128,128]{2,1,0:T(8,128)S(1)} reshape(f32[512,1024]{1,0:T(8,128)} %pad_maximum_fusion.1) | data formatting | bytes 4194304 | tf_op jit(solution)/shard_map/reshape | solution.py:125
  17.1 0.2 pad_maximum_fusion
  17.9 0.0 copy-start.1
  17.9 1.5 %copy-done.1 = f32[32,168,128]{2,1,0:T(8,128)} copy-done((f32[32,168,128]{2,1,0:T(8,128)}, f32[32,168,128]{2,1,0:T(8,128)S(1)}, u32[]{:S(2)}) %copy-start.1) | copy-done | bytes 2752536
  19.4 0.1 dynamic-slice_bitcast_fusion
  19.5 1.9 %collective-permute-start.2 = (f32[16,168,128]{2,1,0:T(8,128)S(1)}, f32[16,168,128]{2,1,0:T(8,128)S(1)}, u32[]{:S(2)}, u32[]{:S(2)}) collective-permute-start(f32[16,168,128]{2,1,0:T(8,128)S(1)} %dynamic-slice_bitcast_fusion), channel_id=1, source_target_pairs={{0,1},{1,0},{2,3},{3,2},{4,5},{5,4},{6,7},{7,6},{8,9},{9,8},{10,11... | collective-permute-start | bytes 4128776 | tf_op jit(solution)/shard_map/ppermute | solution.py:62
  21.4 3.1 %collective-permute-done.2 = f32[16,168,128]{2,1,0:T(8,128)S(1)} collective-permute-done((f32[16,168,128]{2,1,0:T(8,128)S(1)}, f32[16,168,128]{2,1,0:T(8,128)S(1)}, u32[]{:S(2)}, u32[]{:S(2)}) %collective-permute-start.2) | collective-permute-done | bytes 1376288 | tf_op jit(solution)/shard_map/ppermute | solution.py:62
  24.5 1.5 %bitcast_add_fusion = f32[16,168,128]{2,1,0:T(8,128)S(1)} fusion(f32[16,168,128]{2,1,0:T(8,128)S(1)} %collective-permute-done.2, f32[2,16,168,128]{3,2,1,0:T(8,128)} %bitcast.42, s32[]{:T(128)S(6)} %select_n.66), kind=kLoop, calls=%fused_computation.2 | loop fusion | flops 344064 | bytes 4128772 | tf_op jit(solution)/shard_map/add | solution.py:62
  26.0 0.1 dynamic-slice_bitcast_fusion.1
  26.1 3.3 %collective-permute-start.3 = (f32[8,168,128]{2,1,0:T(8,128)S(1)}, f32[8,168,128]{2,1,0:T(8,128)S(1)}, u32[]{:S(2)}, u32[]{:S(2)}) collective-permute-start(f32[8,168,128]{2,1,0:T(8,128)S(1)} %dynamic-slice_bitcast_fusion.1), channel_id=1, source_target_pairs={{0,4},{1,29},{2,6},{3,31},{4,0},{5,9},{6,2},{7,11},{8,12},{9,5},{1... | collective-permute-start | bytes 2064392 | tf_op jit(solution)/shard_map/ppermute | solution.py:62
  29.3 9.6 %collective-permute-done.3 = f32[8,168,128]{2,1,0:T(8,128)S(1)} collective-permute-done((f32[8,168,128]{2,1,0:T(8,128)S(1)}, f32[8,168,128]{2,1,0:T(8,128)S(1)}, u32[]{:S(2)}, u32[]{:S(2)}) %collective-permute-start.3) | collective-permute-done | bytes 688160 | tf_op jit(solution)/shard_map/ppermute | solution.py:62
  38.9 0.1 bitcast_add_fusion.1
  39.0 4.6 %collective-permute-start.4 = (f32[4,168,128]{2,1,0:T(8,128)S(1)}, f32[4,168,128]{2,1,0:T(8,128)S(1)}, u32[]{:S(2)}, u32[]{:S(2)}) collective-permute-start(f32[4,168,128]{2,1,0:T(8,128)S(1)} %dynamic-slice_bitcast_fusion.2), channel_id=1, source_target_pairs={{0,8},{1,3},{2,10},{3,1},{4,12},{5,7},{6,14},{7,5},{8,0},{9,11},{1... | collective-permute-start | bytes 1032200 | tf_op jit(solution)/shard_map/ppermute | solution.py:62
  43.6 0.0 copy-start.4
  43.6 0.0 copy-start.6
  43.6 9.1 %collective-permute-done.4 = f32[4,168,128]{2,1,0:T(8,128)S(1)} collective-permute-done((f32[4,168,128]{2,1,0:T(8,128)S(1)}, f32[4,168,128]{2,1,0:T(8,128)S(1)}, u32[]{:S(2)}, u32[]{:S(2)}) %collective-permute-start.4) | collective-permute-done | bytes 344096 | tf_op jit(solution)/shard_map/ppermute | solution.py:62
  52.8 0.0 copy-start.2
  52.8 4.2 %collective-permute-start.5 = (f32[2,168,128]{2,1,0:T(8,128)S(1)}, f32[2,168,128]{2,1,0:T(8,128)S(1)}, u32[]{:S(2)}, u32[]{:S(2)}) collective-permute-start(f32[2,168,128]{2,1,0:T(8,128)S(1)} %dynamic-slice_bitcast_fusion.3), channel_id=1, source_target_pairs={{0,2},{1,9},{2,0},{3,11},{4,6},{5,29},{6,4},{7,31},{8,10},{9,1},{1... | collective-permute-start | bytes 516104 | tf_op jit(solution)/shard_map/ppermute | solution.py:62
  57.0 4.8 %collective-permute-done.5 = f32[2,168,128]{2,1,0:T(8,128)S(1)} collective-permute-done((f32[2,168,128]{2,1,0:T(8,128)S(1)}, f32[2,168,128]{2,1,0:T(8,128)S(1)}, u32[]{:S(2)}, u32[]{:S(2)}) %collective-permute-start.5) | collective-permute-done | bytes 172064 | tf_op jit(solution)/shard_map/ppermute | solution.py:62
  61.8 4.6 %collective-permute-start.6 = (f32[1,168,128]{2,1,0:T(8,128)S(1)}, f32[1,168,128]{2,1,0:T(8,128)S(1)}, u32[]{:S(2)}, u32[]{:S(2)}) collective-permute-start(f32[1,168,128]{2,1,0:T(8,128)S(1)} %constant_dynamic-slice_fusion), channel_id=1, source_target_pairs={{0,16},{1,17},{2,18},{3,19},{4,20},{5,21},{6,22},{7,23},{8,24},{9,... | collective-permute-start | bytes 258056 | tf_op jit(solution)/shard_map/ppermute | solution.py:62
  66.4 5.7 %collective-permute-done.6 = f32[1,168,128]{2,1,0:T(8,128)S(1)} collective-permute-done((f32[1,168,128]{2,1,0:T(8,128)S(1)}, f32[1,168,128]{2,1,0:T(8,128)S(1)}, u32[]{:S(2)}, u32[]{:S(2)}) %collective-permute-start.6) | collective-permute-done | bytes 86048 | tf_op jit(solution)/shard_map/ppermute | solution.py:62
  72.1 4.3 %collective-permute-start.7 = (f32[168,128]{1,0:T(8,128)S(1)}, f32[168,128]{1,0:T(8,128)S(1)}, u32[]{:S(2)}, u32[]{:S(2)}) collective-permute-start(f32[168,128]{1,0:T(8,128)S(1)} %add_bitcast_fusion), channel_id=1, source_target_pairs={{0,32},{1,129},{2,34},{3,131},{4,36},{5,133},{6,38},{7,135},{8,40}... | collective-permute-start | bytes 258056 | tf_op jit(solution)/shard_map/ppermute | solution.py:77
  76.4 0.1 pad_maximum_fusion.2
  76.5 3.6 %collective-permute-start.1 = (bf16[256,1024]{1,0:T(8,128)(2,1)S(1)}, bf16[256,1024]{1,0:T(8,128)(2,1)S(1)}, u32[]{:S(2)}, u32[]{:S(2)}) collective-permute-start(bf16[256,1024]{1,0:T(8,128)(2,1)S(1)} %pad_maximum_fusion.2), channel_id=1, source_target_pairs={{2,0},{3,1},{4,2},{5,3},{6,4},{7,5},{8,6},{9,7},{10,8},{11,9},{12,... | collective-permute-start | bytes 1572872 | tf_op jit(solution)/shard_map/ppermute | solution.py:10
  80.0 0.0 collective-permute-done.7
  80.1 6.1 %collective-permute-start.8 = (f32[168,128]{1,0:T(8,128)S(1)}, f32[168,128]{1,0:T(8,128)S(1)}, u32[]{:S(2)}, u32[]{:S(2)}) collective-permute-start(f32[168,128]{1,0:T(8,128)S(1)} %add.132), channel_id=1, source_target_pairs={{0,64},{1,257},{2,66},{3,259},{4,68},{5,261},{6,70},{7,263},{8,72}... | collective-permute-start | bytes 258056 | tf_op jit(solution)/shard_map/ppermute | solution.py:77
  86.2 1.4 %convolution_add_fusion.3 = f32[256,256]{1,0:T(8,128)S(1)} fusion(bf16[512,1024]{1,0:T(8,128)(2,1)} %param.7, bf16[256,256]{1,0:T(8,128)(2,1)} %param.6, bf16[256,512]{1,0:T(8,128)(2,1)S(1)} %get-tuple-element.6, bf16[256,512]{1,0:T(8,128)(2,1)S(1)} %get-tuple-element.5), kind=kOutput, calls=%fused_computation.10 | convolution fusion | flops 135397376 | bytes 1441792 | tf_op jit(solution)/shard_map/dot_general | solution.py:20
  87.6 10.9 %collective-permute-done.8 = f32[168,128]{1,0:T(8,128)S(1)} collective-permute-done((f32[168,128]{1,0:T(8,128)S(1)}, f32[168,128]{1,0:T(8,128)S(1)}, u32[]{:S(2)}, u32[]{:S(2)}) %collective-permute-start.8) | collective-permute-done | bytes 86048 | tf_op jit(solution)/shard_map/ppermute | solution.py:77
  98.5 4.4 %collective-permute-start.9 = (f32[168,128]{1,0:T(8,128)S(1)}, f32[168,128]{1,0:T(8,128)S(1)}, u32[]{:S(2)}, u32[]{:S(2)}) collective-permute-start(f32[168,128]{1,0:T(8,128)S(1)} %add.133), channel_id=1, source_target_pairs={{0,128},{1,225},{2,130},{3,227},{4,132},{5,229},{6,134},{7,231},{8... | collective-permute-start | bytes 258056 | tf_op jit(solution)/shard_map/ppermute | solution.py:77
  102.9 0.0 copy-done.4
  102.9 0.0 copy-done.6
  102.9 0.9 fusion.1
  103.8 4.9 %collective-permute-done.9 = f32[168,128]{1,0:T(8,128)S(1)} collective-permute-done((f32[168,128]{1,0:T(8,128)S(1)}, f32[168,128]{1,0:T(8,128)S(1)}, u32[]{:S(2)}, u32[]{:S(2)}) %collective-permute-start.9) | collective-permute-done | bytes 86048 | tf_op jit(solution)/shard_map/ppermute | solution.py:77
  108.8 3.5 %collective-permute-start.10 = (f32[168,128]{1,0:T(8,128)S(1)}, f32[168,128]{1,0:T(8,128)S(1)}, u32[]{:S(2)}, u32[]{:S(2)}) collective-permute-start(f32[168,128]{1,0:T(8,128)S(1)} %add.134), channel_id=1, source_target_pairs={{0,256},{1,65},{2,258},{3,67},{4,260},{5,69},{6,262},{7,71},{8,264... | collective-permute-start | bytes 258056 | tf_op jit(solution)/shard_map/ppermute | solution.py:77
  112.3 0.0 collective-permute-done.1
  112.3 0.0 copy-done.2
  112.3 1.0 fusion.2
  113.3 1.8 %collective-permute-done.10 = f32[168,128]{1,0:T(8,128)S(1)} collective-permute-done((f32[168,128]{1,0:T(8,128)S(1)}, f32[168,128]{1,0:T(8,128)S(1)}, u32[]{:S(2)}, u32[]{:S(2)}) %collective-permute-start.10) | collective-permute-done | bytes 86048 | tf_op jit(solution)/shard_map/ppermute | solution.py:77
  115.2 0.5 slice_bitcast_fusion
  115.7 0.6 reshape.50
  116.3 0.6 reshape.51
  (46 shorter events, 0.5 us)
Async XLA Ops:
  0.6 11.3 %copy-start = (bf16[512,256]{1,0:T(8,128)(2,1)S(1)}, bf16[512,256]{1,0:T(8,128)(2,1)}, u32[]{:S(2)}) copy-start(bf16[512,256]{1,0:T(8,128)(2,1)} %param.9) | copy-start | bytes 786436
  0.6 11.3 %copy-start.7 = (bf16[256,256]{1,0:T(8,128)(2,1)S(1)}, bf16[256,256]{1,0:T(8,128)(2,1)}, u32[]{:S(2)}) copy-start(bf16[256,256]{1,0:T(8,128)(2,1)} %param.6) | copy-start | bytes 393220
  0.7 9.9 %collective-permute-start = (bf16[256,256]{1,0:T(8,128)(2,1)}, bf16[256,256]{1,0:T(8,128)(2,1)S(1)}, u32[]{:S(2)}, u32[]{:S(2)}) collective-permute-start(bf16[256,256]{1,0:T(8,128)(2,1)} %param.5), channel_id=1, source_target_pairs={{0,2},{1,3},{2,4},{3,5},{4,6},{5,7},{6,8},{7,9},{8,10},{9,11},{10,... | collective-permute-start | bytes 393224 | tf_op jit(solution)/shard_map/ppermute | solution.py:10
  11.9 0.9 copy-start.3
  12.4 1.5 %copy-start.5 = (bf16[256,512]{1,0:T(8,128)(2,1)}, bf16[256,512]{1,0:T(8,128)(2,1)S(1)}, u32[]{:S(2)}) copy-start(bf16[256,512]{1,0:T(8,128)(2,1)S(1)} %get-tuple-element.7) | copy-start | bytes 786436
  17.9 1.5 %copy-start.1 = (f32[32,168,128]{2,1,0:T(8,128)}, f32[32,168,128]{2,1,0:T(8,128)S(1)}, u32[]{:S(2)}) copy-start(f32[32,168,128]{2,1,0:T(8,128)S(1)} %slice_dynamic-update-slice_fusion) | copy-start | bytes 8257540
  19.5 5.0 %collective-permute-start.2 = (f32[16,168,128]{2,1,0:T(8,128)S(1)}, f32[16,168,128]{2,1,0:T(8,128)S(1)}, u32[]{:S(2)}, u32[]{:S(2)}) collective-permute-start(f32[16,168,128]{2,1,0:T(8,128)S(1)} %dynamic-slice_bitcast_fusion), channel_id=1, source_target_pairs={{0,1},{1,0},{2,3},{3,2},{4,5},{5,4},{6,7},{7,6},{8,9},{9,8},{10,11... | collective-permute-start | bytes 4128776 | tf_op jit(solution)/shard_map/ppermute | solution.py:62
  26.1 12.8 %collective-permute-start.3 = (f32[8,168,128]{2,1,0:T(8,128)S(1)}, f32[8,168,128]{2,1,0:T(8,128)S(1)}, u32[]{:S(2)}, u32[]{:S(2)}) collective-permute-start(f32[8,168,128]{2,1,0:T(8,128)S(1)} %dynamic-slice_bitcast_fusion.1), channel_id=1, source_target_pairs={{0,4},{1,29},{2,6},{3,31},{4,0},{5,9},{6,2},{7,11},{8,12},{9,5},{1... | collective-permute-start | bytes 2064392 | tf_op jit(solution)/shard_map/ppermute | solution.py:62
  39.0 13.7 %collective-permute-start.4 = (f32[4,168,128]{2,1,0:T(8,128)S(1)}, f32[4,168,128]{2,1,0:T(8,128)S(1)}, u32[]{:S(2)}, u32[]{:S(2)}) collective-permute-start(f32[4,168,128]{2,1,0:T(8,128)S(1)} %dynamic-slice_bitcast_fusion.2), channel_id=1, source_target_pairs={{0,8},{1,3},{2,10},{3,1},{4,12},{5,7},{6,14},{7,5},{8,0},{9,11},{1... | collective-permute-start | bytes 1032200 | tf_op jit(solution)/shard_map/ppermute | solution.py:62
  43.6 59.3 %copy-start.4 = (bf16[256,256]{1,0:T(8,128)(2,1)S(1)}, bf16[256,256]{1,0:T(8,128)(2,1)}, u32[]{:S(2)}) copy-start(bf16[256,256]{1,0:T(8,128)(2,1)} %param.5) | copy-start | bytes 393220
  43.6 59.3 %copy-start.6 = (bf16[256,512]{1,0:T(8,128)(2,1)S(1)}, bf16[256,512]{1,0:T(8,128)(2,1)}, u32[]{:S(2)}) copy-start(bf16[256,512]{1,0:T(8,128)(2,1)} %copy-done.5) | copy-start | bytes 786436
  52.8 59.5 %copy-start.2 = (bf16[512,1024]{1,0:T(8,128)(2,1)S(1)}, bf16[512,1024]{1,0:T(8,128)(2,1)}, u32[]{:S(2)}) copy-start(bf16[512,1024]{1,0:T(8,128)(2,1)} %param.7) | copy-start | bytes 3145732
  52.8 8.9 %collective-permute-start.5 = (f32[2,168,128]{2,1,0:T(8,128)S(1)}, f32[2,168,128]{2,1,0:T(8,128)S(1)}, u32[]{:S(2)}, u32[]{:S(2)}) collective-permute-start(f32[2,168,128]{2,1,0:T(8,128)S(1)} %dynamic-slice_bitcast_fusion.3), channel_id=1, source_target_pairs={{0,2},{1,9},{2,0},{3,11},{4,6},{5,29},{6,4},{7,31},{8,10},{9,1},{1... | collective-permute-start | bytes 516104 | tf_op jit(solution)/shard_map/ppermute | solution.py:62
  61.8 10.3 %collective-permute-start.6 = (f32[1,168,128]{2,1,0:T(8,128)S(1)}, f32[1,168,128]{2,1,0:T(8,128)S(1)}, u32[]{:S(2)}, u32[]{:S(2)}) collective-permute-start(f32[1,168,128]{2,1,0:T(8,128)S(1)} %constant_dynamic-slice_fusion), channel_id=1, source_target_pairs={{0,16},{1,17},{2,18},{3,19},{4,20},{5,21},{6,22},{7,23},{8,24},{9,... | collective-permute-start | bytes 258056 | tf_op jit(solution)/shard_map/ppermute | solution.py:62
  72.1 7.9 %collective-permute-start.7 = (f32[168,128]{1,0:T(8,128)S(1)}, f32[168,128]{1,0:T(8,128)S(1)}, u32[]{:S(2)}, u32[]{:S(2)}) collective-permute-start(f32[168,128]{1,0:T(8,128)S(1)} %add_bitcast_fusion), channel_id=1, source_target_pairs={{0,32},{1,129},{2,34},{3,131},{4,36},{5,133},{6,38},{7,135},{8,40}... | collective-permute-start | bytes 258056 | tf_op jit(solution)/shard_map/ppermute | solution.py:77
  76.5 35.8 %collective-permute-start.1 = (bf16[256,1024]{1,0:T(8,128)(2,1)S(1)}, bf16[256,1024]{1,0:T(8,128)(2,1)S(1)}, u32[]{:S(2)}, u32[]{:S(2)}) collective-permute-start(bf16[256,1024]{1,0:T(8,128)(2,1)S(1)} %pad_maximum_fusion.2), channel_id=1, source_target_pairs={{2,0},{3,1},{4,2},{5,3},{6,4},{7,5},{8,6},{9,7},{10,8},{11,9},{12,... | collective-permute-start | bytes 1572872 | tf_op jit(solution)/shard_map/ppermute | solution.py:10
  80.1 18.4 %collective-permute-start.8 = (f32[168,128]{1,0:T(8,128)S(1)}, f32[168,128]{1,0:T(8,128)S(1)}, u32[]{:S(2)}, u32[]{:S(2)}) collective-permute-start(f32[168,128]{1,0:T(8,128)S(1)} %add.132), channel_id=1, source_target_pairs={{0,64},{1,257},{2,66},{3,259},{4,68},{5,261},{6,70},{7,263},{8,72}... | collective-permute-start | bytes 258056 | tf_op jit(solution)/shard_map/ppermute | solution.py:77
  98.5 10.3 %collective-permute-start.9 = (f32[168,128]{1,0:T(8,128)S(1)}, f32[168,128]{1,0:T(8,128)S(1)}, u32[]{:S(2)}, u32[]{:S(2)}) collective-permute-start(f32[168,128]{1,0:T(8,128)S(1)} %add.133), channel_id=1, source_target_pairs={{0,128},{1,225},{2,130},{3,227},{4,132},{5,229},{6,134},{7,231},{8... | collective-permute-start | bytes 258056 | tf_op jit(solution)/shard_map/ppermute | solution.py:77
  108.8 6.4 %collective-permute-start.10 = (f32[168,128]{1,0:T(8,128)S(1)}, f32[168,128]{1,0:T(8,128)S(1)}, u32[]{:S(2)}, u32[]{:S(2)}) collective-permute-start(f32[168,128]{1,0:T(8,128)S(1)} %add.134), channel_id=1, source_target_pairs={{0,256},{1,65},{2,258},{3,67},{4,260},{5,69},{6,262},{7,71},{8,264... | collective-permute-start | bytes 258056 | tf_op jit(solution)/shard_map/ppermute | solution.py:77
